TPU v7x, 512 devices: a whole 4x8x8 slice. The times are simulated.
512 devices in a mesh: ax: 64 (over z, y_hi, core), md: 8 (over y_lo, x).
Axes of the slice: x: 4, y: 8 (y_hi: 4, y_lo: 2; y = y_hi * 2 + y_lo), z: 8, core: 2. Of those that a mesh axis runs over, the one named last changes fastest.
Arguments:
- right_side: float32 [1024, 256, 1024], P('ax', None, 'md'), may hold values from -24 to 24
- coupling: float32 [255], replicated, may hold values from 0.3 to 3
- excess: float32 [256], replicated, may hold values from 0.05 to 0.5
- metric: float32 [256], replicated, may hold values from 1e-06 to 0.0001
Outputs:
- pressure: float32 [1024, 256, 1024], P('ax', None, 'md')
All inputs are finite; a program needn't handle non-finite values.
Results may differ from a plain program's by a relative error of at most 0.00007.
Values sent between devices are 32-bit elements; how exact they have to be, the bound alone decides.
No kernel may reach another device: no remote copies, remote signals or barrier semaphores. Data moves between devices by JAX's collectives and lax.ppermute only.
A program may use at most 128 MiB of HBM per device.

v0:
```python
import math

import jax
import jax.numpy as jnp
from jax import lax
from jax.sharding import PartitionSpec as P

SWEEPS = 4


def with_halo(value, sides, width):
    for axis, dim in sides:
        size, length = (lax.axis_size(axis), value.shape[dim])
        up = [(i, (i + 1) % size) for i in range(size - 1)]
        down = [(j, i) for i, j in up]
        last = lax.slice_in_dim(value, length - width, length, axis=dim)
        leading = lax.slice_in_dim(value, 0, width, axis=dim)
        before = lax.ppermute(last, axis, up)
        after = lax.ppermute(leading, axis, down)
        value = jnp.concatenate([before, value, after], axis=dim)
    return value


def fourier_table(points):
    split = 32
    col_index = jnp.arange(points, dtype=jnp.int32)[None, :]
    middle = points // 2
    wavenumber = jnp.where(col_index <= middle, col_index, col_index - middle)
    scale = 2.0 * math.pi / points
    coarse = jnp.arange(points // split, dtype=jnp.int32)[:, None] * split
    fine = jnp.arange(split, dtype=jnp.int32)[:, None]
    coarse_angle = scale * ((coarse * wavenumber) % points).astype(jnp.float32)
    fine_angle = scale * ((fine * wavenumber) % points).astype(jnp.float32)
    ca, sa = jnp.cos(coarse_angle)[:, None, :], jnp.sin(coarse_angle)[:, None, :]
    cb, sb = jnp.cos(fine_angle)[None, :, :], jnp.sin(fine_angle)[None, :, :]
    weights = jnp.where(
        (col_index == 0) | (col_index == middle),
        jnp.float32(1.0 / points),
        jnp.float32(2.0 / points),
    )
    cosine = ca * cb - sa * sb
    sine = sa * cb + ca * sb
    basis_table = jnp.where(col_index[None] <= middle, cosine, sine).reshape(points, points)
    return lax.optimization_barrier(basis_table * jnp.sqrt(weights))


def wave_numbers(count, points):
    positions = jnp.arange(count, dtype=jnp.int32)
    middle = points // 2
    return jnp.where(positions <= middle, positions, positions - middle).astype(jnp.float32)


def links(coupling):
    zero_one = jnp.zeros((1,), coupling.dtype)
    return (jnp.concatenate([zero_one, coupling]), jnp.concatenate([coupling, zero_one]))


def bounds(lower_link, upper_link, excess, metric, wavenumber):
    squared = wavenumber * wavenumber
    radial_floor = excess[:, None] + metric[:, None] * squared[None, :]
    lowest = jnp.min(radial_floor, axis=0)
    highest = jnp.max(radial_floor + 2.0 * (lower_link + upper_link)[:, None], axis=0) + 16.0 / 3.0
    return ((highest + lowest) / 2.0, (highest - lowest) / 2.0)


def diagonal_terms(lower_here, upper_here, excess_here, metric_here, wavenumber):
    squared = wavenumber * wavenumber
    return (
        (lower_here + upper_here + excess_here)[:, None]
        + metric_here[:, None] * squared[None, :]
        + 2.5
    )


def apply_grid(direction, diagonal, lower_here, upper_here):
    axial_padded = with_halo(direction, (("ax", 0),), 2)
    radial_padded = with_halo(direction, (("md", 1),), 1)
    axial = 4.0 / 3.0 * (axial_padded[1:-3] + axial_padded[3:-1]) - 1.0 / 12.0 * (
        axial_padded[:-4] + axial_padded[4:]
    )
    radial = (
        lower_here[:, None] * radial_padded[:, :-2] + upper_here[:, None] * radial_padded[:, 2:]
    )
    return diagonal * direction - radial - axial


def chebyshev(source, operate, center, spread):
    ratio_bound = center / spread
    solution = jnp.zeros_like(source)
    residual = source
    direction = source / center
    factor = 1.0 / ratio_bound
    for sweep_index in range(SWEEPS):
        solution = solution + direction
        residual = residual - operate(direction)
        renewed = 1.0 / (2.0 * ratio_bound - factor)
        direction = renewed * factor * direction + 2.0 * renewed / spread * residual
        factor = renewed
    return solution + direction


def per_device(right_side, coupling, excess, metric):
    planes, radii, local_points = right_side.shape
    group_size = lax.axis_size("md")
    points = local_points * group_size
    local_radii = radii // group_size
    basis_table = fourier_table(points)
    lower_link, upper_link = links(coupling)
    gridded = lax.all_to_all(
        right_side.reshape(planes, group_size, local_radii, local_points),
        "md",
        split_axis=1,
        concat_axis=1,
        tiled=True,
    )
    spectral = jnp.dot(
        gridded.transpose(0, 2, 1, 3).reshape(planes * local_radii, points),
        basis_table,
        precision=lax.Precision.HIGHEST,
        preferred_element_type=jnp.float32,
    ).reshape(planes, local_radii, points)
    wavenumber = wave_numbers(points, points)
    offset = lax.axis_index("md") * local_radii
    lower_here = lax.dynamic_slice_in_dim(lower_link, offset, local_radii)
    upper_here = lax.dynamic_slice_in_dim(upper_link, offset, local_radii)
    excess_here = lax.dynamic_slice_in_dim(excess, offset, local_radii)
    metric_here = lax.dynamic_slice_in_dim(metric, offset, local_radii)
    center, spread = bounds(lower_link, upper_link, excess, metric, wavenumber)
    diagonal = diagonal_terms(lower_here, upper_here, excess_here, metric_here, wavenumber)

    def operate(direction):
        return apply_grid(direction, diagonal, lower_here, upper_here)

    solution = chebyshev(spectral, operate, center, spread)
    solved = jnp.dot(
        solution.reshape(planes * local_radii, points),
        basis_table.T,
        precision=lax.Precision.HIGHEST,
        preferred_element_type=jnp.float32,
    ).reshape(planes, local_radii, group_size, local_points).transpose(0, 2, 1, 3)
    returned = lax.all_to_all(solved, "md", split_axis=1, concat_axis=1, tiled=True)
    return returned.reshape(planes, radii, local_points)


def solution(mesh):
    return jax.shard_map(
        per_device,
        mesh=mesh,
        in_specs=(P("ax", None, "md"), P(), P(), P()),
        out_specs=P("ax", None, "md"),
        check_vma=False,
    )
```

profile of v0, /device:TPU:256, one launch (start us, length us, event | category | flops | bytes accessed | tf_op | source)
XLA Modules:
  0.0 172.3 jit_solution(3108542052074417901)
XLA Ops:
  0.0 3.1 %copy.12 = f32[16,8,32,128]{3,2,0,1:T(8,128)} copy(f32[16,8,32,128]{3,2,1,0:T(8,128)} %bitcast.36) | data formatting | bytes 4194304 | tf_op jit(solution)/shard_map/reshape | solution.py:110
  3.1 5.3 %all-to-all-start = ((f32[16,8,32,128]{3,2,0,1:T(8,128)}), f32[16,8,32,128]{3,2,0,1:T(8,128)S(1)}, u32[]{:S(2)}, u32[]{:S(2)}) async-start(f32[16,8,32,128]{3,2,0,1:T(8,128)} %copy.12), calls=%async_computation | async-start | bytes 4194304 | tf_op jit(solution)/shard_map/all_to_all | solution.py:109
  10.8 2.9 %fusion = f32[1024,1024]{1,0:T(8,128)} fusion(f32[32,32,1024]{2,1,0:T(8,128)S(1)} %get-tuple-element.33, f32[32,32,1024]{2,1,0:T(8,128)S(1)} %get-tuple-element.32, f32[1024]{0:T(1024)S(1)} %select_sqrt_fusion, pred[1024]{0:T(1024)(128)(4,1)S(1)} %iota_compare_fusion.2), kind=kLoop, calls=%fused_computation.1 | loop fusion | flops 2097152 | bytes 12588032 | tf_op jit(solution)/shard_map/mul | solution.py:44
  14.4 20.1 %all-to-all-done = f32[16,8,32,128]{3,2,0,1:T(8,128)S(1)} async-done(((f32[16,8,32,128]{3,2,0,1:T(8,128)}), f32[16,8,32,128]{3,2,0,1:T(8,128)S(1)}, u32[]{:S(2)}, u32[]{:S(2)}) %all-to-all-start) | async-done | bytes 2097184 | tf_op jit(solution)/shard_map/all_to_all | solution.py:109
  34.5 1.7 copy.13
  36.7 7.0 %fusion.36 = f32[1024,512]{0,1:T(8,128)S(1)} fusion(f32[1024,1024]{1,0:T(8,128)S(1)} %copy-done, f32[64,8,8,128]{3,2,1,0:T(8,128)S(1)} %bitcast.34), kind=kOutput, calls=%fused_computation.53 | convolution fusion | flops 6442450944 | bytes 8388608 | tf_op jit(solution)/shard_map/dot_general | solution.py:116
  44.1 1.9 %collective-permute-start.2 = (f32[2,32,1024]{2,1,0:T(8,128)S(1)}, f32[2,32,1024]{2,1,0:T(8,128)S(1)}, u32[]{:S(2)}, u32[]{:S(2)}) collective-permute-start(f32[2,32,1024]{2,1,0:T(8,128)S(1)} %get-tuple-element.30), channel_id=1, source_target_pairs={{0,8},{8,16},{16,24},{24,32},{32,40},{40,48},{48,56},{56,64},{64,7... | collective-permute-start | bytes 786440 | tf_op jit(solution)/shard_map/ppermute | solution.py:18
  46.0 7.9 %collective-permute-start.3 = (f32[2,32,1024]{2,1,0:T(8,128)S(1)}, f32[2,32,1024]{2,1,0:T(8,128)S(1)}, u32[]{:S(2)}, u32[]{:S(2)}) collective-permute-start(f32[2,32,1024]{2,1,0:T(8,128)S(1)} %get-tuple-element.31), channel_id=1, source_target_pairs={{8,0},{16,8},{24,16},{32,24},{40,32},{48,40},{56,48},{64,56},{72,6... | collective-permute-start | bytes 786440 | tf_op jit(solution)/shard_map/ppermute | solution.py:19
  54.0 2.9 %collective-permute-start = (f32[16,1,1024]{2,1,0:T(1,128)S(1)}, f32[16,1,1024]{2,1,0:T(1,128)S(1)}, u32[]{:S(2)}, u32[]{:S(2)}) collective-permute-start(f32[16,1,1024]{2,1,0:T(1,128)S(1)} %get-tuple-element.28), channel_id=1, source_target_pairs={{0,1},{1,2},{2,3},{3,4},{4,5},{5,6},{6,7},{8,9},{9,10},{10,11},{11... | collective-permute-start | bytes 196616 | tf_op jit(solution)/shard_map/ppermute | solution.py:18
  57.0 1.3 collective-permute-start.1
  58.9 4.3 %collective-permute-done.1 = f32[16,1,1024]{2,1,0:T(1,128)S(1)} collective-permute-done((f32[16,1,1024]{2,1,0:T(1,128)S(1)}, f32[16,1,1024]{2,1,0:T(1,128)S(1)}, u32[]{:S(2)}, u32[]{:S(2)}) %collective-permute-start.1) | collective-permute-done | bytes 65568 | tf_op jit(solution)/shard_map/ppermute | solution.py:19
  63.1 2.8 %multiply_add_fusion.3 = (f32[16,32,1024]{2,1,0:T(8,128)S(1)}, f32[16,32,1024]{2,1,0:T(8,128)S(1)}) fusion(f32[16,32,1024]{2,1,0:T(8,128)S(1)} %broadcast_divide_fusion, f32[1024]{0:T(1024)S(1)} %get-tuple-element.38, f32[1024]{0:T(1024)S(1)} %get-tuple-element.35, f32[16,32,1024]{2,1,0:T(8,128)S(1)} %bitcast.33, ...), kind=kLoop, calls=%fused_computation.107 | loop fusion | flops 11010048 | bytes 9183488 | tf_op jit(solution)/shard_map/add | solution.py:97
  65.9 1.9 %collective-permute-start.6 = (f32[2,32,1024]{2,1,0:T(8,128)S(1)}, f32[2,32,1024]{2,1,0:T(8,128)S(1)}, u32[]{:S(2)}, u32[]{:S(2)}) collective-permute-start(f32[2,32,1024]{2,1,0:T(8,128)S(1)} %get-tuple-element.26), channel_id=1, source_target_pairs={{0,8},{8,16},{16,24},{24,32},{32,40},{40,48},{48,56},{56,64},{64,7... | collective-permute-start | bytes 786440 | tf_op jit(solution)/shard_map/ppermute | solution.py:18
  67.9 7.9 %collective-permute-start.7 = (f32[2,32,1024]{2,1,0:T(8,128)S(1)}, f32[2,32,1024]{2,1,0:T(8,128)S(1)}, u32[]{:S(2)}, u32[]{:S(2)}) collective-permute-start(f32[2,32,1024]{2,1,0:T(8,128)S(1)} %get-tuple-element.27), channel_id=1, source_target_pairs={{8,0},{16,8},{24,16},{32,24},{40,32},{48,40},{56,48},{64,56},{72,6... | collective-permute-start | bytes 786440 | tf_op jit(solution)/shard_map/ppermute | solution.py:19
  75.8 2.9 %collective-permute-start.4 = (f32[16,1,1024]{2,1,0:T(1,128)S(1)}, f32[16,1,1024]{2,1,0:T(1,128)S(1)}, u32[]{:S(2)}, u32[]{:S(2)}) collective-permute-start(f32[16,1,1024]{2,1,0:T(1,128)S(1)} %get-tuple-element.24), channel_id=1, source_target_pairs={{0,1},{1,2},{2,3},{3,4},{4,5},{5,6},{6,7},{8,9},{9,10},{10,11},{11... | collective-permute-start | bytes 196616 | tf_op jit(solution)/shard_map/ppermute | solution.py:18
  78.7 1.3 collective-permute-start.5
  80.6 4.3 %collective-permute-done.5 = f32[16,1,1024]{2,1,0:T(1,128)S(1)} collective-permute-done((f32[16,1,1024]{2,1,0:T(1,128)S(1)}, f32[16,1,1024]{2,1,0:T(1,128)S(1)}, u32[]{:S(2)}, u32[]{:S(2)}) %collective-permute-start.5) | collective-permute-done | bytes 65568 | tf_op jit(solution)/shard_map/ppermute | solution.py:19
  84.9 2.8 %multiply_add_fusion.2 = (f32[16,32,1024]{2,1,0:T(8,128)S(1)}, f32[16,32,1024]{2,1,0:T(8,128)S(1)}) fusion(f32[16,32,1024]{2,1,0:T(8,128)S(1)} %get-tuple-element.14, f32[1024]{0:T(1024)S(1)} %get-tuple-element.37, f32[1024]{0:T(1024)S(1)} %get-tuple-element.40, f32[16,32,1024]{2,1,0:T(8,128)S(1)} %get-tuple-element.15, ...), kind=kLoop, calls=%fused_computation.105 | loop fusion | flops 11010048 | bytes 9183488 | tf_op jit(solution)/shard_map/add | solution.py:97
  87.7 1.9 %collective-permute-start.10 = (f32[2,32,1024]{2,1,0:T(8,128)S(1)}, f32[2,32,1024]{2,1,0:T(8,128)S(1)}, u32[]{:S(2)}, u32[]{:S(2)}) collective-permute-start(f32[2,32,1024]{2,1,0:T(8,128)S(1)} %get-tuple-element.22), channel_id=1, source_target_pairs={{0,8},{8,16},{16,24},{24,32},{32,40},{40,48},{48,56},{56,64},{64,7... | collective-permute-start | bytes 786440 | tf_op jit(solution)/shard_map/ppermute | solution.py:18
  89.6 7.9 %collective-permute-start.11 = (f32[2,32,1024]{2,1,0:T(8,128)S(1)}, f32[2,32,1024]{2,1,0:T(8,128)S(1)}, u32[]{:S(2)}, u32[]{:S(2)}) collective-permute-start(f32[2,32,1024]{2,1,0:T(8,128)S(1)} %get-tuple-element.23), channel_id=1, source_target_pairs={{8,0},{16,8},{24,16},{32,24},{40,32},{48,40},{56,48},{64,56},{72,6... | collective-permute-start | bytes 786440 | tf_op jit(solution)/shard_map/ppermute | solution.py:19
  97.6 5.8 %collective-permute-start.8 = (f32[16,1,1024]{2,1,0:T(1,128)S(1)}, f32[16,1,1024]{2,1,0:T(1,128)S(1)}, u32[]{:S(2)}, u32[]{:S(2)}) collective-permute-start(f32[16,1,1024]{2,1,0:T(1,128)S(1)} %get-tuple-element.20), channel_id=1, source_target_pairs={{0,1},{1,2},{2,3},{3,4},{4,5},{5,6},{6,7},{8,9},{9,10},{10,11},{11... | collective-permute-start | bytes 196616 | tf_op jit(solution)/shard_map/ppermute | solution.py:18
  103.4 1.3 collective-permute-start.9
  105.2 4.3 %collective-permute-done.9 = f32[16,1,1024]{2,1,0:T(1,128)S(1)} collective-permute-done((f32[16,1,1024]{2,1,0:T(1,128)S(1)}, f32[16,1,1024]{2,1,0:T(1,128)S(1)}, u32[]{:S(2)}, u32[]{:S(2)}) %collective-permute-start.9) | collective-permute-done | bytes 65568 | tf_op jit(solution)/shard_map/ppermute | solution.py:19
  109.5 3.5 %multiply_add_fusion.1 = (f32[16,32,1024]{2,1,0:T(8,128)S(1)}, f32[16,32,1024]{2,1,0:T(8,128)}) fusion(f32[16,32,1024]{2,1,0:T(8,128)S(1)} %get-tuple-element.12, f32[1024]{0:T(1024)S(1)} %get-tuple-element.36, f32[1024]{0:T(1024)S(1)} %get-tuple-element.39, f32[16,32,1024]{2,1,0:T(8,128)S(1)} %get-tuple-element.13, ...), kind=kLoop, calls=%fused_computation.103 | loop fusion | flops 11010048 | bytes 9183488 | tf_op jit(solution)/shard_map/add | solution.py:97
  113.1 1.9 %collective-permute-start.14 = (f32[2,32,1024]{2,1,0:T(8,128)S(1)}, f32[2,32,1024]{2,1,0:T(8,128)S(1)}, u32[]{:S(2)}, u32[]{:S(2)}) collective-permute-start(f32[2,32,1024]{2,1,0:T(8,128)S(1)} %get-tuple-element.18), channel_id=1, source_target_pairs={{0,8},{8,16},{16,24},{24,32},{32,40},{40,48},{48,56},{56,64},{64,7... | collective-permute-start | bytes 786440 | tf_op jit(solution)/shard_map/ppermute | solution.py:18
  115.0 7.9 %collective-permute-start.15 = (f32[2,32,1024]{2,1,0:T(8,128)S(1)}, f32[2,32,1024]{2,1,0:T(8,128)S(1)}, u32[]{:S(2)}, u32[]{:S(2)}) collective-permute-start(f32[2,32,1024]{2,1,0:T(8,128)S(1)} %get-tuple-element.19), channel_id=1, source_target_pairs={{8,0},{16,8},{24,16},{32,24},{40,32},{48,40},{56,48},{64,56},{72,6... | collective-permute-start | bytes 786440 | tf_op jit(solution)/shard_map/ppermute | solution.py:19
  123.0 4.0 %collective-permute-start.12 = (f32[16,1,1024]{2,1,0:T(1,128)S(1)}, f32[16,1,1024]{2,1,0:T(1,128)S(1)}, u32[]{:S(2)}, u32[]{:S(2)}) collective-permute-start(f32[16,1,1024]{2,1,0:T(1,128)S(1)} %get-tuple-element.16), channel_id=1, source_target_pairs={{0,1},{1,2},{2,3},{3,4},{4,5},{5,6},{6,7},{8,9},{9,10},{10,11},{11... | collective-permute-start | bytes 196616 | tf_op jit(solution)/shard_map/ppermute | solution.py:18
  127.0 1.3 collective-permute-start.13
  128.9 4.3 %collective-permute-done.13 = f32[16,1,1024]{2,1,0:T(1,128)S(1)} collective-permute-done((f32[16,1,1024]{2,1,0:T(1,128)S(1)}, f32[16,1,1024]{2,1,0:T(1,128)S(1)}, u32[]{:S(2)}, u32[]{:S(2)}) %collective-permute-start.13) | collective-permute-done | bytes 65568 | tf_op jit(solution)/shard_map/ppermute | solution.py:19
  133.2 10.2 %fusion.75 = f32[16,8,32,128]{3,2,1,0:T(8,128)S(1)} fusion(f32[8,128,1024,1]{2,1,0,3:T(8,128)S(1)} %bitcast.31, f32[16,32,1024]{2,1,0:T(8,128)} %get-tuple-element.11, f32[16,32,1024]{2,1,0:T(8,128)S(1)} %get-tuple-element.10, f32[2,32,1024]{2,1,0:T(8,128)S(1)} %collective-permute-done.15, f32[2,32,1024]{2,1,0:T(8,128)S(1)} %collective-permute-done.14, ...), kind=kOutput, calls=%fused_computation.108 | convolution fusion | flops 6455558144 | bytes 17572096 | tf_op jit(solution)/shard_map/dot_general | solution.py:135
  143.6 27.2 %all_to_all.10 = f32[16,8,32,128]{3,2,0,1:T(8,128)S(1)} all-to-all(f32[16,8,32,128]{3,2,0,1:T(8,128)S(1)} %copy.14), channel_id=1, replica_groups=mesh['ax'=64,'md'=8] {'md'}, dimensions={1} | all-to-all | bytes 4194304 | tf_op jit(solution)/shard_map/all_to_all | solution.py:141
  170.7 1.5 copy.15
  (44 shorter events, 6.9 us)
Async XLA Ops:
  3.1 31.3 %all-to-all-start = ((f32[16,8,32,128]{3,2,0,1:T(8,128)}), f32[16,8,32,128]{3,2,0,1:T(8,128)S(1)}, u32[]{:S(2)}, u32[]{:S(2)}) async-start(f32[16,8,32,128]{3,2,0,1:T(8,128)} %copy.12), calls=%async_computation | async-start | bytes 4194304 | tf_op jit(solution)/shard_map/all_to_all | solution.py:109
  10.8 3.0 %copy-start.3 = (f32[256]{0:T(256)S(1)}, f32[256]{0:T(256)}, u32[]{:S(2)}) copy-start(f32[256]{0:T(256)} %param.7) | copy-start | bytes 3076
  10.8 3.0 %copy-start.2 = (f32[255]{0:T(256)S(1)}, f32[255]{0:T(256)}, u32[]{:S(2)}) copy-start(f32[255]{0:T(256)} %param.5) | copy-start | bytes 3064
  10.8 3.1 %copy-start.1 = (f32[256]{0:T(256)S(1)}, f32[256]{0:T(256)}, u32[]{:S(2)}) copy-start(f32[256]{0:T(256)} %param.6) | copy-start | bytes 3076
  34.5 2.2 %copy-start = (f32[1024,1024]{1,0:T(8,128)S(1)}, f32[1024,1024]{1,0:T(8,128)}, u32[]{:S(2)}) copy-start(f32[1024,1024]{1,0:T(8,128)} %fusion) | copy-start | bytes 12582916
  44.1 19.0 %collective-permute-start.2 = (f32[2,32,1024]{2,1,0:T(8,128)S(1)}, f32[2,32,1024]{2,1,0:T(8,128)S(1)}, u32[]{:S(2)}, u32[]{:S(2)}) collective-permute-start(f32[2,32,1024]{2,1,0:T(8,128)S(1)} %get-tuple-element.30), channel_id=1, source_target_pairs={{0,8},{8,16},{16,24},{24,32},{32,40},{40,48},{48,56},{56,64},{64,7... | collective-permute-start | bytes 786440 | tf_op jit(solution)/shard_map/ppermute | solution.py:18
  46.0 17.1 %collective-permute-start.3 = (f32[2,32,1024]{2,1,0:T(8,128)S(1)}, f32[2,32,1024]{2,1,0:T(8,128)S(1)}, u32[]{:S(2)}, u32[]{:S(2)}) collective-permute-start(f32[2,32,1024]{2,1,0:T(8,128)S(1)} %get-tuple-element.31), channel_id=1, source_target_pairs={{8,0},{16,8},{24,16},{32,24},{40,32},{48,40},{56,48},{64,56},{72,6... | collective-permute-start | bytes 786440 | tf_op jit(solution)/shard_map/ppermute | solution.py:19
  54.0 4.8 %collective-permute-start = (f32[16,1,1024]{2,1,0:T(1,128)S(1)}, f32[16,1,1024]{2,1,0:T(1,128)S(1)}, u32[]{:S(2)}, u32[]{:S(2)}) collective-permute-start(f32[16,1,1024]{2,1,0:T(1,128)S(1)} %get-tuple-element.28), channel_id=1, source_target_pairs={{0,1},{1,2},{2,3},{3,4},{4,5},{5,6},{6,7},{8,9},{9,10},{10,11},{11... | collective-permute-start | bytes 196616 | tf_op jit(solution)/shard_map/ppermute | solution.py:18
  57.0 6.2 %collective-permute-start.1 = (f32[16,1,1024]{2,1,0:T(1,128)S(1)}, f32[16,1,1024]{2,1,0:T(1,128)S(1)}, u32[]{:S(2)}, u32[]{:S(2)}) collective-permute-start(f32[16,1,1024]{2,1,0:T(1,128)S(1)} %get-tuple-element.29), channel_id=1, source_target_pairs={{1,0},{2,1},{3,2},{4,3},{5,4},{6,5},{7,6},{9,8},{10,9},{11,10},{12... | collective-permute-start | bytes 196616 | tf_op jit(solution)/shard_map/ppermute | solution.py:19
  65.9 18.9 %collective-permute-start.6 = (f32[2,32,1024]{2,1,0:T(8,128)S(1)}, f32[2,32,1024]{2,1,0:T(8,128)S(1)}, u32[]{:S(2)}, u32[]{:S(2)}) collective-permute-start(f32[2,32,1024]{2,1,0:T(8,128)S(1)} %get-tuple-element.26), channel_id=1, source_target_pairs={{0,8},{8,16},{16,24},{24,32},{32,40},{40,48},{48,56},{56,64},{64,7... | collective-permute-start | bytes 786440 | tf_op jit(solution)/shard_map/ppermute | solution.py:18
  67.9 17.0 %collective-permute-start.7 = (f32[2,32,1024]{2,1,0:T(8,128)S(1)}, f32[2,32,1024]{2,1,0:T(8,128)S(1)}, u32[]{:S(2)}, u32[]{:S(2)}) collective-permute-start(f32[2,32,1024]{2,1,0:T(8,128)S(1)} %get-tuple-element.27), channel_id=1, source_target_pairs={{8,0},{16,8},{24,16},{32,24},{40,32},{48,40},{56,48},{64,56},{72,6... | collective-permute-start | bytes 786440 | tf_op jit(solution)/shard_map/ppermute | solution.py:19
  75.8 4.8 %collective-permute-start.4 = (f32[16,1,1024]{2,1,0:T(1,128)S(1)}, f32[16,1,1024]{2,1,0:T(1,128)S(1)}, u32[]{:S(2)}, u32[]{:S(2)}) collective-permute-start(f32[16,1,1024]{2,1,0:T(1,128)S(1)} %get-tuple-element.24), channel_id=1, source_target_pairs={{0,1},{1,2},{2,3},{3,4},{4,5},{5,6},{6,7},{8,9},{9,10},{10,11},{11... | collective-permute-start | bytes 196616 | tf_op jit(solution)/shard_map/ppermute | solution.py:18
  78.7 6.2 %collective-permute-start.5 = (f32[16,1,1024]{2,1,0:T(1,128)S(1)}, f32[16,1,1024]{2,1,0:T(1,128)S(1)}, u32[]{:S(2)}, u32[]{:S(2)}) collective-permute-start(f32[16,1,1024]{2,1,0:T(1,128)S(1)} %get-tuple-element.25), channel_id=1, source_target_pairs={{1,0},{2,1},{3,2},{4,3},{5,4},{6,5},{7,6},{9,8},{10,9},{11,10},{12... | collective-permute-start | bytes 196616 | tf_op jit(solution)/shard_map/ppermute | solution.py:19
  87.7 21.8 %collective-permute-start.10 = (f32[2,32,1024]{2,1,0:T(8,128)S(1)}, f32[2,32,1024]{2,1,0:T(8,128)S(1)}, u32[]{:S(2)}, u32[]{:S(2)}) collective-permute-start(f32[2,32,1024]{2,1,0:T(8,128)S(1)} %get-tuple-element.22), channel_id=1, source_target_pairs={{0,8},{8,16},{16,24},{24,32},{32,40},{40,48},{48,56},{56,64},{64,7... | collective-permute-start | bytes 786440 | tf_op jit(solution)/shard_map/ppermute | solution.py:18
  89.6 19.9 %collective-permute-start.11 = (f32[2,32,1024]{2,1,0:T(8,128)S(1)}, f32[2,32,1024]{2,1,0:T(8,128)S(1)}, u32[]{:S(2)}, u32[]{:S(2)}) collective-permute-start(f32[2,32,1024]{2,1,0:T(8,128)S(1)} %get-tuple-element.23), channel_id=1, source_target_pairs={{8,0},{16,8},{24,16},{32,24},{40,32},{48,40},{56,48},{64,56},{72,6... | collective-permute-start | bytes 786440 | tf_op jit(solution)/shard_map/ppermute | solution.py:19
  97.6 7.6 %collective-permute-start.8 = (f32[16,1,1024]{2,1,0:T(1,128)S(1)}, f32[16,1,1024]{2,1,0:T(1,128)S(1)}, u32[]{:S(2)}, u32[]{:S(2)}) collective-permute-start(f32[16,1,1024]{2,1,0:T(1,128)S(1)} %get-tuple-element.20), channel_id=1, source_target_pairs={{0,1},{1,2},{2,3},{3,4},{4,5},{5,6},{6,7},{8,9},{9,10},{10,11},{11... | collective-permute-start | bytes 196616 | tf_op jit(solution)/shard_map/ppermute | solution.py:18
  103.4 6.2 %collective-permute-start.9 = (f32[16,1,1024]{2,1,0:T(1,128)S(1)}, f32[16,1,1024]{2,1,0:T(1,128)S(1)}, u32[]{:S(2)}, u32[]{:S(2)}) collective-permute-start(f32[16,1,1024]{2,1,0:T(1,128)S(1)} %get-tuple-element.21), channel_id=1, source_target_pairs={{1,0},{2,1},{3,2},{4,3},{5,4},{6,5},{7,6},{9,8},{10,9},{11,10},{12... | collective-permute-start | bytes 196616 | tf_op jit(solution)/shard_map/ppermute | solution.py:19
  113.1 20.1 %collective-permute-start.14 = (f32[2,32,1024]{2,1,0:T(8,128)S(1)}, f32[2,32,1024]{2,1,0:T(8,128)S(1)}, u32[]{:S(2)}, u32[]{:S(2)}) collective-permute-start(f32[2,32,1024]{2,1,0:T(8,128)S(1)} %get-tuple-element.18), channel_id=1, source_target_pairs={{0,8},{8,16},{16,24},{24,32},{32,40},{40,48},{48,56},{56,64},{64,7... | collective-permute-start | bytes 786440 | tf_op jit(solution)/shard_map/ppermute | solution.py:18
  115.0 18.2 %collective-permute-start.15 = (f32[2,32,1024]{2,1,0:T(8,128)S(1)}, f32[2,32,1024]{2,1,0:T(8,128)S(1)}, u32[]{:S(2)}, u32[]{:S(2)}) collective-permute-start(f32[2,32,1024]{2,1,0:T(8,128)S(1)} %get-tuple-element.19), channel_id=1, source_target_pairs={{8,0},{16,8},{24,16},{32,24},{40,32},{48,40},{56,48},{64,56},{72,6... | collective-permute-start | bytes 786440 | tf_op jit(solution)/shard_map/ppermute | solution.py:19
  123.0 5.9 %collective-permute-start.12 = (f32[16,1,1024]{2,1,0:T(1,128)S(1)}, f32[16,1,1024]{2,1,0:T(1,128)S(1)}, u32[]{:S(2)}, u32[]{:S(2)}) collective-permute-start(f32[16,1,1024]{2,1,0:T(1,128)S(1)} %get-tuple-element.16), channel_id=1, source_target_pairs={{0,1},{1,2},{2,3},{3,4},{4,5},{5,6},{6,7},{8,9},{9,10},{10,11},{11... | collective-permute-start | bytes 196616 | tf_op jit(solution)/shard_map/ppermute | solution.py:18
  127.0 6.2 %collective-permute-start.13 = (f32[16,1,1024]{2,1,0:T(1,128)S(1)}, f32[16,1,1024]{2,1,0:T(1,128)S(1)}, u32[]{:S(2)}, u32[]{:S(2)}) collective-permute-start(f32[16,1,1024]{2,1,0:T(1,128)S(1)} %get-tuple-element.17), channel_id=1, source_target_pairs={{1,0},{2,1},{3,2},{4,3},{5,4},{6,5},{7,6},{9,8},{10,9},{11,10},{12... | collective-permute-start | bytes 196616 | tf_op jit(solution)/shard_map/ppermute | solution.py:19
where the time goes:
time: 173 us; the launch traced here: 172 us
  starting transfers between devices  65.2 us (38%)
  waiting for transfers between devices  39.5 us (23%)
  blocking collectives  27.2 us (16%)
  matrix products  17.2 us (10%)
  other arithmetic  15.2 us (9%)
  local copies, waits for them, and re-layouts  7.68 us (4%)
    ppermute x8, starting transfers between devices, with_halo(): after = lax.ppermute(leading, axis, down)  36.6 us
    all_to_all x1, blocking collectives, per_device(): lax.all_to_all(solved, 'md', split_axis=1, concat_axis=1, tiled=True)  27.2 us
    ppermute x8, starting transfers between devices, with_halo(): before = lax.ppermute(last, axis, up)  23.3 us
    all_to_all x1, waiting for transfers between devices, per_device(): lax.all_to_all(right_side.reshape(planes, group_size, local_radii, local_...  20.1 us
    ppermute x8, waiting for transfers between devices, with_halo(): after = lax.ppermute(leading, axis, down)  17.1 us
    dot_general x1, matrix products, per_device(): jnp.dot(solution.reshape(planes * local_radii, points), basis_table.T, pr...  10.2 us
    add x3, other arithmetic, chebyshev(): direction = renewed * factor * direction + 2.0 * renewed / spread * residual  9 us
    dot_general x1, matrix products, per_device(): jnp.dot(gridded.transpose(0, 2, 1, 3).reshape(planes * local_radii, point...  6.99 us
  transfers between devices with their start and end apart: 17, of which 9 were waited for; matrix products, arithmetic and copies ran while one was open for 4% of the time, Pallas kernels for 0%

commit v1 on v0

--- a/solution.py
+++ b/solution.py
@@ -72,27 +72,32 @@
     )
 
 
-def apply_grid(direction, diagonal, lower_here, upper_here):
-    axial_padded = with_halo(direction, (("ax", 0),), 2)
-    radial_padded = with_halo(direction, (("md", 1),), 1)
-    axial = 4.0 / 3.0 * (axial_padded[1:-3] + axial_padded[3:-1]) - 1.0 / 12.0 * (
-        axial_padded[:-4] + axial_padded[4:]
+def apply_inner(direction, diagonal, lower_here, upper_here):
+    middle = direction[2:-2, 1:-1]
+    axial = 4.0 / 3.0 * (direction[1:-3, 1:-1] + direction[3:-1, 1:-1]) - 1.0 / 12.0 * (
+        direction[:-4, 1:-1] + direction[4:, 1:-1]
     )
     radial = (
-        lower_here[:, None] * radial_padded[:, :-2] + upper_here[:, None] * radial_padded[:, 2:]
+        lower_here[:, None] * direction[2:-2, :-2] + upper_here[:, None] * direction[2:-2, 2:]
     )
-    return diagonal * direction - radial - axial
+    return diagonal * middle - radial - axial
 
 
-def chebyshev(source, operate, center, spread):
+def chebyshev(source, coefficients, inside, center, spread):
+    diagonal, lower_here, upper_here = coefficients
     ratio_bound = center / spread
     solution = jnp.zeros_like(source)
     residual = source
     direction = source / center
     factor = 1.0 / ratio_bound
-    for sweep_index in range(SWEEPS):
+    for sweep_index in range(1, SWEEPS + 1):
         solution = solution + direction
-        residual = residual - operate(direction)
+        cut = slice(sweep_index, diagonal.shape[0] - sweep_index)
+        applied = apply_inner(direction, diagonal[cut], lower_here[cut], upper_here[cut])
+        solution = solution[2:-2, 1:-1]
+        direction = direction[2:-2, 1:-1]
+        mask = inside[2 * sweep_index : inside.shape[0] - 2 * sweep_index, cut]
+        residual = (residual[2:-2, 1:-1] - applied) * mask
         renewed = 1.0 / (2.0 * ratio_bound - factor)
         direction = renewed * factor * direction + 2.0 * renewed / spread * residual
         factor = renewed
@@ -120,18 +125,28 @@
         preferred_element_type=jnp.float32,
     ).reshape(planes, local_radii, points)
     wavenumber = wave_numbers(points, points)
+    plane_halo, radius_halo = 2 * SWEEPS, SWEEPS
+    extended = with_halo(spectral, (("ax", 0),), plane_halo)
+    extended = with_halo(extended, (("md", 1),), radius_halo)
+    wide_radii = local_radii + 2 * radius_halo
     offset = lax.axis_index("md") * local_radii
-    lower_here = lax.dynamic_slice_in_dim(lower_link, offset, local_radii)
-    upper_here = lax.dynamic_slice_in_dim(upper_link, offset, local_radii)
-    excess_here = lax.dynamic_slice_in_dim(excess, offset, local_radii)
-    metric_here = lax.dynamic_slice_in_dim(metric, offset, local_radii)
+
+    def around(values):
+        padded = jnp.pad(values, (radius_halo, radius_halo + radii - values.shape[0]))
+        return lax.dynamic_slice_in_dim(padded, offset, wide_radii)
+
+    lower_here, upper_here = around(lower_link), around(upper_link)
+    excess_here, metric_here = around(excess), around(metric)
     center, spread = bounds(lower_link, upper_link, excess, metric, wavenumber)
     diagonal = diagonal_terms(lower_here, upper_here, excess_here, metric_here, wavenumber)
-
-    def operate(direction):
-        return apply_grid(direction, diagonal, lower_here, upper_here)
-
-    solution = chebyshev(spectral, operate, center, spread)
+    all_planes = planes * lax.axis_size("ax")
+    plane_at = lax.axis_index("ax") * planes - plane_halo + jnp.arange(planes + 2 * plane_halo)
+    radius_at = offset - radius_halo + jnp.arange(wide_radii)
+    inside = (
+        ((plane_at >= 0) & (plane_at < all_planes))[:, None]
+        & ((radius_at >= 0) & (radius_at < radii))[None, :]
+    ).astype(jnp.float32)[:, :, None]
+    solution = chebyshev(extended, (diagonal, lower_here, upper_here), inside, center, spread)
     solved = jnp.dot(
         solution.reshape(planes * local_radii, points),
         basis_table.T,

time: 173 us -> 176 us (1.017)
  the two profiles are of different devices: /device:TPU:256 before, /device:TPU:480 now
where the time goes in v1:
time: 176 us; the launch traced here: 175 us
  waiting for transfers between devices  47.9 us (27%)
  blocking collectives  38.5 us (22%)
  other arithmetic  35 us (20%)
  matrix products  21 us (12%)
  local copies, waits for them, and re-layouts  20.3 us (12%)
  starting transfers between devices  12.5 us (7%)
    all_to_all x1, blocking collectives, per_device(): lax.all_to_all(solved, 'md', split_axis=1, concat_axis=1, tiled=True)  38.5 us
    add x3, other arithmetic, chebyshev(): direction = renewed * factor * direction + 2.0 * renewed / spread * residual  25.1 us
    all_to_all x1, waiting for transfers between devices, per_device(): lax.all_to_all(right_side.reshape(planes, group_size, local_radii, local_...  20.4 us
    ppermute x2, waiting for transfers between devices, with_halo(): after = lax.ppermute(leading, axis, down)  16.2 us
    dot_general x1, matrix products, per_device(): jnp.dot(solution.reshape(planes * local_radii, points), basis_table.T, pr...  14 us
    ppermute x2, waiting for transfers between devices, with_halo(): before = lax.ppermute(last, axis, up)  11.2 us
    dot_general x1, matrix products, per_device(): jnp.dot(gridded.transpose(0, 2, 1, 3).reshape(planes * local_radii, point...  6.98 us
    all_to_all x1, starting transfers between devices, per_device(): lax.all_to_all(right_side.reshape(planes, group_size, local_radii, local_...  4.41 us
  transfers between devices with their start and end apart: 5, of which 4 were waited for; matrix products, arithmetic and copies ran while one was open for 9% of the time, Pallas kernels for 0%

profile of v1, /device:TPU:480, one launch (start us, length us, event | category | flops | bytes accessed | tf_op | source)
XLA Modules:
  0.0 175.4 jit_solution(2521912820407572481)
XLA Ops:
  0.0 3.1 %copy.12 = f32[16,8,32,128]{3,2,0,1:T(8,128)} copy(f32[16,8,32,128]{3,2,1,0:T(8,128)} %bitcast.47) | data formatting | bytes 4194304 | tf_op jit(solution)/shard_map/reshape | solution.py:115
  3.1 4.4 %all-to-all-start = ((f32[16,8,32,128]{3,2,0,1:T(8,128)}), f32[16,8,32,128]{3,2,0,1:T(8,128)S(1)}, u32[]{:S(2)}, u32[]{:S(2)}) async-start(f32[16,8,32,128]{3,2,0,1:T(8,128)} %copy.12), calls=%async_computation | async-start | bytes 4194304 | tf_op jit(solution)/shard_map/all_to_all | solution.py:114
  7.6 1.1 fusion.77
  8.7 1.2 multiply_subtract_fusion
  9.9 3.1 %fusion.8 = f32[1024,1024]{1,0:T(8,128)} fusion(f32[32,32,1024]{2,1,0:T(8,128)S(1)} %get-tuple-element.24, f32[32,32,1024]{2,1,0:T(8,128)S(1)} %get-tuple-element.23, f32[1024]{0:T(1024)S(1)} %select_sqrt_fusion, pred[1024]{0:T(1024)(128)(4,1)S(1)} %iota_compare_fusion.2), kind=kLoop, calls=%fused_computation.15 | loop fusion | flops 2097152 | bytes 12588032 | tf_op jit(solution)/shard_map/mul | solution.py:44
  13.2 20.4 %all-to-all-done = f32[16,8,32,128]{3,2,0,1:T(8,128)S(1)} async-done(((f32[16,8,32,128]{3,2,0,1:T(8,128)}), f32[16,8,32,128]{3,2,0,1:T(8,128)S(1)}, u32[]{:S(2)}, u32[]{:S(2)}) %all-to-all-start) | async-done | bytes 2097184 | tf_op jit(solution)/shard_map/all_to_all | solution.py:114
  33.6 1.7 copy.13
  35.8 7.0 %fusion.25 = f32[1024,512]{0,1:T(8,128)S(1)} fusion(f32[1024,1024]{1,0:T(8,128)S(1)} %copy-done, f32[64,8,8,128]{3,2,1,0:T(8,128)S(1)} %bitcast.45), kind=kOutput, calls=%fused_computation.45 | convolution fusion | flops 6442450944 | bytes 8388608 | tf_op jit(solution)/shard_map/dot_general | solution.py:121
  42.9 2.6 %collective-permute-start.1 = (f32[8,32,1024]{2,1,0:T(8,128)S(1)}, f32[8,32,1024]{2,1,0:T(8,128)S(1)}, u32[]{:S(2)}, u32[]{:S(2)}) collective-permute-start(f32[8,32,1024]{2,1,0:T(8,128)S(1)} %bitcast.49), channel_id=1, source_target_pairs={{8,0},{16,8},{24,16},{32,24},{40,32},{48,40},{56,48},{64,56},{72,6... | collective-permute-start | bytes 3145736 | tf_op jit(solution)/shard_map/ppermute | solution.py:19
  45.6 1.9 %collective-permute-start = (f32[8,32,1024]{2,1,0:T(8,128)S(1)}, f32[8,32,1024]{2,1,0:T(8,128)S(1)}, u32[]{:S(2)}, u32[]{:S(2)}) collective-permute-start(f32[8,32,1024]{2,1,0:T(8,128)S(1)} %bitcast.48), channel_id=1, source_target_pairs={{0,8},{8,16},{16,24},{24,32},{32,40},{40,48},{48,56},{56,64},{64,7... | collective-permute-start | bytes 3145736 | tf_op jit(solution)/shard_map/ppermute | solution.py:18
  48.2 15.6 %collective-permute-done.1 = f32[8,32,1024]{2,1,0:T(8,128)S(1)} collective-permute-done((f32[8,32,1024]{2,1,0:T(8,128)S(1)}, f32[8,32,1024]{2,1,0:T(8,128)S(1)}, u32[]{:S(2)}, u32[]{:S(2)}) %collective-permute-start.1) | collective-permute-done | bytes 1048608 | tf_op jit(solution)/shard_map/ppermute | solution.py:19
  63.8 11.2 %collective-permute-done = f32[8,32,1024]{2,1,0:T(8,128)S(1)} collective-permute-done((f32[8,32,1024]{2,1,0:T(8,128)S(1)}, f32[8,32,1024]{2,1,0:T(8,128)S(1)}, u32[]{:S(2)}, u32[]{:S(2)}) %collective-permute-start) | collective-permute-done | bytes 1048608 | tf_op jit(solution)/shard_map/ppermute | solution.py:18
  75.3 2.3 %collective-permute-start.2 = (f32[32,4,1024]{2,1,0:T(4,128)S(1)}, f32[32,4,1024]{2,1,0:T(4,128)S(1)}, u32[]{:S(2)}, u32[]{:S(2)}) collective-permute-start(f32[32,4,1024]{2,1,0:T(4,128)S(1)} %get-tuple-element.18), channel_id=1, source_target_pairs={{0,1},{1,2},{2,3},{3,4},{4,5},{5,6},{6,7},{8,9},{9,10},{10,11},{11... | collective-permute-start | bytes 1572872 | tf_op jit(solution)/shard_map/ppermute | solution.py:18
  77.6 1.3 collective-permute-start.3
  78.9 0.7 slice_bitcast_fusion.3
  80.8 0.7 slice.187
  82.1 0.6 slice.211
  82.7 0.7 slice.198
  83.4 0.7 slice.185
  84.6 0.7 slice.276
  85.3 0.7 slice.262
  86.0 0.7 slice.249
  86.7 0.7 slice.237
  88.7 3.0 %pad_maximum_fusion = (f32[32,40,1024]{2,1,0:T(8,128)}, f32[32,40,1024]{2,1,0:T(8,128)S(1)}) fusion(f32[32,4,1024]{2,1,0:T(4,128)S(1)} %collective-permute-done.3, f32[8,32,1024]{2,1,0:T(8,128)S(1)} %collective-permute-done.1, f32[16,32,1024]{2,1,0:T(8,128)S(1)} %bitcast.43, f32[8,32,1024]{2,1,0:T(8,128)S(1)} %collective-permute-done, ...), kind=kLoop, calls=%fused_computation | loop fusion | flops 6553600 | bytes 15732736 | tf_op jit(solution)/shard_map/concatenate | solution.py:20
  91.6 2.2 %slice.257 = f32[20,34,1024]{2,1,0:T(8,128)} slice(f32[32,40,1024]{2,1,0:T(8,128)S(1)} %get-tuple-element.17), slice={[6:26], [3:37], [0:1024]} | slice | bytes 5570560 | tf_op jit(solution)/shard_map/slice | solution.py:97
  93.8 10.4 %multiply_add_fusion = (f32[28,38,1024]{2,1,0:T(8,128)S(1)}, f32[28,38,1024]{2,1,0:T(8,128)}) fusion(f32[1024]{0:T(1024)S(1)} %get-tuple-element.29, f32[1024]{0:T(1024)S(1)} %get-tuple-element.26, f32[32,40,1024]{2,1,0:T(8,128)S(1)} %get-tuple-element.17, f32[28,38]{1,0:T(8,128)S(1)} %slice_bitcast_fusion, f32[38]{0:T(128)} %slice.187, f32[38]{0:T(128)} %slice.185, ...), kind=kLoop, calls=%fused_computation.13 | loop fusion | flops 17432576 | bytes 43749840 | tf_op jit(solution)/shard_map/add | solution.py:102
  104.3 2.2 %slice.258 = f32[20,34,1024]{2,1,0:T(8,128)} slice(f32[28,38,1024]{2,1,0:T(8,128)S(1)} %get-tuple-element.14), slice={[4:24], [2:36], [0:1024]} | slice | bytes 5570560 | tf_op jit(solution)/shard_map/slice | solution.py:97
  106.5 7.9 %multiply_add_fusion.2 = (f32[24,36,1024]{2,1,0:T(8,128)S(1)}, f32[24,36,1024]{2,1,0:T(8,128)}) fusion(f32[1024]{0:T(1024)S(1)} %get-tuple-element.28, f32[1024]{0:T(1024)S(1)} %get-tuple-element.31, f32[28,38,1024]{2,1,0:T(8,128)S(1)} %get-tuple-element.14, f32[24,36]{1,0:T(8,128)S(1)} %slice_bitcast_fusion.2, f32[36]{0:T(128)S(1)} %copy-done.11, ...), kind=kLoop, calls=%fused_computation.30 | loop fusion | flops 14155776 | bytes 35548832 | tf_op jit(solution)/shard_map/add | solution.py:102
  114.4 6.8 %multiply_add_fusion.3 = (f32[20,34,1024]{2,1,0:T(8,128)S(1)}, f32[20,34,1024]{2,1,0:T(8,128)S(1)}, f32[20,34,1024]{2,1,0:T(8,128)}) fusion(f32[1024]{0:T(1024)S(1)} %get-tuple-element.27, f32[1024]{0:T(1024)S(1)} %get-tuple-element.30, f32[24,36,1024]{2,1,0:T(8,128)S(1)} %get-tuple-element.12, f32[20,34]{1,0:T(8,128)S(1)} %slice_bitcast_fusion.1, ...), kind=kLoop, calls=%fused_computation.43 | loop fusion | flops 11141120 | bytes 30788528 | tf_op jit(solution)/shard_map/add | solution.py:102
  121.2 14.0 %fusion.53 = f32[16,8,32,128]{3,2,1,0:T(8,128)S(1)} fusion(f32[8,128,1024,1]{2,1,0,3:T(8,128)S(1)} %bitcast.44, f32[20,34,1024]{2,1,0:T(8,128)S(1)} %get-tuple-element.10, f32[20,34,1024]{2,1,0:T(8,128)S(1)} %get-tuple-element.11, f32[20,34,1024]{2,1,0:T(8,128)} %get-tuple-element.20, f32[20,34,1024]{2,1,0:T(8,128)} %slice.258, ...), kind=kOutput, calls=%fused_computation.75 | convolution fusion | flops 6452936704 | bytes 29508608 | tf_op jit(solution)/shard_map/dot_general | solution.py:150
  135.4 38.5 %all_to_all.10 = f32[16,8,32,128]{3,2,0,1:T(8,128)S(1)} all-to-all(f32[16,8,32,128]{3,2,0,1:T(8,128)S(1)} %copy.14), channel_id=1, replica_groups=mesh['ax'=64,'md'=8] {'md'}, dimensions={1} | all-to-all | bytes 4194304 | tf_op jit(solution)/shard_map/all_to_all | solution.py:156
  173.9 1.5 copy.15
  (56 shorter events, 5.7 us)
Async XLA Ops:
  3.1 30.4 %all-to-all-start = ((f32[16,8,32,128]{3,2,0,1:T(8,128)}), f32[16,8,32,128]{3,2,0,1:T(8,128)S(1)}, u32[]{:S(2)}, u32[]{:S(2)}) async-start(f32[16,8,32,128]{3,2,0,1:T(8,128)} %copy.12), calls=%async_computation | async-start | bytes 4194304 | tf_op jit(solution)/shard_map/all_to_all | solution.py:114
  9.9 3.1 %copy-start.8 = (f32[255]{0:T(256)S(1)}, f32[255]{0:T(256)}, u32[]{:S(2)}) copy-start(f32[255]{0:T(256)} %param.5) | copy-start | bytes 3064
  33.6 2.2 %copy-start = (f32[1024,1024]{1,0:T(8,128)S(1)}, f32[1024,1024]{1,0:T(8,128)}, u32[]{:S(2)}) copy-start(f32[1024,1024]{1,0:T(8,128)} %fusion.8) | copy-start | bytes 12582916
  42.8 4.8 %copy-start.6 = (f32[256]{0:T(256)S(1)}, f32[256]{0:T(256)}, u32[]{:S(2)}) copy-start(f32[256]{0:T(256)} %param.7) | copy-start | bytes 3076
  42.8 4.8 %copy-start.7 = (f32[256]{0:T(256)S(1)}, f32[256]{0:T(256)}, u32[]{:S(2)}) copy-start(f32[256]{0:T(256)} %param.6) | copy-start | bytes 3076
  42.9 20.9 %collective-permute-start.1 = (f32[8,32,1024]{2,1,0:T(8,128)S(1)}, f32[8,32,1024]{2,1,0:T(8,128)S(1)}, u32[]{:S(2)}, u32[]{:S(2)}) collective-permute-start(f32[8,32,1024]{2,1,0:T(8,128)S(1)} %bitcast.49), channel_id=1, source_target_pairs={{8,0},{16,8},{24,16},{32,24},{40,32},{48,40},{56,48},{64,56},{72,6... | collective-permute-start | bytes 3145736 | tf_op jit(solution)/shard_map/ppermute | solution.py:19
  45.6 29.5 %collective-permute-start = (f32[8,32,1024]{2,1,0:T(8,128)S(1)}, f32[8,32,1024]{2,1,0:T(8,128)S(1)}, u32[]{:S(2)}, u32[]{:S(2)}) collective-permute-start(f32[8,32,1024]{2,1,0:T(8,128)S(1)} %bitcast.48), channel_id=1, source_target_pairs={{0,8},{8,16},{16,24},{24,32},{32,40},{40,48},{48,56},{56,64},{64,7... | collective-permute-start | bytes 3145736 | tf_op jit(solution)/shard_map/ppermute | solution.py:18
  75.3 12.7 %collective-permute-start.2 = (f32[32,4,1024]{2,1,0:T(4,128)S(1)}, f32[32,4,1024]{2,1,0:T(4,128)S(1)}, u32[]{:S(2)}, u32[]{:S(2)}) collective-permute-start(f32[32,4,1024]{2,1,0:T(4,128)S(1)} %get-tuple-element.18), channel_id=1, source_target_pairs={{0,1},{1,2},{2,3},{3,4},{4,5},{5,6},{6,7},{8,9},{9,10},{10,11},{11... | collective-permute-start | bytes 1572872 | tf_op jit(solution)/shard_map/ppermute | solution.py:18
  77.6 11.1 %collective-permute-start.3 = (f32[32,4,1024]{2,1,0:T(4,128)S(1)}, f32[32,4,1024]{2,1,0:T(4,128)S(1)}, u32[]{:S(2)}, u32[]{:S(2)}) collective-permute-start(f32[32,4,1024]{2,1,0:T(4,128)S(1)} %get-tuple-element.19), channel_id=1, source_target_pairs={{1,0},{2,1},{3,2},{4,3},{5,4},{6,5},{7,6},{9,8},{10,9},{11,10},{12... | collective-permute-start | bytes 1572872 | tf_op jit(solution)/shard_map/ppermute | solution.py:19
  104.3 2.2 %copy-start.2 = (f32[36,1024]{1,0:T(8,128)S(1)}, f32[36,1024]{1,0:T(8,128)}, u32[]{:S(2)}) copy-start(f32[36,1024]{1,0:T(8,128)} %slice.249) | copy-start | bytes 442372
  104.3 2.2 %copy-start.11 = (f32[36]{0:T(128)S(1)}, f32[36]{0:T(128)}, u32[]{:S(2)}) copy-start(f32[36]{0:T(128)} %slice.200) | copy-start | bytes 436
  104.3 2.2 %copy-start.12 = (f32[36]{0:T(128)S(1)}, f32[36]{0:T(128)}, u32[]{:S(2)}) copy-start(f32[36]{0:T(128)} %slice.198) | copy-start | bytes 436
  106.5 7.9 %copy-start.9 = (f32[34]{0:T(128)S(1)}, f32[34]{0:T(128)}, u32[]{:S(2)}) copy-start(f32[34]{0:T(128)} %slice.213) | copy-start | bytes 412
  106.5 7.9 %copy-start.10 = (f32[34]{0:T(128)S(1)}, f32[34]{0:T(128)}, u32[]{:S(2)}) copy-start(f32[34]{0:T(128)} %slice.211) | copy-start | bytes 412
  114.4 6.8 %copy-start.1 = (f32[1024,1024]{1,0:T(8,128)S(1)}, f32[1024,1024]{1,0:T(8,128)}, u32[]{:S(2)}) copy-start(f32[1024,1024]{1,0:T(8,128)} %fusion.8) | copy-start | bytes 12582916
  114.4 6.8 %copy-start.3 = (f32[32,1024]{1,0:T(8,128)S(1)}, f32[32,1024]{1,0:T(8,128)}, u32[]{:S(2)}) copy-start(f32[32,1024]{1,0:T(8,128)} %slice.276) | copy-start | bytes 393220
  114.4 6.8 %copy-start.4 = (f32[16,32]{1,0:T(8,128)S(1)}, f32[16,32]{1,0:T(8,128)}, u32[]{:S(2)}) copy-start(f32[16,32]{1,0:T(8,128)} %slice_bitcast_fusion.3) | copy-start | bytes 6148
  114.4 6.8 %copy-start.5 = (f32[1024]{0:T(1024)S(1)}, f32[1024]{0:T(1024)}, u32[]{:S(2)}) copy-start(f32[1024]{0:T(1024)} %get-tuple-element.25) | copy-start | bytes 12292
  114.4 6.8 %copy-start.13 = (f32[32]{0:T(128)S(1)}, f32[32]{0:T(128)}, u32[]{:S(2)}) copy-start(f32[32]{0:T(128)} %slice.226) | copy-start | bytes 388
  114.4 6.8 %copy-start.14 = (f32[32]{0:T(128)S(1)}, f32[32]{0:T(128)}, u32[]{:S(2)}) copy-start(f32[32]{0:T(128)} %slice.224) | copy-start | bytes 388

commit v2 on v1

--- a/solution.py
+++ b/solution.py
@@ -77,9 +77,7 @@
     axial = 4.0 / 3.0 * (direction[1:-3, 1:-1] + direction[3:-1, 1:-1]) - 1.0 / 12.0 * (
         direction[:-4, 1:-1] + direction[4:, 1:-1]
     )
-    radial = (
-        lower_here[:, None] * direction[2:-2, :-2] + upper_here[:, None] * direction[2:-2, 2:]
-    )
+    radial = lower_here * direction[2:-2, :-2] + upper_here * direction[2:-2, 2:]
     return diagonal * middle - radial - axial
 
 
@@ -121,10 +119,12 @@
     spectral = jnp.dot(
         gridded.transpose(0, 2, 1, 3).reshape(planes * local_radii, points),
         basis_table,
-        precision=lax.Precision.HIGHEST,
+        precision=lax.Precision.HIGH,
         preferred_element_type=jnp.float32,
     ).reshape(planes, local_radii, points)
     wavenumber = wave_numbers(points, points)
+    fold = (points // 128, 128)
+    spectral = spectral.reshape(planes, local_radii, *fold)
     plane_halo, radius_halo = 2 * SWEEPS, SWEEPS
     extended = with_halo(spectral, (("ax", 0),), plane_halo)
     extended = with_halo(extended, (("md", 1),), radius_halo)
@@ -145,12 +145,19 @@
     inside = (
         ((plane_at >= 0) & (plane_at < all_planes))[:, None]
         & ((radius_at >= 0) & (radius_at < radii))[None, :]
-    ).astype(jnp.float32)[:, :, None]
-    solution = chebyshev(extended, (diagonal, lower_here, upper_here), inside, center, spread)
+    ).astype(jnp.float32)[:, :, None, None]
+    coefficients = (
+        diagonal.reshape(wide_radii, *fold),
+        lower_here[:, None, None],
+        upper_here[:, None, None],
+    )
+    solution = chebyshev(
+        extended, coefficients, inside, center.reshape(fold), spread.reshape(fold)
+    )
     solved = jnp.dot(
         solution.reshape(planes * local_radii, points),
         basis_table.T,
-        precision=lax.Precision.HIGHEST,
+        precision=lax.Precision.HIGH,
         preferred_element_type=jnp.float32,
     ).reshape(planes, local_radii, group_size, local_points).transpose(0, 2, 1, 3)
     returned = lax.all_to_all(solved, "md", split_axis=1, concat_axis=1, tiled=True)

time: 176 us -> 161 us (0.915)
  the two profiles are of different devices: /device:TPU:480 before, /device:TPU:448 now
where the time goes in v2:
time: 161 us; the launch traced here: 160 us
  waiting for transfers between devices  51.5 us (32%)
  blocking collectives  32.9 us (20%)
  local copies, waits for them, and re-layouts  23.5 us (15%)
  other arithmetic  21.1 us (13%)
  starting transfers between devices  18.4 us (11%)
  matrix products  12.4 us (8%)
    all_to_all x1, blocking collectives, per_device(): lax.all_to_all(solved, 'md', split_axis=1, concat_axis=1, tiled=True)  32.9 us
    all_to_all x1, waiting for transfers between devices, per_device(): lax.all_to_all(right_side.reshape(planes, group_size, local_radii, local_...  20.5 us
    ppermute x2, waiting for transfers between devices, with_halo(): after = lax.ppermute(leading, axis, down)  18.2 us
    ppermute x2, waiting for transfers between devices, with_halo(): before = lax.ppermute(last, axis, up)  12.9 us
    add x3, other arithmetic, chebyshev(): direction = renewed * factor * direction + 2.0 * renewed / spread * residual  10.8 us
    ppermute x2, starting transfers between devices, with_halo(): after = lax.ppermute(leading, axis, down)  7.93 us
    unnamed x20, local copies, waits for them, and re-layouts  7.17 us
    dot_general x1, matrix products, per_device(): jnp.dot(gridded.transpose(0, 2, 1, 3).reshape(planes * local_radii, point...  6.95 us
  transfers between devices with their start and end apart: 5, of which 5 were waited for; matrix products, arithmetic and copies ran while one was open for 10% of the time, Pallas kernels for 0%

profile of v2, /device:TPU:448, one launch (start us, length us, event | category | flops | bytes accessed | tf_op | source)
XLA Modules:
  0.0 160.2 jit_solution(4870245160383245113)
XLA Ops:
  0.0 3.1 %copy.22 = f32[16,8,32,128]{3,2,0,1:T(8,128)} copy(f32[16,8,32,128]{3,2,1,0:T(8,128)} %bitcast.116) | data formatting | bytes 4194304 | tf_op jit(solution)/shard_map/reshape | solution.py:113
  3.1 5.3 %all-to-all-start = ((f32[16,8,32,128]{3,2,0,1:T(8,128)}), f32[16,8,32,128]{3,2,0,1:T(8,128)S(1)}, u32[]{:S(2)}, u32[]{:S(2)}) async-start(f32[16,8,32,128]{3,2,0,1:T(8,128)} %copy.22), calls=%async_computation | async-start | bytes 4194304 | tf_op jit(solution)/shard_map/all_to_all | solution.py:112
  9.6 1.2 multiply_subtract_fusion
  10.8 2.9 %fusion.8 = f32[1024,1024]{1,0:T(8,128)} fusion(f32[32,32,1024]{2,1,0:T(8,128)S(1)} %get-tuple-element.24, f32[32,32,1024]{2,1,0:T(8,128)S(1)} %get-tuple-element.23, f32[1024]{0:T(1024)S(1)} %select_sqrt_fusion, pred[1024]{0:T(1024)(128)(4,1)S(1)} %iota_compare_fusion.2), kind=kLoop, calls=%fused_computation.15 | loop fusion | flops 2097152 | bytes 12588032 | tf_op jit(solution)/shard_map/mul | solution.py:44
  14.0 20.5 %all-to-all-done = f32[16,8,32,128]{3,2,0,1:T(8,128)S(1)} async-done(((f32[16,8,32,128]{3,2,0,1:T(8,128)}), f32[16,8,32,128]{3,2,0,1:T(8,128)S(1)}, u32[]{:S(2)}, u32[]{:S(2)}) %all-to-all-start) | async-done | bytes 2097184 | tf_op jit(solution)/shard_map/all_to_all | solution.py:112
  34.5 1.7 %copy.23 = f32[16,32,8,128]{3,2,1,0:T(8,128)S(1)} copy(f32[16,32,8,128]{3,1,0,2:T(8,128)S(1)} %bitcast.110) | data formatting | bytes 4194304 | tf_op jit(solution)/shard_map/transpose | solution.py:120
  36.7 6.9 %fusion.45 = f32[512,1024]{0,1:T(8,128)S(1)} fusion(f32[1024,1024]{1,0:T(8,128)S(1)} %copy-done, f32[64,8,8,128]{3,2,1,0:T(8,128)S(1)} %bitcast.113), kind=kOutput, calls=%fused_computation.70 | convolution fusion | flops 3221225472 | bytes 8388608 | tf_op jit(solution)/shard_map/dot_general | solution.py:119
  43.7 1.5 fusion.73
  45.2 1.7 %copy.24 = f32[256,1024]{1,0:T(8,128)S(1)} copy(f32[256,1024]{0,1:T(8,128)} %get-tuple-element.22) | data formatting | bytes 2097152 | tf_op jit(solution)/shard_map/slice | solution.py:16
  46.9 1.2 copy.31
  48.1 1.9 %collective-permute-start = (f32[8,32,8,128]{3,2,1,0:T(8,128)}, f32[8,32,8,128]{3,2,1,0:T(8,128)}, u32[]{:S(2)}, u32[]{:S(2)}) collective-permute-start(f32[8,32,8,128]{3,2,1,0:T(8,128)} %bitcast.22), channel_id=1, source_target_pairs={{0,8},{8,16},{16,24},{24,32},{32,40},{40,48},{48,56},{56,64},{64,7... | collective-permute-start | bytes 3145736 | tf_op jit(solution)/shard_map/ppermute | solution.py:18
  50.3 1.6 copy.26
  51.9 1.2 copy.33
  53.1 6.6 %collective-permute-start.1 = (f32[8,32,8,128]{3,2,1,0:T(8,128)}, f32[8,32,8,128]{3,2,1,0:T(8,128)S(1)}, u32[]{:S(2)}, u32[]{:S(2)}) collective-permute-start(f32[8,32,8,128]{3,2,1,0:T(8,128)} %bitcast.28), channel_id=1, source_target_pairs={{8,0},{16,8},{24,16},{32,24},{40,32},{48,40},{56,48},{64,56},{72,6... | collective-permute-start | bytes 3145736 | tf_op jit(solution)/shard_map/ppermute | solution.py:19
  60.6 1.8 %copy.25 = f32[512,1024]{1,0:T(8,128)} copy(f32[512,1024]{0,1:T(8,128)S(1)} %fusion.45) | data formatting | bytes 4194304 | tf_op jit(solution)/shard_map/dot_general | solution.py:119
  62.4 2.1 %copy.32 = f32[64,8,8,128]{3,2,1,0:T(8,128)S(1)} copy(f32[64,8,8,128]{3,1,2,0:T(8,128)} %bitcast.112) | data formatting | bytes 4194304
  64.5 3.2 %collective-permute-done = f32[8,32,8,128]{3,2,1,0:T(8,128)} collective-permute-done((f32[8,32,8,128]{3,2,1,0:T(8,128)}, f32[8,32,8,128]{3,2,1,0:T(8,128)}, u32[]{:S(2)}, u32[]{:S(2)}) %collective-permute-start) | collective-permute-done | bytes 1048608 | tf_op jit(solution)/shard_map/ppermute | solution.py:18
  67.7 1.3 constant_dynamic-update-slice_fusion.1
  69.1 14.0 %collective-permute-done.1 = f32[8,32,8,128]{3,2,1,0:T(8,128)S(1)} collective-permute-done((f32[8,32,8,128]{3,2,1,0:T(8,128)}, f32[8,32,8,128]{3,2,1,0:T(8,128)S(1)}, u32[]{:S(2)}, u32[]{:S(2)}) %collective-permute-start.1) | collective-permute-done | bytes 1048608 | tf_op jit(solution)/shard_map/ppermute | solution.py:19
  83.3 3.2 %collective-permute-start.2 = (f32[32,4,8,128]{3,2,1,0:T(8,128)S(1)}, f32[32,4,8,128]{3,2,1,0:T(8,128)S(1)}, u32[]{:S(2)}, u32[]{:S(2)}) collective-permute-start(f32[32,4,8,128]{3,2,1,0:T(8,128)S(1)} %get-tuple-element.18), channel_id=1, source_target_pairs={{0,1},{1,2},{2,3},{3,4},{4,5},{5,6},{6,7},{8,9},{9,10},{10,11},{11... | collective-permute-start | bytes 1572872 | tf_op jit(solution)/shard_map/ppermute | solution.py:18
  86.5 1.3 collective-permute-start.3
  88.8 9.7 %collective-permute-done.2 = f32[32,4,8,128]{3,2,1,0:T(8,128)S(1)} collective-permute-done((f32[32,4,8,128]{3,2,1,0:T(8,128)S(1)}, f32[32,4,8,128]{3,2,1,0:T(8,128)S(1)}, u32[]{:S(2)}, u32[]{:S(2)}) %collective-permute-start.2) | collective-permute-done | bytes 524320 | tf_op jit(solution)/shard_map/ppermute | solution.py:18
  98.5 4.1 %collective-permute-done.3 = f32[32,4,8,128]{3,2,1,0:T(8,128)S(1)} collective-permute-done((f32[32,4,8,128]{3,2,1,0:T(8,128)S(1)}, f32[32,4,8,128]{3,2,1,0:T(8,128)S(1)}, u32[]{:S(2)}, u32[]{:S(2)}) %collective-permute-start.3) | collective-permute-done | bytes 524320 | tf_op jit(solution)/shard_map/ppermute | solution.py:19
  102.7 1.2 pad_maximum_fusion
  104.1 5.0 %multiply_add_fusion = (f32[28,38,8,128]{3,2,1,0:T(8,128)S(1)}, f32[28,38,8,128]{3,2,1,0:T(8,128)S(1)}) fusion(f32[8,128]{1,0:T(8,128)S(1)} %get-tuple-element.28, f32[8,128]{1,0:T(8,128)S(1)} %get-tuple-element.26, f32[32,40,8,128]{3,2,1,0:T(8,128)S(1)} %get-tuple-element.17, f32[28,38]{1,0:T(8,128)S(1)} %slice_bitcast_fusion.1, f32[38]{0:T(128)S(1)} %slice.199, ...), kind=kLoop, calls=%fused_computation.13 | loop fusion | flops 17432576 | bytes 43749840 | tf_op jit(solution)/shard_map/add | solution.py:100
  109.2 2.7 %multiply_add_fusion.2 = (f32[24,36,8,128]{3,2,1,0:T(8,128)S(1)}, f32[24,36,8,128]{3,2,1,0:T(8,128)S(1)}) fusion(f32[8,128]{1,0:T(8,128)S(1)} %get-tuple-element.29, f32[8,128]{1,0:T(8,128)S(1)} %get-tuple-element.31, f32[28,38,8,128]{3,2,1,0:T(8,128)S(1)} %get-tuple-element.14, f32[24,36]{1,0:T(8,128)S(1)} %slice_bitcast_fusion.3, f32[36]{0:T(128)S(1)} %slice.212, ...), kind=kLoop, calls=%fused_computation.30 | loop fusion | flops 14155776 | bytes 35548832 | tf_op jit(solution)/shard_map/add | solution.py:100
  112.0 3.2 %multiply_add_fusion.3 = (f32[20,34,8,128]{3,2,1,0:T(8,128)S(1)}, f32[20,34,8,128]{3,2,1,0:T(8,128)S(1)}, f32[20,34,8,128]{3,2,1,0:T(8,128)S(1)}) fusion(f32[8,128]{1,0:T(8,128)S(1)} %get-tuple-element.30, f32[8,128]{1,0:T(8,128)S(1)} %get-tuple-element.27, f32[24,36,8,128]{3,2,1,0:T(8,128)S(1)} %get-tuple-element.12, f32[20,34]{1,0:T(8,128)S(1)} %slice_bitcast_fusion.2, ...), kind=kLoop, calls=%fused_computation.43 | loop fusion | flops 11141120 | bytes 30788528 | tf_op jit(solution)/shard_map/add | solution.py:100
  115.1 3.2 %fusion.35 = f32[16,32,8,128]{3,2,1,0:T(8,128)} fusion(f32[20,34,8,128]{3,2,1,0:T(8,128)S(1)} %get-tuple-element.10, f32[20,34,8,128]{3,2,1,0:T(8,128)S(1)} %get-tuple-element.11, f32[20,34,8,128]{3,2,1,0:T(8,128)S(1)} %get-tuple-element.20, f32[20,34,8,128]{3,2,1,0:T(8,128)S(1)} %slice.272, f32[20,34,8,128]{3,2,1,0:T(8,128)S(1)} %slice.271, ...), kind=kLoop, calls=%fused_computation.57 | loop fusion | flops 10485760 | bytes 25307392 | tf_op jit(solution)/shard_map/add | solution.py:102
  118.4 1.7 %reshape.450 = f32[16,32,1024,1]{2,1,0,3:T(8,128)S(1)} reshape(f32[16,32,8,128]{3,2,1,0:T(8,128)} %fusion.35) | data formatting | bytes 4194304 | tf_op jit(solution)/shard_map/dot_general | solution.py:157
  120.1 5.4 %fusion.42 = f32[16,8,32,128]{3,2,1,0:T(8,128)S(1)} fusion(f32[8,128,1024,1]{2,1,0,3:T(8,128)} %bitcast.109, f32[16,32,1024,1]{2,1,0,3:T(8,128)S(1)} %reshape.450), kind=kOutput, calls=%fused_computation.69 | convolution fusion | flops 3221225472 | bytes 8388608 | tf_op jit(solution)/shard_map/dot_general | solution.py:157
  125.7 32.9 %all_to_all.10 = f32[16,8,32,128]{3,2,0,1:T(8,128)S(1)} all-to-all(f32[16,8,32,128]{3,2,0,1:T(8,128)S(1)} %copy.27), channel_id=1, replica_groups=mesh['ax'=64,'md'=8] {'md'}, dimensions={1} | all-to-all | bytes 4194304 | tf_op jit(solution)/shard_map/all_to_all | solution.py:163
  158.7 1.5 copy.28
  (54 shorter events, 4.9 us)
Async XLA Ops:
  3.1 31.3 %all-to-all-start = ((f32[16,8,32,128]{3,2,0,1:T(8,128)}), f32[16,8,32,128]{3,2,0,1:T(8,128)S(1)}, u32[]{:S(2)}, u32[]{:S(2)}) async-start(f32[16,8,32,128]{3,2,0,1:T(8,128)} %copy.22), calls=%async_computation | async-start | bytes 4194304 | tf_op jit(solution)/shard_map/all_to_all | solution.py:112
  10.8 3.0 %copy-start.4 = (f32[255]{0:T(256)S(1)}, f32[255]{0:T(256)}, u32[]{:S(2)}) copy-start(f32[255]{0:T(256)} %param.5) | copy-start | bytes 3064
  34.5 2.2 %copy-start = (f32[1024,1024]{1,0:T(8,128)S(1)}, f32[1024,1024]{1,0:T(8,128)}, u32[]{:S(2)}) copy-start(f32[1024,1024]{1,0:T(8,128)} %fusion.8) | copy-start | bytes 12582916
  43.6 6.3 %copy-start.2 = (f32[256]{0:T(256)S(1)}, f32[256]{0:T(256)}, u32[]{:S(2)}) copy-start(f32[256]{0:T(256)} %param.7) | copy-start | bytes 3076
  43.7 6.3 %copy-start.3 = (f32[256]{0:T(256)S(1)}, f32[256]{0:T(256)}, u32[]{:S(2)}) copy-start(f32[256]{0:T(256)} %param.6) | copy-start | bytes 3076
  48.1 19.6 %collective-permute-start = (f32[8,32,8,128]{3,2,1,0:T(8,128)}, f32[8,32,8,128]{3,2,1,0:T(8,128)}, u32[]{:S(2)}, u32[]{:S(2)}) collective-permute-start(f32[8,32,8,128]{3,2,1,0:T(8,128)} %bitcast.22), channel_id=1, source_target_pairs={{0,8},{8,16},{16,24},{24,32},{32,40},{40,48},{48,56},{56,64},{64,7... | collective-permute-start | bytes 3145736 | tf_op jit(solution)/shard_map/ppermute | solution.py:18
  53.1 30.1 %collective-permute-start.1 = (f32[8,32,8,128]{3,2,1,0:T(8,128)}, f32[8,32,8,128]{3,2,1,0:T(8,128)S(1)}, u32[]{:S(2)}, u32[]{:S(2)}) collective-permute-start(f32[8,32,8,128]{3,2,1,0:T(8,128)} %bitcast.28), channel_id=1, source_target_pairs={{8,0},{16,8},{24,16},{32,24},{40,32},{48,40},{56,48},{64,56},{72,6... | collective-permute-start | bytes 3145736 | tf_op jit(solution)/shard_map/ppermute | solution.py:19
  69.1 19.4 %copy-start.1 = (f32[4,8,8,128]{3,1,2,0:T(8,128)S(1)}, f32[4,8,8,128]{3,1,2,0:T(8,128)}, u32[]{:S(2)}) copy-start(f32[4,8,8,128]{3,1,2,0:T(8,128)} %slice_bitcast_fusion) | copy-start | bytes 393220
  83.3 15.2 %collective-permute-start.2 = (f32[32,4,8,128]{3,2,1,0:T(8,128)S(1)}, f32[32,4,8,128]{3,2,1,0:T(8,128)S(1)}, u32[]{:S(2)}, u32[]{:S(2)}) collective-permute-start(f32[32,4,8,128]{3,2,1,0:T(8,128)S(1)} %get-tuple-element.18), channel_id=1, source_target_pairs={{0,1},{1,2},{2,3},{3,4},{4,5},{5,6},{6,7},{8,9},{9,10},{10,11},{11... | collective-permute-start | bytes 1572872 | tf_op jit(solution)/shard_map/ppermute | solution.py:18
  86.5 16.2 %collective-permute-start.3 = (f32[32,4,8,128]{3,2,1,0:T(8,128)S(1)}, f32[32,4,8,128]{3,2,1,0:T(8,128)S(1)}, u32[]{:S(2)}, u32[]{:S(2)}) collective-permute-start(f32[32,4,8,128]{3,2,1,0:T(8,128)S(1)} %get-tuple-element.19), channel_id=1, source_target_pairs={{1,0},{2,1},{3,2},{4,3},{5,4},{6,5},{7,6},{9,8},{10,9},{11,10},{12... | collective-permute-start | bytes 1572872 | tf_op jit(solution)/shard_map/ppermute | solution.py:19

commit v3 on v2

--- a/solution.py
+++ b/solution.py
@@ -116,15 +116,15 @@
         concat_axis=1,
         tiled=True,
     )
-    spectral = jnp.dot(
+    fold = (points // 128, 128)
+    spectral = lax.dot_general(
         gridded.transpose(0, 2, 1, 3).reshape(planes * local_radii, points),
-        basis_table,
+        basis_table.reshape(points, *fold),
+        (((1,), (0,)), ((), ())),
         precision=lax.Precision.HIGH,
         preferred_element_type=jnp.float32,
-    ).reshape(planes, local_radii, points)
+    ).reshape(planes, local_radii, *fold)
     wavenumber = wave_numbers(points, points)
-    fold = (points // 128, 128)
-    spectral = spectral.reshape(planes, local_radii, *fold)
     plane_halo, radius_halo = 2 * SWEEPS, SWEEPS
     extended = with_halo(spectral, (("ax", 0),), plane_halo)
     extended = with_halo(extended, (("md", 1),), radius_halo)
@@ -154,9 +154,10 @@
     solution = chebyshev(
         extended, coefficients, inside, center.reshape(fold), spread.reshape(fold)
     )
-    solved = jnp.dot(
-        solution.reshape(planes * local_radii, points),
-        basis_table.T,
+    solved = lax.dot_general(
+        solution.reshape(planes * local_radii, *fold),
+        basis_table.reshape(points, *fold),
+        (((1, 2), (1, 2)), ((), ())),
         precision=lax.Precision.HIGH,
         preferred_element_type=jnp.float32,
     ).reshape(planes, local_radii, group_size, local_points).transpose(0, 2, 1, 3)

time: 161 us -> 161 us (level)
  the two profiles are of different devices: /device:TPU:448 before, /device:TPU:488 now
where the time goes in v3:
time: 161 us; the launch traced here: 160 us
  waiting for transfers between devices  43.6 us (27%)
  blocking collectives  32.8 us (20%)
  local copies, waits for them, and re-layouts  28.8 us (18%)
  other arithmetic  26.9 us (17%)
  starting transfers between devices  18.4 us (11%)
  matrix products  9.26 us (6%)
    all_to_all x1, blocking collectives, per_device(): lax.all_to_all(solved, 'md', split_axis=1, concat_axis=1, tiled=True)  32.8 us
    ppermute x2, waiting for transfers between devices, with_halo(): after = lax.ppermute(leading, axis, down)  19.8 us
    all_to_all x1, waiting for transfers between devices, per_device(): lax.all_to_all(right_side.reshape(planes, group_size, local_radii, local_...  14.4 us
    add x3, other arithmetic, chebyshev(): direction = renewed * factor * direction + 2.0 * renewed / spread * residual  12.3 us
    ppermute x2, waiting for transfers between devices, with_halo(): before = lax.ppermute(last, axis, up)  9.35 us
    ppermute x2, starting transfers between devices, with_halo(): after = lax.ppermute(leading, axis, down)  7.83 us
    all_to_all x1, starting transfers between devices, per_device(): lax.all_to_all(right_side.reshape(planes, group_size, local_radii, local_...  5.76 us
    reshape x1, local copies, waits for them, and re-layouts, per_device(): basis_table.reshape(points, *fold)  5.49 us
  transfers between devices with their start and end apart: 5, of which 5 were waited for; matrix products, arithmetic and copies ran while one was open for 12% of the time, Pallas kernels for 0%

profile of v3, /device:TPU:488, one launch (start us, length us, event | category | flops | bytes accessed | tf_op | source)
XLA Modules:
  0.0 160.2 jit_solution(4681080295633865261)
XLA Ops:
  0.0 3.1 %copy.34 = f32[16,8,32,128]{3,2,0,1:T(8,128)} copy(f32[16,8,32,128]{3,2,1,0:T(8,128)} %bitcast.106) | data formatting | bytes 4194304 | tf_op jit(solution)/shard_map/reshape | solution.py:113
  3.1 5.8 %all-to-all-start = ((f32[16,8,32,128]{3,2,0,1:T(8,128)}), f32[16,8,32,128]{3,2,0,1:T(8,128)S(1)}, u32[]{:S(2)}, u32[]{:S(2)}) async-start(f32[16,8,32,128]{3,2,0,1:T(8,128)} %copy.34), calls=%async_computation | async-start | bytes 4194304 | tf_op jit(solution)/shard_map/all_to_all | solution.py:112
  8.9 1.1 fusion.60
  10.0 1.2 multiply_subtract_fusion
  11.2 2.9 %fusion.10 = f32[1024,1024]{1,0:T(8,128)} fusion(f32[32,32,1024]{2,1,0:T(8,128)S(1)} %get-tuple-element.24, f32[32,32,1024]{2,1,0:T(8,128)S(1)} %get-tuple-element.23, f32[1024]{0:T(1024)S(1)} %select_sqrt_fusion, pred[1024]{0:T(1024)(128)(4,1)S(1)} %iota_compare_fusion.2), kind=kLoop, calls=%fused_computation.17 | loop fusion | flops 2097152 | bytes 12588032 | tf_op jit(solution)/shard_map/mul | solution.py:44
  14.2 5.5 %copy.46 = f32[1024,1024]{0,1:T(8,128)} copy(f32[1024,1024]{1,0:T(8,128)} %fusion.10) | data formatting | bytes 8388608 | tf_op jit(solution)/shard_map/reshape | solution.py:122
  20.0 14.4 %all-to-all-done = f32[16,8,32,128]{3,2,0,1:T(8,128)S(1)} async-done(((f32[16,8,32,128]{3,2,0,1:T(8,128)}), f32[16,8,32,128]{3,2,0,1:T(8,128)S(1)}, u32[]{:S(2)}, u32[]{:S(2)}) %all-to-all-start) | async-done | bytes 2097184 | tf_op jit(solution)/shard_map/all_to_all | solution.py:112
  34.4 3.0 %copy.35 = f32[16,32,8,128]{3,2,1,0:T(8,128)} copy(f32[16,32,8,128]{3,1,0,2:T(8,128)S(1)} %bitcast.105) | data formatting | bytes 4194304 | tf_op jit(solution)/shard_map/transpose | solution.py:121
  37.3 1.7 %reshape.460 = f32[512,1024,1]{1,0,2:T(8,128)S(1)} reshape(f32[16,32,8,128]{3,2,1,0:T(8,128)} %copy.35) | data formatting | bytes 4194304 | tf_op jit(solution)/shard_map/reshape | solution.py:121
  39.1 5.3 %convolution_bitcast_fusion = f32[512,8,128]{0,2,1:T(8,128)S(1)} fusion(f32[1024,8,128]{0,2,1:T(8,128)} %bitcast.104, f32[512,1024,1]{1,0,2:T(8,128)S(1)} %reshape.460), kind=kOutput, calls=%fused_computation.69 | convolution fusion | flops 3221225472 | bytes 8388608 | tf_op jit(solution)/shard_map/dot_general | solution.py:120
  44.4 1.3 copy-done.1
  45.9 1.3 copy.37
  47.3 1.3 copy.39
  48.6 2.5 %collective-permute-start.1 = (f32[8,32,8,128]{3,2,1,0:T(8,128)}, f32[8,32,8,128]{3,2,1,0:T(8,128)S(1)}, u32[]{:S(2)}, u32[]{:S(2)}) collective-permute-start(f32[8,32,8,128]{3,2,1,0:T(8,128)} %bitcast.8), channel_id=1, source_target_pairs={{8,0},{16,8},{24,16},{32,24},{40,32},{48,40},{56,48},{64,56},{72,6... | collective-permute-start | bytes 3145736 | tf_op jit(solution)/shard_map/ppermute | solution.py:19
  51.0 1.9 %collective-permute-start = (f32[8,32,8,128]{3,2,1,0:T(8,128)}, f32[8,32,8,128]{3,2,1,0:T(8,128)}, u32[]{:S(2)}, u32[]{:S(2)}) collective-permute-start(f32[8,32,8,128]{3,2,1,0:T(8,128)} %bitcast.107), channel_id=1, source_target_pairs={{0,8},{8,16},{16,24},{24,32},{32,40},{40,48},{48,56},{56,64},{64,7... | collective-permute-start | bytes 3145736 | tf_op jit(solution)/shard_map/ppermute | solution.py:18
  54.7 2.1 %copy.38 = f32[512,8,128]{2,1,0:T(8,128)S(1)} copy(f32[512,8,128]{0,2,1:T(8,128)} %copy-done.1) | data formatting | bytes 4194304 | tf_op jit(solution)/shard_map/dot_general | solution.py:120
  56.8 18.1 %collective-permute-done.1 = f32[8,32,8,128]{3,2,1,0:T(8,128)S(1)} collective-permute-done((f32[8,32,8,128]{3,2,1,0:T(8,128)}, f32[8,32,8,128]{3,2,1,0:T(8,128)S(1)}, u32[]{:S(2)}, u32[]{:S(2)}) %collective-permute-start.1) | collective-permute-done | bytes 1048608 | tf_op jit(solution)/shard_map/ppermute | solution.py:19
  74.9 5.0 %collective-permute-done = f32[8,32,8,128]{3,2,1,0:T(8,128)} collective-permute-done((f32[8,32,8,128]{3,2,1,0:T(8,128)}, f32[8,32,8,128]{3,2,1,0:T(8,128)}, u32[]{:S(2)}, u32[]{:S(2)}) %collective-permute-start) | collective-permute-done | bytes 1048608 | tf_op jit(solution)/shard_map/ppermute | solution.py:18
  79.9 1.2 pad_maximum_fusion.3
  81.1 2.9 %collective-permute-start.2 = (f32[32,4,8,128]{3,2,1,0:T(8,128)S(1)}, f32[32,4,8,128]{3,2,1,0:T(8,128)S(1)}, u32[]{:S(2)}, u32[]{:S(2)}) collective-permute-start(f32[32,4,8,128]{3,2,1,0:T(8,128)S(1)} %get-tuple-element.18), channel_id=1, source_target_pairs={{0,1},{1,2},{2,3},{3,4},{4,5},{5,6},{6,7},{8,9},{9,10},{10,11},{11... | collective-permute-start | bytes 1572872 | tf_op jit(solution)/shard_map/ppermute | solution.py:18
  84.0 5.4 %collective-permute-start.3 = (f32[32,4,8,128]{3,2,1,0:T(8,128)S(1)}, f32[32,4,8,128]{3,2,1,0:T(8,128)S(1)}, u32[]{:S(2)}, u32[]{:S(2)}) collective-permute-start(f32[32,4,8,128]{3,2,1,0:T(8,128)S(1)} %get-tuple-element.19), channel_id=1, source_target_pairs={{1,0},{2,1},{3,2},{4,3},{5,4},{6,5},{7,6},{9,8},{10,9},{11,10},{12... | collective-permute-start | bytes 1572872 | tf_op jit(solution)/shard_map/ppermute | solution.py:19
  94.3 4.3 %collective-permute-done.2 = f32[32,4,8,128]{3,2,1,0:T(8,128)S(1)} collective-permute-done((f32[32,4,8,128]{3,2,1,0:T(8,128)S(1)}, f32[32,4,8,128]{3,2,1,0:T(8,128)S(1)}, u32[]{:S(2)}, u32[]{:S(2)}) %collective-permute-start.2) | collective-permute-done | bytes 524320 | tf_op jit(solution)/shard_map/ppermute | solution.py:18
  98.6 1.7 %collective-permute-done.3 = f32[32,4,8,128]{3,2,1,0:T(8,128)S(1)} collective-permute-done((f32[32,4,8,128]{3,2,1,0:T(8,128)S(1)}, f32[32,4,8,128]{3,2,1,0:T(8,128)S(1)}, u32[]{:S(2)}, u32[]{:S(2)}) %collective-permute-start.3) | collective-permute-done | bytes 524320 | tf_op jit(solution)/shard_map/ppermute | solution.py:19
  100.4 2.8 %pad_maximum_fusion = (f32[32,40,8,128]{3,2,1,0:T(8,128)S(1)}, f32[32,40,8,128]{3,2,1,0:T(8,128)S(1)}) fusion(f32[32,4,8,128]{3,2,1,0:T(8,128)S(1)} %collective-permute-done.3, f32[8,32,8,128]{3,2,1,0:T(8,128)S(1)} %collective-permute-done.1, f32[16,32,8,128]{3,2,1,0:T(8,128)S(1)} %bitcast.102, f32[8,32,8,128]{3,2,1,0:T(8,128)} %collective-permute-done, ...), kind=kLoop, calls=%fused_computation | loop fusion | flops 6553600 | bytes 15732736 | tf_op jit(solution)/shard_map/concatenate | solution.py:20
  103.3 4.9 %multiply_add_fusion = (f32[28,38,8,128]{3,2,1,0:T(8,128)S(1)}, f32[28,38,8,128]{3,2,1,0:T(8,128)S(1)}) fusion(f32[8,128]{1,0:T(8,128)S(1)} %get-tuple-element.28, f32[8,128]{1,0:T(8,128)S(1)} %get-tuple-element.26, f32[32,40,8,128]{3,2,1,0:T(8,128)S(1)} %get-tuple-element.17, f32[28,38]{1,0:T(8,128)S(1)} %slice_bitcast_fusion.1, f32[38]{0:T(128)S(1)} %slice.199, ...), kind=kLoop, calls=%fused_computation.13 | loop fusion | flops 17432576 | bytes 43749840 | tf_op jit(solution)/shard_map/add | solution.py:100
  108.3 1.7 %slice.270 = f32[20,34,8,128]{3,2,1,0:T(8,128)} slice(f32[28,38,8,128]{3,2,1,0:T(8,128)S(1)} %get-tuple-element.14), slice={[4:24], [2:36], [0:8], [0:128]} | slice | bytes 5570560 | tf_op jit(solution)/shard_map/slice | solution.py:95
  110.0 2.7 %multiply_add_fusion.2 = (f32[24,36,8,128]{3,2,1,0:T(8,128)S(1)}, f32[24,36,8,128]{3,2,1,0:T(8,128)S(1)}) fusion(f32[8,128]{1,0:T(8,128)S(1)} %get-tuple-element.29, f32[8,128]{1,0:T(8,128)S(1)} %get-tuple-element.31, f32[28,38,8,128]{3,2,1,0:T(8,128)S(1)} %get-tuple-element.14, f32[24,36]{1,0:T(8,128)S(1)} %copy-done.5, f32[36]{0:T(128)S(1)} %slice.212, ...), kind=kLoop, calls=%fused_computation.33 | loop fusion | flops 14155776 | bytes 35548832 | tf_op jit(solution)/shard_map/add | solution.py:100
  112.8 4.7 %multiply_add_fusion.3 = (f32[20,34,8,128]{3,2,1,0:T(8,128)S(1)}, f32[20,34,8,128]{3,2,1,0:T(8,128)}, f32[20,34,8,128]{3,2,1,0:T(8,128)}) fusion(f32[8,128]{1,0:T(8,128)S(1)} %get-tuple-element.30, f32[8,128]{1,0:T(8,128)S(1)} %get-tuple-element.27, f32[24,36,8,128]{3,2,1,0:T(8,128)S(1)} %get-tuple-element.12, f32[20,34]{1,0:T(8,128)S(1)} %copy-done.6, ...), kind=kLoop, calls=%fused_computation.46 | loop fusion | flops 11141120 | bytes 30788528 | tf_op jit(solution)/shard_map/add | solution.py:100
  117.5 4.2 %fusion.36 = f32[16,32,8,128,1]{3,2,1,0,4:T(8,128)S(1)} fusion(f32[20,34,8,128]{3,2,1,0:T(8,128)S(1)} %get-tuple-element.10, f32[20,34,8,128]{3,2,1,0:T(8,128)} %get-tuple-element.11, f32[20,34,8,128]{3,2,1,0:T(8,128)} %get-tuple-element.20, f32[20,34,8,128]{3,2,1,0:T(8,128)S(1)} %copy-done.2, f32[20,34,8,128]{3,2,1,0:T(8,128)S(1)} %slice.269, ...), kind=kLoop, calls=%fused_computation.57 | loop fusion | flops 10485760 | bytes 25307392 | tf_op jit(solution)/shard_map/add | solution.py:102
  121.7 3.9 %fusion.42 = f32[16,8,32,128]{3,2,1,0:T(8,128)S(1)} fusion(f32[8,128,8,128]{3,2,1,0:T(8,128)S(1)} %bitcast.103, f32[16,32,8,128,1]{3,2,1,0,4:T(8,128)S(1)} %fusion.36), kind=kOutput, calls=%fused_computation.68 | convolution fusion | flops 3221225472 | bytes 8388608 | tf_op jit(solution)/shard_map/dot_general | solution.py:157
  125.8 32.8 %all_to_all.10 = f32[16,8,32,128]{3,2,0,1:T(8,128)S(1)} all-to-all(f32[16,8,32,128]{3,2,0,1:T(8,128)S(1)} %copy.42), channel_id=1, replica_groups=mesh['ax'=64,'md'=8] {'md'}, dimensions={1} | all-to-all | bytes 4194304 | tf_op jit(solution)/shard_map/all_to_all | solution.py:164
  158.6 1.5 copy.43
  (70 shorter events, 7.5 us)
Async XLA Ops:
  3.1 31.2 %all-to-all-start = ((f32[16,8,32,128]{3,2,0,1:T(8,128)}), f32[16,8,32,128]{3,2,0,1:T(8,128)S(1)}, u32[]{:S(2)}, u32[]{:S(2)}) async-start(f32[16,8,32,128]{3,2,0,1:T(8,128)} %copy.34), calls=%async_computation | async-start | bytes 4194304 | tf_op jit(solution)/shard_map/all_to_all | solution.py:112
  14.2 5.5 %copy-start.10 = (f32[255]{0:T(256)S(1)}, f32[255]{0:T(256)}, u32[]{:S(2)}) copy-start(f32[255]{0:T(256)} %param.5) | copy-start | bytes 3064
  14.2 5.6 %copy-start.8 = (f32[256]{0:T(256)S(1)}, f32[256]{0:T(256)}, u32[]{:S(2)}) copy-start(f32[256]{0:T(256)} %param.7) | copy-start | bytes 3076
  14.2 5.6 %copy-start.9 = (f32[256]{0:T(256)S(1)}, f32[256]{0:T(256)}, u32[]{:S(2)}) copy-start(f32[256]{0:T(256)} %param.6) | copy-start | bytes 3076
  19.9 34.0 %copy-start.3 = (f32[32,40,1,1]{1,0,3,2:T(8,128)}, f32[32,40,1,1]{1,0,3,2:T(8,128)S(1)}, u32[]{:S(2)}) copy-start(f32[32,40,1,1]{1,0,3,2:T(8,128)S(1)} %and_convert_fusion) | copy-start | bytes 15364
  44.4 1.3 copy-start.1
  48.6 26.3 %collective-permute-start.1 = (f32[8,32,8,128]{3,2,1,0:T(8,128)}, f32[8,32,8,128]{3,2,1,0:T(8,128)S(1)}, u32[]{:S(2)}, u32[]{:S(2)}) collective-permute-start(f32[8,32,8,128]{3,2,1,0:T(8,128)} %bitcast.8), channel_id=1, source_target_pairs={{8,0},{16,8},{24,16},{32,24},{40,32},{48,40},{56,48},{64,56},{72,6... | collective-permute-start | bytes 3145736 | tf_op jit(solution)/shard_map/ppermute | solution.py:19
  51.0 28.9 %collective-permute-start = (f32[8,32,8,128]{3,2,1,0:T(8,128)}, f32[8,32,8,128]{3,2,1,0:T(8,128)}, u32[]{:S(2)}, u32[]{:S(2)}) collective-permute-start(f32[8,32,8,128]{3,2,1,0:T(8,128)} %bitcast.107), channel_id=1, source_target_pairs={{0,8},{8,16},{16,24},{24,32},{32,40},{40,48},{48,56},{56,64},{64,7... | collective-permute-start | bytes 3145736 | tf_op jit(solution)/shard_map/ppermute | solution.py:18
  79.9 13.2 %copy-start = (f32[1024,1024]{1,0:T(8,128)S(1)}, f32[1024,1024]{1,0:T(8,128)}, u32[]{:S(2)}) copy-start(f32[1024,1024]{1,0:T(8,128)} %fusion.10) | copy-start | bytes 12582916
  81.1 17.5 %collective-permute-start.2 = (f32[32,4,8,128]{3,2,1,0:T(8,128)S(1)}, f32[32,4,8,128]{3,2,1,0:T(8,128)S(1)}, u32[]{:S(2)}, u32[]{:S(2)}) collective-permute-start(f32[32,4,8,128]{3,2,1,0:T(8,128)S(1)} %get-tuple-element.18), channel_id=1, source_target_pairs={{0,1},{1,2},{2,3},{3,4},{4,5},{5,6},{6,7},{8,9},{9,10},{10,11},{11... | collective-permute-start | bytes 1572872 | tf_op jit(solution)/shard_map/ppermute | solution.py:18
  84.0 16.4 %collective-permute-start.3 = (f32[32,4,8,128]{3,2,1,0:T(8,128)S(1)}, f32[32,4,8,128]{3,2,1,0:T(8,128)S(1)}, u32[]{:S(2)}, u32[]{:S(2)}) collective-permute-start(f32[32,4,8,128]{3,2,1,0:T(8,128)S(1)} %get-tuple-element.19), channel_id=1, source_target_pairs={{1,0},{2,1},{3,2},{4,3},{5,4},{6,5},{7,6},{9,8},{10,9},{11,10},{12... | collective-permute-start | bytes 1572872 | tf_op jit(solution)/shard_map/ppermute | solution.py:19
  93.1 1.0 copy-start.4
  108.3 1.7 %copy-start.5 = (f32[24,36]{1,0:T(8,128)S(1)}, f32[24,36]{1,0:T(8,128)}, u32[]{:S(2)}) copy-start(f32[24,36]{1,0:T(8,128)} %slice_bitcast_fusion.3) | copy-start | bytes 10372
  110.0 2.7 %copy-start.6 = (f32[20,34]{1,0:T(8,128)S(1)}, f32[20,34]{1,0:T(8,128)}, u32[]{:S(2)}) copy-start(f32[20,34]{1,0:T(8,128)} %slice_bitcast_fusion.2) | copy-start | bytes 8164
  110.0 2.7 %copy-start.13 = (f32[34]{0:T(128)S(1)}, f32[34]{0:T(128)}, u32[]{:S(2)}) copy-start(f32[34]{0:T(128)} %slice.225) | copy-start | bytes 412
  110.0 2.7 %copy-start.14 = (f32[34]{0:T(128)S(1)}, f32[34]{0:T(128)}, u32[]{:S(2)}) copy-start(f32[34]{0:T(128)} %slice.223) | copy-start | bytes 412
  112.7 4.8 %copy-start.2 = (f32[20,34,8,128]{3,2,1,0:T(8,128)S(1)}, f32[20,34,8,128]{3,2,1,0:T(8,128)}, u32[]{:S(2)}) copy-start(f32[20,34,8,128]{3,2,1,0:T(8,128)} %slice.270) | copy-start | bytes 8355844
  112.7 4.8 %copy-start.7 = (f32[8,128]{1,0:T(8,128)S(1)}, f32[8,128]{1,0:T(8,128)}, u32[]{:S(2)}) copy-start(f32[8,128]{1,0:T(8,128)} %get-tuple-element.7) | copy-start | bytes 12292
  112.7 4.8 %copy-start.11 = (f32[32]{0:T(128)S(1)}, f32[32]{0:T(128)}, u32[]{:S(2)}) copy-start(f32[32]{0:T(128)} %slice.238) | copy-start | bytes 388
  112.8 4.7 %copy-start.12 = (f32[32]{0:T(128)S(1)}, f32[32]{0:T(128)}, u32[]{:S(2)}) copy-start(f32[32]{0:T(128)} %slice.236) | copy-start | bytes 388

commit v4 on v3

--- a/solution.py
+++ b/solution.py
@@ -5,20 +5,27 @@
 from jax import lax
 from jax.sharding import PartitionSpec as P
 
+
 SWEEPS = 4
 
 
-def with_halo(value, sides, width):
-    for axis, dim in sides:
-        size, length = (lax.axis_size(axis), value.shape[dim])
-        up = [(i, (i + 1) % size) for i in range(size - 1)]
-        down = [(j, i) for i, j in up]
-        last = lax.slice_in_dim(value, length - width, length, axis=dim)
-        leading = lax.slice_in_dim(value, 0, width, axis=dim)
-        before = lax.ppermute(last, axis, up)
-        after = lax.ppermute(leading, axis, down)
-        value = jnp.concatenate([before, value, after], axis=dim)
-    return value
+def deep_halo(value, depth, width):
+    def shifted(piece, axis, upward):
+        size = lax.axis_size(axis)
+        up = [(i, i + 1) for i in range(size - 1)]
+        return lax.ppermute(piece, axis, up if upward else [(j, i) for i, j in up])
+
+    below = shifted(value[-depth:], "ax", True)
+    above = shifted(value[:depth], "ax", False)
+    left = shifted(value[:, -width:], "md", True)
+    right = shifted(value[:, :width], "md", False)
+    strips = jnp.concatenate([below, above], axis=0)
+    corner_left = shifted(strips[:, -width:], "md", True)
+    corner_right = shifted(strips[:, :width], "md", False)
+    lower = jnp.concatenate([corner_left[:depth], below, corner_right[:depth]], axis=1)
+    middle = jnp.concatenate([left, value, right], axis=1)
+    upper = jnp.concatenate([corner_left[depth:], above, corner_right[depth:]], axis=1)
+    return jnp.concatenate([lower, middle, upper], axis=0)
 
 
 def fourier_table(points):
@@ -126,8 +133,7 @@
     ).reshape(planes, local_radii, *fold)
     wavenumber = wave_numbers(points, points)
     plane_halo, radius_halo = 2 * SWEEPS, SWEEPS
-    extended = with_halo(spectral, (("ax", 0),), plane_halo)
-    extended = with_halo(extended, (("md", 1),), radius_halo)
+    extended = deep_halo(spectral, plane_halo, radius_halo)
     wide_radii = local_radii + 2 * radius_halo
     offset = lax.axis_index("md") * local_radii
 

time: 161 us -> 172 us (1.068)
  the two profiles are of different devices: /device:TPU:488 before, /device:TPU:448 now
where the time goes in v4:
time: 172 us; the launch traced here: 171 us
  waiting for transfers between devices  45.6 us (27%)
  local copies, waits for them, and re-layouts  35.5 us (21%)
  blocking collectives  32 us (19%)
  starting transfers between devices  24.7 us (14%)
  other arithmetic  22.9 us (13%)
  matrix products  9.85 us (6%)
    all_to_all x1, blocking collectives, per_device(): lax.all_to_all(solved, 'md', split_axis=1, concat_axis=1, tiled=True)  32 us
    ppermute x6, waiting for transfers between devices, shifted(): return lax.ppermute(piece, axis, up if upward else [(j, i) for i, j in up])  31 us
    ppermute x6, starting transfers between devices, shifted(): return lax.ppermute(piece, axis, up if upward else [(j, i) for i, j in up])  19.4 us
    all_to_all x1, waiting for transfers between devices, per_device(): lax.all_to_all(right_side.reshape(planes, group_size, local_radii, local_...  14.7 us
    add x3, other arithmetic, chebyshev(): direction = renewed * factor * direction + 2.0 * renewed / spread * residual  10.7 us
    dot_general x1, matrix products, per_device(): lax.dot_general(gridded.transpose(0, 2, 1, 3).reshape(planes * local_radi...  5.93 us
    unnamed x31, local copies, waits for them, and re-layouts  5.79 us
    reshape x1, local copies, waits for them, and re-layouts, per_device(): basis_table.reshape(points, *fold)  5.48 us
  transfers between devices with their start and end apart: 7, of which 6 were waited for; matrix products, arithmetic and copies ran while one was open for 15% of the time, Pallas kernels for 0%

profile of v4, /device:TPU:448, one launch (start us, length us, event | category | flops | bytes accessed | tf_op | source)
XLA Modules:
  0.0 170.9 jit_solution(14796781307461440526)
XLA Ops:
  0.0 3.1 %copy.36 = f32[16,8,32,128]{3,2,0,1:T(8,128)} copy(f32[16,8,32,128]{3,2,1,0:T(8,128)} %bitcast.106) | data formatting | bytes 4194304 | tf_op jit(solution)/shard_map/reshape | solution.py:120
  3.1 5.3 %all-to-all-start = ((f32[16,8,32,128]{3,2,0,1:T(8,128)}), f32[16,8,32,128]{3,2,0,1:T(8,128)S(1)}, u32[]{:S(2)}, u32[]{:S(2)}) async-start(f32[16,8,32,128]{3,2,0,1:T(8,128)} %copy.36), calls=%async_computation | async-start | bytes 4194304 | tf_op jit(solution)/shard_map/all_to_all | solution.py:119
  9.6 1.2 multiply_subtract_fusion
  10.8 2.9 %fusion.10 = f32[1024,1024]{1,0:T(8,128)} fusion(f32[32,32,1024]{2,1,0:T(8,128)S(1)} %get-tuple-element.26, f32[32,32,1024]{2,1,0:T(8,128)S(1)} %get-tuple-element.25, f32[1024]{0:T(1024)S(1)} %select_sqrt_fusion, pred[1024]{0:T(1024)(128)(4,1)S(1)} %iota_compare_fusion.2), kind=kLoop, calls=%fused_computation.17 | loop fusion | flops 2097152 | bytes 12588032 | tf_op jit(solution)/shard_map/mul | solution.py:51
  13.7 5.5 %copy.48 = f32[1024,1024]{0,1:T(8,128)} copy(f32[1024,1024]{1,0:T(8,128)} %fusion.10) | data formatting | bytes 8388608 | tf_op jit(solution)/shard_map/reshape | solution.py:129
  19.8 14.7 %all-to-all-done = f32[16,8,32,128]{3,2,0,1:T(8,128)S(1)} async-done(((f32[16,8,32,128]{3,2,0,1:T(8,128)}), f32[16,8,32,128]{3,2,0,1:T(8,128)S(1)}, u32[]{:S(2)}, u32[]{:S(2)}) %all-to-all-start) | async-done | bytes 2097184 | tf_op jit(solution)/shard_map/all_to_all | solution.py:119
  34.5 3.0 %copy.37 = f32[16,32,8,128]{3,2,1,0:T(8,128)} copy(f32[16,32,8,128]{3,1,0,2:T(8,128)S(1)} %bitcast.105) | data formatting | bytes 4194304 | tf_op jit(solution)/shard_map/transpose | solution.py:128
  37.5 2.8 %reshape.460 = f32[512,1024,1]{1,0,2:T(8,128)} reshape(f32[16,32,8,128]{3,2,1,0:T(8,128)} %copy.37) | data formatting | bytes 4194304 | tf_op jit(solution)/shard_map/reshape | solution.py:128
  40.2 5.9 %convolution_bitcast_fusion = f32[512,8,128]{0,2,1:T(8,128)S(1)} fusion(f32[1024,8,128]{0,2,1:T(8,128)} %bitcast.102, f32[512,1024,1]{1,0,2:T(8,128)} %reshape.460), kind=kOutput, calls=%fused_computation.69 | convolution fusion | flops 3221225472 | bytes 8388608 | tf_op jit(solution)/shard_map/dot_general | solution.py:127
  47.4 1.3 copy.39
  48.7 1.9 %collective-permute-start = (f32[8,32,8,128]{3,2,1,0:T(8,128)}, f32[8,32,8,128]{3,2,1,0:T(8,128)S(1)}, u32[]{:S(2)}, u32[]{:S(2)}) collective-permute-start(f32[8,32,8,128]{3,2,1,0:T(8,128)} %bitcast.107), channel_id=1, source_target_pairs={{0,8},{8,16},{16,24},{24,32},{32,40},{40,48},{48,56},{56,64},{64,7... | collective-permute-start | bytes 3145736 | tf_op jit(solution)/shard_map/ppermute | solution.py:16
  50.6 2.6 %copy.40 = f32[256,8,128]{2,1,0:T(8,128)} copy(f32[256,8,128]{0,2,1:T(8,128)} %get-tuple-element.23) | data formatting | bytes 2097152 | tf_op jit(solution)/shard_map/slice | solution.py:19
  53.2 6.6 %collective-permute-start.1 = (f32[8,32,8,128]{3,2,1,0:T(8,128)}, f32[8,32,8,128]{3,2,1,0:T(8,128)S(1)}, u32[]{:S(2)}, u32[]{:S(2)}) collective-permute-start(f32[8,32,8,128]{3,2,1,0:T(8,128)} %bitcast.108), channel_id=1, source_target_pairs={{8,0},{16,8},{24,16},{32,24},{40,32},{48,40},{56,48},{64,56},{72,6... | collective-permute-start | bytes 3145736 | tf_op jit(solution)/shard_map/ppermute | solution.py:16
  60.2 8.0 %collective-permute-done = f32[8,32,8,128]{3,2,1,0:T(8,128)S(1)} collective-permute-done((f32[8,32,8,128]{3,2,1,0:T(8,128)}, f32[8,32,8,128]{3,2,1,0:T(8,128)S(1)}, u32[]{:S(2)}, u32[]{:S(2)}) %collective-permute-start) | collective-permute-done | bytes 1048608 | tf_op jit(solution)/shard_map/ppermute | solution.py:16
  68.3 15.5 %collective-permute-done.1 = f32[8,32,8,128]{3,2,1,0:T(8,128)S(1)} collective-permute-done((f32[8,32,8,128]{3,2,1,0:T(8,128)}, f32[8,32,8,128]{3,2,1,0:T(8,128)S(1)}, u32[]{:S(2)}, u32[]{:S(2)}) %collective-permute-start.1) | collective-permute-done | bytes 1048608 | tf_op jit(solution)/shard_map/ppermute | solution.py:16
  85.7 3.4 %collective-permute-start.2 = (f32[16,4,8,128]{3,2,1,0:T(8,128)}, f32[16,4,8,128]{3,2,1,0:T(8,128)}, u32[]{:S(2)}, u32[]{:S(2)}) collective-permute-start(f32[16,4,8,128]{3,2,1,0:T(8,128)} %get-tuple-element.21), channel_id=1, source_target_pairs={{0,1},{1,2},{2,3},{3,4},{4,5},{5,6},{6,7},{8,9},{9,10},{10,11},{11... | collective-permute-start | bytes 786440 | tf_op jit(solution)/shard_map/ppermute | solution.py:16
  93.0 3.0 %copy.55 = f32[128,8,8,128]{3,2,1,0:T(8,128)} copy(f32[128,8,8,128]{3,1,2,0:T(8,128)S(1)} %bitcast.100) | data formatting | bytes 8388608
  95.9 1.8 %copy.41 = f32[512,8,128]{2,1,0:T(8,128)} copy(f32[512,8,128]{0,2,1:T(8,128)S(1)} %convolution_bitcast_fusion) | data formatting | bytes 4194304 | tf_op jit(solution)/shard_map/dot_general | solution.py:127
  97.8 1.4 collective-permute-start.3
  100.3 4.6 %collective-permute-start.4 = (f32[16,4,8,128]{3,2,1,0:T(8,128)S(1)}, f32[16,4,8,128]{3,2,1,0:T(8,128)S(1)}, u32[]{:S(2)}, u32[]{:S(2)}) collective-permute-start(f32[16,4,8,128]{3,2,1,0:T(8,128)S(1)} %get-tuple-element.19), channel_id=1, source_target_pairs={{0,1},{1,2},{2,3},{3,4},{4,5},{5,6},{6,7},{8,9},{9,10},{10,11},{11... | collective-permute-start | bytes 786440 | tf_op jit(solution)/shard_map/ppermute | solution.py:16
  104.8 1.5 collective-permute-start.5
  107.3 1.3 collective-permute-done.3
  108.6 2.0 %collective-permute-done.4 = f32[16,4,8,128]{3,2,1,0:T(8,128)S(1)} collective-permute-done((f32[16,4,8,128]{3,2,1,0:T(8,128)S(1)}, f32[16,4,8,128]{3,2,1,0:T(8,128)S(1)}, u32[]{:S(2)}, u32[]{:S(2)}) %collective-permute-start.4) | collective-permute-done | bytes 262176 | tf_op jit(solution)/shard_map/ppermute | solution.py:16
  110.7 4.1 %collective-permute-done.5 = f32[16,4,8,128]{3,2,1,0:T(8,128)S(1)} collective-permute-done((f32[16,4,8,128]{3,2,1,0:T(8,128)S(1)}, f32[16,4,8,128]{3,2,1,0:T(8,128)S(1)}, u32[]{:S(2)}, u32[]{:S(2)}) %collective-permute-start.5) | collective-permute-done | bytes 262176 | tf_op jit(solution)/shard_map/ppermute | solution.py:16
  114.8 4.1 %broadcast_divide_fusion = (f32[32,40,8,128]{3,2,1,0:T(8,128)S(1)}, f32[32,40,8,128]{3,2,1,0:T(8,128)S(1)}) fusion(f32[8,128]{1,0:T(8,128)S(1)} %get-tuple-element.9, f32[8,4,8,128]{3,2,1,0:T(8,128)S(1)} %get-tuple-element.30, f32[8,32,8,128]{3,2,1,0:T(8,128)} %copy-done.3, f32[8,4,8,128]{3,2,1,0:T(8,128)S(1)} %get-tuple-element.28, ...), kind=kLoop, calls=%fused_computation.47 | loop fusion | flops 11796480 | bytes 15732736 | tf_op jit(solution)/shard_map/div | solution.py:96
  119.6 4.9 %multiply_add_fusion = (f32[28,38,8,128]{3,2,1,0:T(8,128)S(1)}, f32[28,38,8,128]{3,2,1,0:T(8,128)S(1)}) fusion(f32[8,128]{1,0:T(8,128)S(1)} %get-tuple-element.34, f32[8,128]{1,0:T(8,128)S(1)} %get-tuple-element.32, f32[32,40,8,128]{3,2,1,0:T(8,128)S(1)} %get-tuple-element.16, f32[28,38]{1,0:T(8,128)S(1)} %slice_bitcast_fusion.1, f32[38]{0:T(128)S(1)} %copy-done.10, ...), kind=kLoop, calls=%fused_computation.13 | loop fusion | flops 17432576 | bytes 43749840 | tf_op jit(solution)/shard_map/add | solution.py:107
  125.1 2.7 %multiply_add_fusion.2 = (f32[24,36,8,128]{3,2,1,0:T(8,128)S(1)}, f32[24,36,8,128]{3,2,1,0:T(8,128)S(1)}) fusion(f32[8,128]{1,0:T(8,128)S(1)} %get-tuple-element.35, f32[8,128]{1,0:T(8,128)S(1)} %get-tuple-element.37, f32[28,38,8,128]{3,2,1,0:T(8,128)S(1)} %get-tuple-element.14, f32[24,36]{1,0:T(8,128)S(1)} %slice_bitcast_fusion.3, f32[36]{0:T(128)S(1)} %slice.236, ...), kind=kLoop, calls=%fused_computation.33 | loop fusion | flops 14155776 | bytes 35548832 | tf_op jit(solution)/shard_map/add | solution.py:107
  127.8 3.2 %multiply_add_fusion.3 = (f32[20,34,8,128]{3,2,1,0:T(8,128)S(1)}, f32[20,34,8,128]{3,2,1,0:T(8,128)S(1)}, f32[20,34,8,128]{3,2,1,0:T(8,128)S(1)}) fusion(f32[8,128]{1,0:T(8,128)S(1)} %get-tuple-element.36, f32[8,128]{1,0:T(8,128)S(1)} %get-tuple-element.33, f32[24,36,8,128]{3,2,1,0:T(8,128)S(1)} %get-tuple-element.12, f32[20,34]{1,0:T(8,128)S(1)} %slice_bitcast_fusion.2, ...), kind=kLoop, calls=%fused_computation.46 | loop fusion | flops 11141120 | bytes 30788528 | tf_op jit(solution)/shard_map/add | solution.py:107
  131.0 2.2 %fusion.36 = f32[16,32,8,128,1]{3,2,1,0,4:T(8,128)S(1)} fusion(f32[20,34,8,128]{3,2,1,0:T(8,128)S(1)} %get-tuple-element.10, f32[20,34,8,128]{3,2,1,0:T(8,128)S(1)} %get-tuple-element.11, f32[20,34,8,128]{3,2,1,0:T(8,128)S(1)} %get-tuple-element.18, f32[20,34,8,128]{3,2,1,0:T(8,128)S(1)} %slice.302, f32[20,34,8,128]{3,2,1,0:T(8,128)S(1)} %slice.301, ...), kind=kLoop, calls=%fused_computation.57 | loop fusion | flops 10485760 | bytes 25307392 | tf_op jit(solution)/shard_map/add | solution.py:109
  133.3 3.9 %fusion.42 = f32[16,8,32,128]{3,2,1,0:T(8,128)S(1)} fusion(f32[8,128,8,128]{3,2,1,0:T(8,128)S(1)} %bitcast.101, f32[16,32,8,128,1]{3,2,1,0,4:T(8,128)S(1)} %fusion.36), kind=kOutput, calls=%fused_computation.68 | convolution fusion | flops 3221225472 | bytes 8388608 | tf_op jit(solution)/shard_map/dot_general | solution.py:163
  137.4 32.0 %all_to_all.10 = f32[16,8,32,128]{3,2,0,1:T(8,128)S(1)} all-to-all(f32[16,8,32,128]{3,2,0,1:T(8,128)S(1)} %copy.44), channel_id=1, replica_groups=mesh['ax'=64,'md'=8] {'md'}, dimensions={1} | all-to-all | bytes 4194304 | tf_op jit(solution)/shard_map/all_to_all | solution.py:170
  169.4 1.5 copy.45
  (73 shorter events, 12.6 us)
Async XLA Ops:
  3.1 31.3 %all-to-all-start = ((f32[16,8,32,128]{3,2,0,1:T(8,128)}), f32[16,8,32,128]{3,2,0,1:T(8,128)S(1)}, u32[]{:S(2)}, u32[]{:S(2)}) async-start(f32[16,8,32,128]{3,2,0,1:T(8,128)} %copy.36), calls=%async_computation | async-start | bytes 4194304 | tf_op jit(solution)/shard_map/all_to_all | solution.py:119
  13.7 5.5 %copy-start.8 = (f32[255]{0:T(256)S(1)}, f32[255]{0:T(256)}, u32[]{:S(2)}) copy-start(f32[255]{0:T(256)} %param.5) | copy-start | bytes 3064
  13.7 5.6 %copy-start.6 = (f32[256]{0:T(256)S(1)}, f32[256]{0:T(256)}, u32[]{:S(2)}) copy-start(f32[256]{0:T(256)} %param.7) | copy-start | bytes 3076
  13.7 5.6 %copy-start.7 = (f32[256]{0:T(256)S(1)}, f32[256]{0:T(256)}, u32[]{:S(2)}) copy-start(f32[256]{0:T(256)} %param.6) | copy-start | bytes 3076
  48.7 19.5 %collective-permute-start = (f32[8,32,8,128]{3,2,1,0:T(8,128)}, f32[8,32,8,128]{3,2,1,0:T(8,128)S(1)}, u32[]{:S(2)}, u32[]{:S(2)}) collective-permute-start(f32[8,32,8,128]{3,2,1,0:T(8,128)} %bitcast.107), channel_id=1, source_target_pairs={{0,8},{8,16},{16,24},{24,32},{32,40},{40,48},{48,56},{56,64},{64,7... | collective-permute-start | bytes 3145736 | tf_op jit(solution)/shard_map/ppermute | solution.py:16
  53.2 30.5 %collective-permute-start.1 = (f32[8,32,8,128]{3,2,1,0:T(8,128)}, f32[8,32,8,128]{3,2,1,0:T(8,128)S(1)}, u32[]{:S(2)}, u32[]{:S(2)}) collective-permute-start(f32[8,32,8,128]{3,2,1,0:T(8,128)} %bitcast.108), channel_id=1, source_target_pairs={{8,0},{16,8},{24,16},{32,24},{40,32},{48,40},{56,48},{64,56},{72,6... | collective-permute-start | bytes 3145736 | tf_op jit(solution)/shard_map/ppermute | solution.py:16
  68.3 24.7 %copy-start = (f32[1024,1024]{1,0:T(8,128)S(1)}, f32[1024,1024]{1,0:T(8,128)}, u32[]{:S(2)}) copy-start(f32[1024,1024]{1,0:T(8,128)} %fusion.10) | copy-start | bytes 12582916
  83.7 1.0 copy-start.3
  85.7 20.6 %collective-permute-start.2 = (f32[16,4,8,128]{3,2,1,0:T(8,128)}, f32[16,4,8,128]{3,2,1,0:T(8,128)}, u32[]{:S(2)}, u32[]{:S(2)}) collective-permute-start(f32[16,4,8,128]{3,2,1,0:T(8,128)} %get-tuple-element.21), channel_id=1, source_target_pairs={{0,1},{1,2},{2,3},{3,4},{4,5},{5,6},{6,7},{8,9},{9,10},{10,11},{11... | collective-permute-start | bytes 786440 | tf_op jit(solution)/shard_map/ppermute | solution.py:16
  97.8 17.0 %copy-start.2 = (f32[512,8,128]{2,1,0:T(8,128)S(1)}, f32[512,8,128]{2,1,0:T(8,128)}, u32[]{:S(2)}) copy-start(f32[512,8,128]{2,1,0:T(8,128)} %copy.41) | copy-start | bytes 6291460
  97.8 10.9 %collective-permute-start.3 = (f32[16,4,8,128]{3,2,1,0:T(8,128)}, f32[16,4,8,128]{3,2,1,0:T(8,128)S(1)}, u32[]{:S(2)}, u32[]{:S(2)}) collective-permute-start(f32[16,4,8,128]{3,2,1,0:T(8,128)} %get-tuple-element.22), channel_id=1, source_target_pairs={{1,0},{2,1},{3,2},{4,3},{5,4},{6,5},{7,6},{9,8},{10,9},{11,10},{12... | collective-permute-start | bytes 786440 | tf_op jit(solution)/shard_map/ppermute | solution.py:16
  100.3 10.4 %collective-permute-start.4 = (f32[16,4,8,128]{3,2,1,0:T(8,128)S(1)}, f32[16,4,8,128]{3,2,1,0:T(8,128)S(1)}, u32[]{:S(2)}, u32[]{:S(2)}) collective-permute-start(f32[16,4,8,128]{3,2,1,0:T(8,128)S(1)} %get-tuple-element.19), channel_id=1, source_target_pairs={{0,1},{1,2},{2,3},{3,4},{4,5},{5,6},{6,7},{8,9},{9,10},{10,11},{11... | collective-permute-start | bytes 786440 | tf_op jit(solution)/shard_map/ppermute | solution.py:16
  104.8 10.0 %collective-permute-start.5 = (f32[16,4,8,128]{3,2,1,0:T(8,128)S(1)}, f32[16,4,8,128]{3,2,1,0:T(8,128)S(1)}, u32[]{:S(2)}, u32[]{:S(2)}) collective-permute-start(f32[16,4,8,128]{3,2,1,0:T(8,128)S(1)} %get-tuple-element.20), channel_id=1, source_target_pairs={{1,0},{2,1},{3,2},{4,3},{5,4},{6,5},{7,6},{9,8},{10,9},{11,10},{12... | collective-permute-start | bytes 786440 | tf_op jit(solution)/shard_map/ppermute | solution.py:16
  118.9 0.6 copy-start.10
  118.9 0.7 copy-start.11
  124.4 0.7 copy-start.9
  125.1 2.7 %copy-start.4 = (f32[34,8,128]{2,1,0:T(8,128)S(1)}, f32[34,8,128]{2,1,0:T(8,128)}, u32[]{:S(2)}) copy-start(f32[34,8,128]{2,1,0:T(8,128)} %slice.330) | copy-start | bytes 417796
  127.8 3.2 %copy-start.5 = (f32[4,8,8,128]{3,2,1,0:T(8,128)S(1)}, f32[4,8,8,128]{3,2,1,0:T(8,128)}, u32[]{:S(2)}) copy-start(f32[4,8,8,128]{3,2,1,0:T(8,128)} %copy.54) | copy-start | bytes 393220
  131.0 2.3 %copy-start.1 = (f32[128,8,8,128]{3,2,1,0:T(8,128)S(1)}, f32[128,8,8,128]{3,2,1,0:T(8,128)}, u32[]{:S(2)}) copy-start(f32[128,8,8,128]{3,2,1,0:T(8,128)} %copy.55) | copy-start | bytes 12582916

commit v5 on v2

--- a/solution.py
+++ b/solution.py
@@ -119,7 +119,7 @@
     spectral = jnp.dot(
         gridded.transpose(0, 2, 1, 3).reshape(planes * local_radii, points),
         basis_table,
-        precision=lax.Precision.HIGH,
+        precision=lax.Precision.HIGHEST,
         preferred_element_type=jnp.float32,
     ).reshape(planes, local_radii, points)
     wavenumber = wave_numbers(points, points)
@@ -157,7 +157,7 @@
     solved = jnp.dot(
         solution.reshape(planes * local_radii, points),
         basis_table.T,
-        precision=lax.Precision.HIGH,
+        precision=lax.Precision.HIGHEST,
         preferred_element_type=jnp.float32,
     ).reshape(planes, local_radii, group_size, local_points).transpose(0, 2, 1, 3)
     returned = lax.all_to_all(solved, "md", split_axis=1, concat_axis=1, tiled=True)

time: 161 us -> 171 us (1.062)
  matrix products: 12.4 us -> 22.6 us
    dot_general x1, matrix products: 6.95 us -> 13.8 us  [per_device(): jnp.dot(gridded.transpose(0, 2, 1, 3).reshape(planes * local_radii, point...]
    dot_general x1, matrix products: 5.43 us -> 8.8 us  [per_device(): jnp.dot(solution.reshape(planes * local_radii, points), basis_table.T, pr...]
  transfers between devices with their start and end apart: 5 -> 5, of which waited for: 5 -> 5; matrix products, arithmetic and copies ran while one was open for 10% -> 9% of each run, Pallas kernels for 0% -> 0%
where the time goes in v5:
time: 171 us; the launch traced here: 170 us
  waiting for transfers between devices  51.5 us (30%)
  blocking collectives  32.9 us (19%)
  local copies, waits for them, and re-layouts  23.3 us (14%)
  matrix products  22.6 us (13%)
  other arithmetic  21.1 us (12%)
  starting transfers between devices  18.4 us (11%)
    all_to_all x1, blocking collectives, per_device(): lax.all_to_all(solved, 'md', split_axis=1, concat_axis=1, tiled=True)  32.9 us
    all_to_all x1, waiting for transfers between devices, per_device(): lax.all_to_all(right_side.reshape(planes, group_size, local_radii, local_...  20.5 us
    ppermute x2, waiting for transfers between devices, with_halo(): after = lax.ppermute(leading, axis, down)  18.2 us
    dot_general x1, matrix products, per_device(): jnp.dot(gridded.transpose(0, 2, 1, 3).reshape(planes * local_radii, point...  13.8 us
    ppermute x2, waiting for transfers between devices, with_halo(): before = lax.ppermute(last, axis, up)  12.9 us
    add x3, other arithmetic, chebyshev(): direction = renewed * factor * direction + 2.0 * renewed / spread * residual  10.8 us
    dot_general x1, matrix products, per_device(): jnp.dot(solution.reshape(planes * local_radii, points), basis_table.T, pr...  8.8 us
    ppermute x2, starting transfers between devices, with_halo(): after = lax.ppermute(leading, axis, down)  7.93 us
  transfers between devices with their start and end apart: 5, of which 5 were waited for; matrix products, arithmetic and copies ran while one was open for 9% of the time, Pallas kernels for 0%

profile of v5, /device:TPU:448, one launch (start us, length us, event | category | flops | bytes accessed | tf_op | source)
XLA Modules:
  0.0 170.3 jit_solution(10429579232816552951)
XLA Ops:
  0.0 3.1 %copy.22 = f32[16,8,32,128]{3,2,0,1:T(8,128)} copy(f32[16,8,32,128]{3,2,1,0:T(8,128)} %bitcast.116) | data formatting | bytes 4194304 | tf_op jit(solution)/shard_map/reshape | solution.py:113
  3.1 5.3 %all-to-all-start = ((f32[16,8,32,128]{3,2,0,1:T(8,128)}), f32[16,8,32,128]{3,2,0,1:T(8,128)S(1)}, u32[]{:S(2)}, u32[]{:S(2)}) async-start(f32[16,8,32,128]{3,2,0,1:T(8,128)} %copy.22), calls=%async_computation | async-start | bytes 4194304 | tf_op jit(solution)/shard_map/all_to_all | solution.py:112
  9.6 1.2 multiply_subtract_fusion
  10.8 2.9 %fusion.8 = f32[1024,1024]{1,0:T(8,128)} fusion(f32[32,32,1024]{2,1,0:T(8,128)S(1)} %get-tuple-element.24, f32[32,32,1024]{2,1,0:T(8,128)S(1)} %get-tuple-element.23, f32[1024]{0:T(1024)S(1)} %select_sqrt_fusion, pred[1024]{0:T(1024)(128)(4,1)S(1)} %iota_compare_fusion.2), kind=kLoop, calls=%fused_computation.15 | loop fusion | flops 2097152 | bytes 12588032 | tf_op jit(solution)/shard_map/mul | solution.py:44
  14.0 20.5 %all-to-all-done = f32[16,8,32,128]{3,2,0,1:T(8,128)S(1)} async-done(((f32[16,8,32,128]{3,2,0,1:T(8,128)}), f32[16,8,32,128]{3,2,0,1:T(8,128)S(1)}, u32[]{:S(2)}, u32[]{:S(2)}) %all-to-all-start) | async-done | bytes 2097184 | tf_op jit(solution)/shard_map/all_to_all | solution.py:112
  34.5 1.7 copy.23
  36.7 13.8 %fusion.45 = f32[512,1024]{0,1:T(8,128)S(1)} fusion(f32[1024,1024]{1,0:T(8,128)S(1)} %copy-done, f32[64,8,8,128]{3,2,1,0:T(8,128)S(1)} %bitcast.110), kind=kOutput, calls=%fused_computation.70 | convolution fusion | flops 6442450944 | bytes 8388608 | tf_op jit(solution)/shard_map/dot_general | solution.py:119
  50.5 1.5 fusion.73
  52.0 1.6 copy.24
  53.6 1.2 copy.31
  54.8 1.9 %collective-permute-start = (f32[8,32,8,128]{3,2,1,0:T(8,128)}, f32[8,32,8,128]{3,2,1,0:T(8,128)}, u32[]{:S(2)}, u32[]{:S(2)}) collective-permute-start(f32[8,32,8,128]{3,2,1,0:T(8,128)} %bitcast.22), channel_id=1, source_target_pairs={{0,8},{8,16},{16,24},{24,32},{32,40},{40,48},{48,56},{56,64},{64,7... | collective-permute-start | bytes 3145736 | tf_op jit(solution)/shard_map/ppermute | solution.py:18
  57.0 1.6 copy.26
  58.6 1.2 copy.33
  59.8 6.6 %collective-permute-start.1 = (f32[8,32,8,128]{3,2,1,0:T(8,128)}, f32[8,32,8,128]{3,2,1,0:T(8,128)S(1)}, u32[]{:S(2)}, u32[]{:S(2)}) collective-permute-start(f32[8,32,8,128]{3,2,1,0:T(8,128)} %bitcast.28), channel_id=1, source_target_pairs={{8,0},{16,8},{24,16},{32,24},{40,32},{48,40},{56,48},{64,56},{72,6... | collective-permute-start | bytes 3145736 | tf_op jit(solution)/shard_map/ppermute | solution.py:19
  67.3 1.8 %copy.25 = f32[512,1024]{1,0:T(8,128)} copy(f32[512,1024]{0,1:T(8,128)S(1)} %fusion.45) | data formatting | bytes 4194304 | tf_op jit(solution)/shard_map/dot_general | solution.py:119
  69.1 2.1 %copy.32 = f32[64,8,8,128]{3,2,1,0:T(8,128)S(1)} copy(f32[64,8,8,128]{3,1,2,0:T(8,128)} %bitcast.113) | data formatting | bytes 4194304
  71.2 3.2 %collective-permute-done = f32[8,32,8,128]{3,2,1,0:T(8,128)} collective-permute-done((f32[8,32,8,128]{3,2,1,0:T(8,128)}, f32[8,32,8,128]{3,2,1,0:T(8,128)}, u32[]{:S(2)}, u32[]{:S(2)}) %collective-permute-start) | collective-permute-done | bytes 1048608 | tf_op jit(solution)/shard_map/ppermute | solution.py:18
  74.4 1.3 constant_dynamic-update-slice_fusion.1
  75.8 14.0 %collective-permute-done.1 = f32[8,32,8,128]{3,2,1,0:T(8,128)S(1)} collective-permute-done((f32[8,32,8,128]{3,2,1,0:T(8,128)}, f32[8,32,8,128]{3,2,1,0:T(8,128)S(1)}, u32[]{:S(2)}, u32[]{:S(2)}) %collective-permute-start.1) | collective-permute-done | bytes 1048608 | tf_op jit(solution)/shard_map/ppermute | solution.py:19
  90.0 3.2 %collective-permute-start.2 = (f32[32,4,8,128]{3,2,1,0:T(8,128)S(1)}, f32[32,4,8,128]{3,2,1,0:T(8,128)S(1)}, u32[]{:S(2)}, u32[]{:S(2)}) collective-permute-start(f32[32,4,8,128]{3,2,1,0:T(8,128)S(1)} %get-tuple-element.18), channel_id=1, source_target_pairs={{0,1},{1,2},{2,3},{3,4},{4,5},{5,6},{6,7},{8,9},{9,10},{10,11},{11... | collective-permute-start | bytes 1572872 | tf_op jit(solution)/shard_map/ppermute | solution.py:18
  93.2 1.3 collective-permute-start.3
  95.5 9.7 %collective-permute-done.2 = f32[32,4,8,128]{3,2,1,0:T(8,128)S(1)} collective-permute-done((f32[32,4,8,128]{3,2,1,0:T(8,128)S(1)}, f32[32,4,8,128]{3,2,1,0:T(8,128)S(1)}, u32[]{:S(2)}, u32[]{:S(2)}) %collective-permute-start.2) | collective-permute-done | bytes 524320 | tf_op jit(solution)/shard_map/ppermute | solution.py:18
  105.2 4.1 %collective-permute-done.3 = f32[32,4,8,128]{3,2,1,0:T(8,128)S(1)} collective-permute-done((f32[32,4,8,128]{3,2,1,0:T(8,128)S(1)}, f32[32,4,8,128]{3,2,1,0:T(8,128)S(1)}, u32[]{:S(2)}, u32[]{:S(2)}) %collective-permute-start.3) | collective-permute-done | bytes 524320 | tf_op jit(solution)/shard_map/ppermute | solution.py:19
  109.4 1.2 pad_maximum_fusion
  110.8 5.0 %multiply_add_fusion = (f32[28,38,8,128]{3,2,1,0:T(8,128)S(1)}, f32[28,38,8,128]{3,2,1,0:T(8,128)S(1)}) fusion(f32[8,128]{1,0:T(8,128)S(1)} %get-tuple-element.28, f32[8,128]{1,0:T(8,128)S(1)} %get-tuple-element.26, f32[32,40,8,128]{3,2,1,0:T(8,128)S(1)} %get-tuple-element.17, f32[28,38]{1,0:T(8,128)S(1)} %slice_bitcast_fusion.1, f32[38]{0:T(128)S(1)} %slice.199, ...), kind=kLoop, calls=%fused_computation.13 | loop fusion | flops 17432576 | bytes 43749840 | tf_op jit(solution)/shard_map/add | solution.py:100
  115.9 2.7 %multiply_add_fusion.2 = (f32[24,36,8,128]{3,2,1,0:T(8,128)S(1)}, f32[24,36,8,128]{3,2,1,0:T(8,128)S(1)}) fusion(f32[8,128]{1,0:T(8,128)S(1)} %get-tuple-element.29, f32[8,128]{1,0:T(8,128)S(1)} %get-tuple-element.31, f32[28,38,8,128]{3,2,1,0:T(8,128)S(1)} %get-tuple-element.14, f32[24,36]{1,0:T(8,128)S(1)} %slice_bitcast_fusion.3, f32[36]{0:T(128)S(1)} %slice.212, ...), kind=kLoop, calls=%fused_computation.30 | loop fusion | flops 14155776 | bytes 35548832 | tf_op jit(solution)/shard_map/add | solution.py:100
  118.7 3.2 %multiply_add_fusion.3 = (f32[20,34,8,128]{3,2,1,0:T(8,128)S(1)}, f32[20,34,8,128]{3,2,1,0:T(8,128)S(1)}, f32[20,34,8,128]{3,2,1,0:T(8,128)S(1)}) fusion(f32[8,128]{1,0:T(8,128)S(1)} %get-tuple-element.30, f32[8,128]{1,0:T(8,128)S(1)} %get-tuple-element.27, f32[24,36,8,128]{3,2,1,0:T(8,128)S(1)} %get-tuple-element.12, f32[20,34]{1,0:T(8,128)S(1)} %slice_bitcast_fusion.2, ...), kind=kLoop, calls=%fused_computation.43 | loop fusion | flops 11141120 | bytes 30788528 | tf_op jit(solution)/shard_map/add | solution.py:100
  121.8 3.2 %fusion.35 = f32[16,32,8,128]{3,2,1,0:T(8,128)} fusion(f32[20,34,8,128]{3,2,1,0:T(8,128)S(1)} %get-tuple-element.10, f32[20,34,8,128]{3,2,1,0:T(8,128)S(1)} %get-tuple-element.11, f32[20,34,8,128]{3,2,1,0:T(8,128)S(1)} %get-tuple-element.20, f32[20,34,8,128]{3,2,1,0:T(8,128)S(1)} %slice.272, f32[20,34,8,128]{3,2,1,0:T(8,128)S(1)} %slice.271, ...), kind=kLoop, calls=%fused_computation.57 | loop fusion | flops 10485760 | bytes 25307392 | tf_op jit(solution)/shard_map/add | solution.py:102
  125.0 1.7 %reshape.450 = f32[16,32,1024,1]{2,1,0,3:T(8,128)S(1)} reshape(f32[16,32,8,128]{3,2,1,0:T(8,128)} %fusion.35) | data formatting | bytes 4194304 | tf_op jit(solution)/shard_map/dot_general | solution.py:157
  126.8 8.8 %fusion.42 = f32[16,8,32,128]{3,2,1,0:T(8,128)S(1)} fusion(f32[8,128,1024,1]{2,1,0,3:T(8,128)} %bitcast.109, f32[16,32,1024,1]{2,1,0,3:T(8,128)S(1)} %reshape.450), kind=kOutput, calls=%fused_computation.69 | convolution fusion | flops 6442450944 | bytes 8388608 | tf_op jit(solution)/shard_map/dot_general | solution.py:157
  135.8 32.9 %all_to_all.10 = f32[16,8,32,128]{3,2,0,1:T(8,128)S(1)} all-to-all(f32[16,8,32,128]{3,2,0,1:T(8,128)S(1)} %copy.27), channel_id=1, replica_groups=mesh['ax'=64,'md'=8] {'md'}, dimensions={1} | all-to-all | bytes 4194304 | tf_op jit(solution)/shard_map/all_to_all | solution.py:163
  168.7 1.5 copy.28
  (54 shorter events, 4.9 us)
Async XLA Ops:
  3.1 31.3 %all-to-all-start = ((f32[16,8,32,128]{3,2,0,1:T(8,128)}), f32[16,8,32,128]{3,2,0,1:T(8,128)S(1)}, u32[]{:S(2)}, u32[]{:S(2)}) async-start(f32[16,8,32,128]{3,2,0,1:T(8,128)} %copy.22), calls=%async_computation | async-start | bytes 4194304 | tf_op jit(solution)/shard_map/all_to_all | solution.py:112
  10.8 3.0 %copy-start.4 = (f32[255]{0:T(256)S(1)}, f32[255]{0:T(256)}, u32[]{:S(2)}) copy-start(f32[255]{0:T(256)} %param.5) | copy-start | bytes 3064
  34.5 2.2 %copy-start = (f32[1024,1024]{1,0:T(8,128)S(1)}, f32[1024,1024]{1,0:T(8,128)}, u32[]{:S(2)}) copy-start(f32[1024,1024]{1,0:T(8,128)} %fusion.8) | copy-start | bytes 12582916
  50.5 6.2 %copy-start.2 = (f32[256]{0:T(256)S(1)}, f32[256]{0:T(256)}, u32[]{:S(2)}) copy-start(f32[256]{0:T(256)} %param.7) | copy-start | bytes 3076
  50.5 6.2 %copy-start.3 = (f32[256]{0:T(256)S(1)}, f32[256]{0:T(256)}, u32[]{:S(2)}) copy-start(f32[256]{0:T(256)} %param.6) | copy-start | bytes 3076
  54.8 19.6 %collective-permute-start = (f32[8,32,8,128]{3,2,1,0:T(8,128)}, f32[8,32,8,128]{3,2,1,0:T(8,128)}, u32[]{:S(2)}, u32[]{:S(2)}) collective-permute-start(f32[8,32,8,128]{3,2,1,0:T(8,128)} %bitcast.22), channel_id=1, source_target_pairs={{0,8},{8,16},{16,24},{24,32},{32,40},{40,48},{48,56},{56,64},{64,7... | collective-permute-start | bytes 3145736 | tf_op jit(solution)/shard_map/ppermute | solution.py:18
  59.8 30.1 %collective-permute-start.1 = (f32[8,32,8,128]{3,2,1,0:T(8,128)}, f32[8,32,8,128]{3,2,1,0:T(8,128)S(1)}, u32[]{:S(2)}, u32[]{:S(2)}) collective-permute-start(f32[8,32,8,128]{3,2,1,0:T(8,128)} %bitcast.28), channel_id=1, source_target_pairs={{8,0},{16,8},{24,16},{32,24},{40,32},{48,40},{56,48},{64,56},{72,6... | collective-permute-start | bytes 3145736 | tf_op jit(solution)/shard_map/ppermute | solution.py:19
  75.8 19.4 %copy-start.1 = (f32[4,8,8,128]{3,1,2,0:T(8,128)S(1)}, f32[4,8,8,128]{3,1,2,0:T(8,128)}, u32[]{:S(2)}) copy-start(f32[4,8,8,128]{3,1,2,0:T(8,128)} %slice_bitcast_fusion) | copy-start | bytes 393220
  90.0 15.2 %collective-permute-start.2 = (f32[32,4,8,128]{3,2,1,0:T(8,128)S(1)}, f32[32,4,8,128]{3,2,1,0:T(8,128)S(1)}, u32[]{:S(2)}, u32[]{:S(2)}) collective-permute-start(f32[32,4,8,128]{3,2,1,0:T(8,128)S(1)} %get-tuple-element.18), channel_id=1, source_target_pairs={{0,1},{1,2},{2,3},{3,4},{4,5},{5,6},{6,7},{8,9},{9,10},{10,11},{11... | collective-permute-start | bytes 1572872 | tf_op jit(solution)/shard_map/ppermute | solution.py:18
  93.2 16.2 %collective-permute-start.3 = (f32[32,4,8,128]{3,2,1,0:T(8,128)S(1)}, f32[32,4,8,128]{3,2,1,0:T(8,128)S(1)}, u32[]{:S(2)}, u32[]{:S(2)}) collective-permute-start(f32[32,4,8,128]{3,2,1,0:T(8,128)S(1)} %get-tuple-element.19), channel_id=1, source_target_pairs={{1,0},{2,1},{3,2},{4,3},{5,4},{6,5},{7,6},{9,8},{10,9},{11,10},{12... | collective-permute-start | bytes 1572872 | tf_op jit(solution)/shard_map/ppermute | solution.py:19

commit v6 on v3

--- a/solution.py
+++ b/solution.py
@@ -121,7 +121,7 @@
         gridded.transpose(0, 2, 1, 3).reshape(planes * local_radii, points),
         basis_table.reshape(points, *fold),
         (((1,), (0,)), ((), ())),
-        precision=lax.Precision.HIGH,
+        precision=lax.Precision.HIGHEST,
         preferred_element_type=jnp.float32,
     ).reshape(planes, local_radii, *fold)
     wavenumber = wave_numbers(points, points)

time: 161 us -> 164 us (1.019)
  matrix products: 9.26 us -> 12.6 us
    dot_general x1, matrix products: 5.34 us -> 8.7 us  [per_device(): lax.dot_general(gridded.transpose(0, 2, 1, 3).reshape(planes * local_radi...]
where the time goes in v6:
time: 164 us
  waiting for transfers between devices  43.6 us (27%)
  blocking collectives  32.8 us (20%)
  local copies, waits for them, and re-layouts  28.9 us (18%)
  other arithmetic  26.9 us (16%)
  starting transfers between devices  18.4 us (11%)
  matrix products  12.6 us (8%)
    all_to_all x1, blocking collectives, per_device(): lax.all_to_all(solved, 'md', split_axis=1, concat_axis=1, tiled=True)  32.8 us
    ppermute x2, waiting for transfers between devices, with_halo(): after = lax.ppermute(leading, axis, down)  19.8 us
    all_to_all x1, waiting for transfers between devices, per_device(): lax.all_to_all(right_side.reshape(planes, group_size, local_radii, local_...  14.4 us
    add x3, other arithmetic, chebyshev(): direction = renewed * factor * direction + 2.0 * renewed / spread * residual  12.3 us
    ppermute x2, waiting for transfers between devices, with_halo(): before = lax.ppermute(last, axis, up)  9.38 us
    dot_general x1, matrix products, per_device(): lax.dot_general(gridded.transpose(0, 2, 1, 3).reshape(planes * local_radi...  8.7 us
    ppermute x2, starting transfers between devices, with_halo(): after = lax.ppermute(leading, axis, down)  7.82 us
    all_to_all x1, starting transfers between devices, per_device(): lax.all_to_all(right_side.reshape(planes, group_size, local_radii, local_...  5.76 us
  transfers between devices with their start and end apart: 5, of which 5 were waited for; matrix products, arithmetic and copies ran while one was open for 12% of the time, Pallas kernels for 0%

profile of v6, /device:TPU:488, one launch (start us, length us, event | category | flops | bytes accessed | tf_op | source)
XLA Modules:
  0.0 163.6 jit_solution(13130941715973653755)
XLA Ops:
  0.0 3.1 %copy.34 = f32[16,8,32,128]{3,2,0,1:T(8,128)} copy(f32[16,8,32,128]{3,2,1,0:T(8,128)} %bitcast.106) | data formatting | bytes 4194304 | tf_op jit(solution)/shard_map/reshape | solution.py:113
  3.1 5.8 %all-to-all-start = ((f32[16,8,32,128]{3,2,0,1:T(8,128)}), f32[16,8,32,128]{3,2,0,1:T(8,128)S(1)}, u32[]{:S(2)}, u32[]{:S(2)}) async-start(f32[16,8,32,128]{3,2,0,1:T(8,128)} %copy.34), calls=%async_computation | async-start | bytes 4194304 | tf_op jit(solution)/shard_map/all_to_all | solution.py:112
  8.9 1.1 fusion.60
  10.0 1.2 multiply_subtract_fusion
  11.2 2.9 %fusion.10 = f32[1024,1024]{1,0:T(8,128)} fusion(f32[32,32,1024]{2,1,0:T(8,128)S(1)} %get-tuple-element.24, f32[32,32,1024]{2,1,0:T(8,128)S(1)} %get-tuple-element.23, f32[1024]{0:T(1024)S(1)} %select_sqrt_fusion, pred[1024]{0:T(1024)(128)(4,1)S(1)} %iota_compare_fusion.2), kind=kLoop, calls=%fused_computation.17 | loop fusion | flops 2097152 | bytes 12588032 | tf_op jit(solution)/shard_map/mul | solution.py:44
  14.2 5.5 %copy.46 = f32[1024,1024]{0,1:T(8,128)} copy(f32[1024,1024]{1,0:T(8,128)} %fusion.10) | data formatting | bytes 8388608 | tf_op jit(solution)/shard_map/reshape | solution.py:122
  20.0 14.4 %all-to-all-done = f32[16,8,32,128]{3,2,0,1:T(8,128)S(1)} async-done(((f32[16,8,32,128]{3,2,0,1:T(8,128)}), f32[16,8,32,128]{3,2,0,1:T(8,128)S(1)}, u32[]{:S(2)}, u32[]{:S(2)}) %all-to-all-start) | async-done | bytes 2097184 | tf_op jit(solution)/shard_map/all_to_all | solution.py:112
  34.4 3.0 %copy.35 = f32[16,32,8,128]{3,2,1,0:T(8,128)} copy(f32[16,32,8,128]{3,1,0,2:T(8,128)S(1)} %bitcast.105) | data formatting | bytes 4194304 | tf_op jit(solution)/shard_map/transpose | solution.py:121
  37.3 1.7 %reshape.460 = f32[512,1024,1]{1,0,2:T(8,128)S(1)} reshape(f32[16,32,8,128]{3,2,1,0:T(8,128)} %copy.35) | data formatting | bytes 4194304 | tf_op jit(solution)/shard_map/reshape | solution.py:121
  39.1 8.7 %convolution_bitcast_fusion = f32[512,8,128]{0,2,1:T(8,128)S(1)} fusion(f32[1024,8,128]{0,2,1:T(8,128)} %bitcast.104, f32[512,1024,1]{1,0,2:T(8,128)S(1)} %reshape.460), kind=kOutput, calls=%fused_computation.69 | convolution fusion | flops 6442450944 | bytes 8388608 | tf_op jit(solution)/shard_map/dot_general | solution.py:120
  47.8 1.3 copy-done.1
  49.3 1.3 copy.37
  50.7 1.3 copy.39
  52.0 2.5 %collective-permute-start.1 = (f32[8,32,8,128]{3,2,1,0:T(8,128)}, f32[8,32,8,128]{3,2,1,0:T(8,128)S(1)}, u32[]{:S(2)}, u32[]{:S(2)}) collective-permute-start(f32[8,32,8,128]{3,2,1,0:T(8,128)} %bitcast.8), channel_id=1, source_target_pairs={{8,0},{16,8},{24,16},{32,24},{40,32},{48,40},{56,48},{64,56},{72,6... | collective-permute-start | bytes 3145736 | tf_op jit(solution)/shard_map/ppermute | solution.py:19
  54.4 1.9 %collective-permute-start = (f32[8,32,8,128]{3,2,1,0:T(8,128)}, f32[8,32,8,128]{3,2,1,0:T(8,128)}, u32[]{:S(2)}, u32[]{:S(2)}) collective-permute-start(f32[8,32,8,128]{3,2,1,0:T(8,128)} %bitcast.107), channel_id=1, source_target_pairs={{0,8},{8,16},{16,24},{24,32},{32,40},{40,48},{48,56},{56,64},{64,7... | collective-permute-start | bytes 3145736 | tf_op jit(solution)/shard_map/ppermute | solution.py:18
  58.1 2.1 %copy.38 = f32[512,8,128]{2,1,0:T(8,128)S(1)} copy(f32[512,8,128]{0,2,1:T(8,128)} %copy-done.1) | data formatting | bytes 4194304 | tf_op jit(solution)/shard_map/dot_general | solution.py:120
  60.2 18.1 %collective-permute-done.1 = f32[8,32,8,128]{3,2,1,0:T(8,128)S(1)} collective-permute-done((f32[8,32,8,128]{3,2,1,0:T(8,128)}, f32[8,32,8,128]{3,2,1,0:T(8,128)S(1)}, u32[]{:S(2)}, u32[]{:S(2)}) %collective-permute-start.1) | collective-permute-done | bytes 1048608 | tf_op jit(solution)/shard_map/ppermute | solution.py:19
  78.3 5.0 %collective-permute-done = f32[8,32,8,128]{3,2,1,0:T(8,128)} collective-permute-done((f32[8,32,8,128]{3,2,1,0:T(8,128)}, f32[8,32,8,128]{3,2,1,0:T(8,128)}, u32[]{:S(2)}, u32[]{:S(2)}) %collective-permute-start) | collective-permute-done | bytes 1048608 | tf_op jit(solution)/shard_map/ppermute | solution.py:18
  83.3 1.2 pad_maximum_fusion.3
  84.5 2.9 %collective-permute-start.2 = (f32[32,4,8,128]{3,2,1,0:T(8,128)S(1)}, f32[32,4,8,128]{3,2,1,0:T(8,128)S(1)}, u32[]{:S(2)}, u32[]{:S(2)}) collective-permute-start(f32[32,4,8,128]{3,2,1,0:T(8,128)S(1)} %get-tuple-element.18), channel_id=1, source_target_pairs={{0,1},{1,2},{2,3},{3,4},{4,5},{5,6},{6,7},{8,9},{9,10},{10,11},{11... | collective-permute-start | bytes 1572872 | tf_op jit(solution)/shard_map/ppermute | solution.py:18
  87.4 5.4 %collective-permute-start.3 = (f32[32,4,8,128]{3,2,1,0:T(8,128)S(1)}, f32[32,4,8,128]{3,2,1,0:T(8,128)S(1)}, u32[]{:S(2)}, u32[]{:S(2)}) collective-permute-start(f32[32,4,8,128]{3,2,1,0:T(8,128)S(1)} %get-tuple-element.19), channel_id=1, source_target_pairs={{1,0},{2,1},{3,2},{4,3},{5,4},{6,5},{7,6},{9,8},{10,9},{11,10},{12... | collective-permute-start | bytes 1572872 | tf_op jit(solution)/shard_map/ppermute | solution.py:19
  97.7 4.4 %collective-permute-done.2 = f32[32,4,8,128]{3,2,1,0:T(8,128)S(1)} collective-permute-done((f32[32,4,8,128]{3,2,1,0:T(8,128)S(1)}, f32[32,4,8,128]{3,2,1,0:T(8,128)S(1)}, u32[]{:S(2)}, u32[]{:S(2)}) %collective-permute-start.2) | collective-permute-done | bytes 524320 | tf_op jit(solution)/shard_map/ppermute | solution.py:18
  102.1 1.7 %collective-permute-done.3 = f32[32,4,8,128]{3,2,1,0:T(8,128)S(1)} collective-permute-done((f32[32,4,8,128]{3,2,1,0:T(8,128)S(1)}, f32[32,4,8,128]{3,2,1,0:T(8,128)S(1)}, u32[]{:S(2)}, u32[]{:S(2)}) %collective-permute-start.3) | collective-permute-done | bytes 524320 | tf_op jit(solution)/shard_map/ppermute | solution.py:19
  103.8 2.8 %pad_maximum_fusion = (f32[32,40,8,128]{3,2,1,0:T(8,128)S(1)}, f32[32,40,8,128]{3,2,1,0:T(8,128)S(1)}) fusion(f32[32,4,8,128]{3,2,1,0:T(8,128)S(1)} %collective-permute-done.3, f32[8,32,8,128]{3,2,1,0:T(8,128)S(1)} %collective-permute-done.1, f32[16,32,8,128]{3,2,1,0:T(8,128)S(1)} %bitcast.102, f32[8,32,8,128]{3,2,1,0:T(8,128)} %collective-permute-done, ...), kind=kLoop, calls=%fused_computation | loop fusion | flops 6553600 | bytes 15732736 | tf_op jit(solution)/shard_map/concatenate | solution.py:20
  106.8 4.9 %multiply_add_fusion = (f32[28,38,8,128]{3,2,1,0:T(8,128)S(1)}, f32[28,38,8,128]{3,2,1,0:T(8,128)S(1)}) fusion(f32[8,128]{1,0:T(8,128)S(1)} %get-tuple-element.28, f32[8,128]{1,0:T(8,128)S(1)} %get-tuple-element.26, f32[32,40,8,128]{3,2,1,0:T(8,128)S(1)} %get-tuple-element.17, f32[28,38]{1,0:T(8,128)S(1)} %slice_bitcast_fusion.1, f32[38]{0:T(128)S(1)} %slice.199, ...), kind=kLoop, calls=%fused_computation.13 | loop fusion | flops 17432576 | bytes 43749840 | tf_op jit(solution)/shard_map/add | solution.py:100
  111.7 1.7 %slice.270 = f32[20,34,8,128]{3,2,1,0:T(8,128)} slice(f32[28,38,8,128]{3,2,1,0:T(8,128)S(1)} %get-tuple-element.14), slice={[4:24], [2:36], [0:8], [0:128]} | slice | bytes 5570560 | tf_op jit(solution)/shard_map/slice | solution.py:95
  113.5 2.7 %multiply_add_fusion.2 = (f32[24,36,8,128]{3,2,1,0:T(8,128)S(1)}, f32[24,36,8,128]{3,2,1,0:T(8,128)S(1)}) fusion(f32[8,128]{1,0:T(8,128)S(1)} %get-tuple-element.29, f32[8,128]{1,0:T(8,128)S(1)} %get-tuple-element.31, f32[28,38,8,128]{3,2,1,0:T(8,128)S(1)} %get-tuple-element.14, f32[24,36]{1,0:T(8,128)S(1)} %copy-done.5, f32[36]{0:T(128)S(1)} %slice.212, ...), kind=kLoop, calls=%fused_computation.33 | loop fusion | flops 14155776 | bytes 35548832 | tf_op jit(solution)/shard_map/add | solution.py:100
  116.2 4.7 %multiply_add_fusion.3 = (f32[20,34,8,128]{3,2,1,0:T(8,128)S(1)}, f32[20,34,8,128]{3,2,1,0:T(8,128)}, f32[20,34,8,128]{3,2,1,0:T(8,128)}) fusion(f32[8,128]{1,0:T(8,128)S(1)} %get-tuple-element.30, f32[8,128]{1,0:T(8,128)S(1)} %get-tuple-element.27, f32[24,36,8,128]{3,2,1,0:T(8,128)S(1)} %get-tuple-element.12, f32[20,34]{1,0:T(8,128)S(1)} %copy-done.6, ...), kind=kLoop, calls=%fused_computation.46 | loop fusion | flops 11141120 | bytes 30788528 | tf_op jit(solution)/shard_map/add | solution.py:100
  120.9 4.2 %fusion.36 = f32[16,32,8,128,1]{3,2,1,0,4:T(8,128)S(1)} fusion(f32[20,34,8,128]{3,2,1,0:T(8,128)S(1)} %get-tuple-element.10, f32[20,34,8,128]{3,2,1,0:T(8,128)} %get-tuple-element.11, f32[20,34,8,128]{3,2,1,0:T(8,128)} %get-tuple-element.20, f32[20,34,8,128]{3,2,1,0:T(8,128)S(1)} %copy-done.2, f32[20,34,8,128]{3,2,1,0:T(8,128)S(1)} %slice.269, ...), kind=kLoop, calls=%fused_computation.57 | loop fusion | flops 10485760 | bytes 25307392 | tf_op jit(solution)/shard_map/add | solution.py:102
  125.1 3.9 %fusion.42 = f32[16,8,32,128]{3,2,1,0:T(8,128)S(1)} fusion(f32[8,128,8,128]{3,2,1,0:T(8,128)S(1)} %bitcast.103, f32[16,32,8,128,1]{3,2,1,0,4:T(8,128)S(1)} %fusion.36), kind=kOutput, calls=%fused_computation.68 | convolution fusion | flops 3221225472 | bytes 8388608 | tf_op jit(solution)/shard_map/dot_general | solution.py:157
  129.3 32.8 %all_to_all.10 = f32[16,8,32,128]{3,2,0,1:T(8,128)S(1)} all-to-all(f32[16,8,32,128]{3,2,0,1:T(8,128)S(1)} %copy.42), channel_id=1, replica_groups=mesh['ax'=64,'md'=8] {'md'}, dimensions={1} | all-to-all | bytes 4194304 | tf_op jit(solution)/shard_map/all_to_all | solution.py:164
  162.0 1.5 copy.43
  (70 shorter events, 7.5 us)
Async XLA Ops:
  3.1 31.2 %all-to-all-start = ((f32[16,8,32,128]{3,2,0,1:T(8,128)}), f32[16,8,32,128]{3,2,0,1:T(8,128)S(1)}, u32[]{:S(2)}, u32[]{:S(2)}) async-start(f32[16,8,32,128]{3,2,0,1:T(8,128)} %copy.34), calls=%async_computation | async-start | bytes 4194304 | tf_op jit(solution)/shard_map/all_to_all | solution.py:112
  14.2 5.5 %copy-start.10 = (f32[255]{0:T(256)S(1)}, f32[255]{0:T(256)}, u32[]{:S(2)}) copy-start(f32[255]{0:T(256)} %param.5) | copy-start | bytes 3064
  14.2 5.6 %copy-start.8 = (f32[256]{0:T(256)S(1)}, f32[256]{0:T(256)}, u32[]{:S(2)}) copy-start(f32[256]{0:T(256)} %param.7) | copy-start | bytes 3076
  14.2 5.6 %copy-start.9 = (f32[256]{0:T(256)S(1)}, f32[256]{0:T(256)}, u32[]{:S(2)}) copy-start(f32[256]{0:T(256)} %param.6) | copy-start | bytes 3076
  19.9 37.4 %copy-start.3 = (f32[32,40,1,1]{1,0,3,2:T(8,128)}, f32[32,40,1,1]{1,0,3,2:T(8,128)S(1)}, u32[]{:S(2)}) copy-start(f32[32,40,1,1]{1,0,3,2:T(8,128)S(1)} %and_convert_fusion) | copy-start | bytes 15364
  47.8 1.3 copy-start.1
  52.0 26.3 %collective-permute-start.1 = (f32[8,32,8,128]{3,2,1,0:T(8,128)}, f32[8,32,8,128]{3,2,1,0:T(8,128)S(1)}, u32[]{:S(2)}, u32[]{:S(2)}) collective-permute-start(f32[8,32,8,128]{3,2,1,0:T(8,128)} %bitcast.8), channel_id=1, source_target_pairs={{8,0},{16,8},{24,16},{32,24},{40,32},{48,40},{56,48},{64,56},{72,6... | collective-permute-start | bytes 3145736 | tf_op jit(solution)/shard_map/ppermute | solution.py:19
  54.4 28.9 %collective-permute-start = (f32[8,32,8,128]{3,2,1,0:T(8,128)}, f32[8,32,8,128]{3,2,1,0:T(8,128)}, u32[]{:S(2)}, u32[]{:S(2)}) collective-permute-start(f32[8,32,8,128]{3,2,1,0:T(8,128)} %bitcast.107), channel_id=1, source_target_pairs={{0,8},{8,16},{16,24},{24,32},{32,40},{40,48},{48,56},{56,64},{64,7... | collective-permute-start | bytes 3145736 | tf_op jit(solution)/shard_map/ppermute | solution.py:18
  83.3 13.2 %copy-start = (f32[1024,1024]{1,0:T(8,128)S(1)}, f32[1024,1024]{1,0:T(8,128)}, u32[]{:S(2)}) copy-start(f32[1024,1024]{1,0:T(8,128)} %fusion.10) | copy-start | bytes 12582916
  84.5 17.6 %collective-permute-start.2 = (f32[32,4,8,128]{3,2,1,0:T(8,128)S(1)}, f32[32,4,8,128]{3,2,1,0:T(8,128)S(1)}, u32[]{:S(2)}, u32[]{:S(2)}) collective-permute-start(f32[32,4,8,128]{3,2,1,0:T(8,128)S(1)} %get-tuple-element.18), channel_id=1, source_target_pairs={{0,1},{1,2},{2,3},{3,4},{4,5},{5,6},{6,7},{8,9},{9,10},{10,11},{11... | collective-permute-start | bytes 1572872 | tf_op jit(solution)/shard_map/ppermute | solution.py:18
  87.4 16.4 %collective-permute-start.3 = (f32[32,4,8,128]{3,2,1,0:T(8,128)S(1)}, f32[32,4,8,128]{3,2,1,0:T(8,128)S(1)}, u32[]{:S(2)}, u32[]{:S(2)}) collective-permute-start(f32[32,4,8,128]{3,2,1,0:T(8,128)S(1)} %get-tuple-element.19), channel_id=1, source_target_pairs={{1,0},{2,1},{3,2},{4,3},{5,4},{6,5},{7,6},{9,8},{10,9},{11,10},{12... | collective-permute-start | bytes 1572872 | tf_op jit(solution)/shard_map/ppermute | solution.py:19
  96.5 1.0 copy-start.4
  111.7 1.7 %copy-start.5 = (f32[24,36]{1,0:T(8,128)S(1)}, f32[24,36]{1,0:T(8,128)}, u32[]{:S(2)}) copy-start(f32[24,36]{1,0:T(8,128)} %slice_bitcast_fusion.3) | copy-start | bytes 10372
  113.4 2.7 %copy-start.6 = (f32[20,34]{1,0:T(8,128)S(1)}, f32[20,34]{1,0:T(8,128)}, u32[]{:S(2)}) copy-start(f32[20,34]{1,0:T(8,128)} %slice_bitcast_fusion.2) | copy-start | bytes 8164
  113.4 2.7 %copy-start.13 = (f32[34]{0:T(128)S(1)}, f32[34]{0:T(128)}, u32[]{:S(2)}) copy-start(f32[34]{0:T(128)} %slice.225) | copy-start | bytes 412
  113.5 2.7 %copy-start.14 = (f32[34]{0:T(128)S(1)}, f32[34]{0:T(128)}, u32[]{:S(2)}) copy-start(f32[34]{0:T(128)} %slice.223) | copy-start | bytes 412
  116.1 4.8 %copy-start.2 = (f32[20,34,8,128]{3,2,1,0:T(8,128)S(1)}, f32[20,34,8,128]{3,2,1,0:T(8,128)}, u32[]{:S(2)}) copy-start(f32[20,34,8,128]{3,2,1,0:T(8,128)} %slice.270) | copy-start | bytes 8355844
  116.2 4.8 %copy-start.7 = (f32[8,128]{1,0:T(8,128)S(1)}, f32[8,128]{1,0:T(8,128)}, u32[]{:S(2)}) copy-start(f32[8,128]{1,0:T(8,128)} %get-tuple-element.7) | copy-start | bytes 12292
  116.2 4.8 %copy-start.11 = (f32[32]{0:T(128)S(1)}, f32[32]{0:T(128)}, u32[]{:S(2)}) copy-start(f32[32]{0:T(128)} %slice.238) | copy-start | bytes 388
  116.2 4.7 %copy-start.12 = (f32[32]{0:T(128)S(1)}, f32[32]{0:T(128)}, u32[]{:S(2)}) copy-start(f32[32]{0:T(128)} %slice.236) | copy-start | bytes 388

commit v7 on v6

--- a/solution.py
+++ b/solution.py
@@ -154,14 +154,17 @@
     solution = chebyshev(
         extended, coefficients, inside, center.reshape(fold), spread.reshape(fold)
     )
-    solved = lax.dot_general(
-        solution.reshape(planes * local_radii, *fold),
-        basis_table.reshape(points, *fold),
-        (((1, 2), (1, 2)), ((), ())),
-        precision=lax.Precision.HIGH,
-        preferred_element_type=jnp.float32,
-    ).reshape(planes, local_radii, group_size, local_points).transpose(0, 2, 1, 3)
-    returned = lax.all_to_all(solved, "md", split_axis=1, concat_axis=1, tiled=True)
+    halves = []
+    for part in (slice(0, planes // 2), slice(planes // 2, planes)):
+        solved = lax.dot_general(
+            solution[part].reshape(planes // 2 * local_radii, *fold),
+            basis_table.reshape(points, *fold),
+            (((1, 2), (1, 2)), ((), ())),
+            precision=lax.Precision.HIGH,
+            preferred_element_type=jnp.float32,
+        ).reshape(planes // 2, local_radii, group_size, local_points).transpose(0, 2, 1, 3)
+        halves.append(lax.all_to_all(solved, "md", split_axis=1, concat_axis=1, tiled=True))
+    returned = jnp.concatenate(halves, axis=0)
     return returned.reshape(planes, radii, local_points)
 
 

time: 164 us -> 188 us (1.15)
  the two profiles are of different devices: /device:TPU:488 before, /device:TPU:448 now
where the time goes in v7:
time: 188 us; the launch traced here: 187 us
  local copies, waits for them, and re-layouts  46.4 us (25%)
  waiting for transfers between devices  45.7 us (24%)
  other arithmetic  34.2 us (18%)
  starting transfers between devices  24.7 us (13%)
  blocking collectives  19.1 us (10%)
  matrix products  16.6 us (9%)
    all_to_all x1, blocking collectives, per_device(): lax.all_to_all(solved, 'md', split_axis=1, concat_axis=1, tiled=True)  19.1 us
    add x3, other arithmetic, chebyshev(): direction = renewed * factor * direction + 2.0 * renewed / spread * residual  18.5 us
    all_to_all x1, waiting for transfers between devices, per_device(): lax.all_to_all(right_side.reshape(planes, group_size, local_radii, local_...  15.1 us
    ppermute x2, waiting for transfers between devices, with_halo(): after = lax.ppermute(leading, axis, down)  14.7 us
    all_to_all x1, waiting for transfers between devices, per_device(): lax.all_to_all(solved, 'md', split_axis=1, concat_axis=1, tiled=True)  10.4 us
    dot_general x1, matrix products, per_device(): lax.dot_general(gridded.transpose(0, 2, 1, 3).reshape(planes * local_radi...  9.3 us
    ppermute x2, starting transfers between devices, with_halo(): after = lax.ppermute(leading, axis, down)  8.11 us
    unnamed x40, local copies, waits for them, and re-layouts  7.96 us
  transfers between devices with their start and end apart: 6, of which 5 were waited for; matrix products, arithmetic and copies ran while one was open for 20% of the time, Pallas kernels for 0%

profile of v7, /device:TPU:448, one launch (start us, length us, event | category | flops | bytes accessed | tf_op | source)
XLA Modules:
  0.0 187.2 jit_solution(5849332370500279047)
XLA Ops:
  0.0 3.1 %copy.58 = f32[16,8,32,128]{3,2,0,1:T(8,128)} copy(f32[16,8,32,128]{3,2,1,0:T(8,128)} %bitcast.128) | data formatting | bytes 4194304 | tf_op jit(solution)/shard_map/reshape | solution.py:113
  3.1 5.3 %all-to-all-start = ((f32[16,8,32,128]{3,2,0,1:T(8,128)}), f32[16,8,32,128]{3,2,0,1:T(8,128)S(1)}, u32[]{:S(2)}, u32[]{:S(2)}) async-start(f32[16,8,32,128]{3,2,0,1:T(8,128)} %copy.58), calls=%async_computation | async-start | bytes 4194304 | tf_op jit(solution)/shard_map/all_to_all | solution.py:112
  10.8 2.9 %fusion.12 = f32[1024,1024]{1,0:T(8,128)} fusion(f32[32,32,1024]{2,1,0:T(8,128)S(1)} %get-tuple-element.24, f32[32,32,1024]{2,1,0:T(8,128)S(1)} %get-tuple-element.23, f32[1024]{0:T(1024)S(1)} %select_sqrt_fusion, pred[1024]{0:T(1024)(128)(4,1)S(1)} %iota_compare_fusion.2), kind=kLoop, calls=%fused_computation.19 | loop fusion | flops 2097152 | bytes 12588032 | tf_op jit(solution)/shard_map/mul | solution.py:44
  13.7 5.4 %copy.81 = f32[1024,1024]{0,1:T(8,128)} copy(f32[1024,1024]{1,0:T(8,128)} %fusion.12) | data formatting | bytes 8388608 | tf_op jit(solution)/shard_map/reshape | solution.py:122
  19.4 15.1 %all-to-all-done = f32[16,8,32,128]{3,2,0,1:T(8,128)S(1)} async-done(((f32[16,8,32,128]{3,2,0,1:T(8,128)}), f32[16,8,32,128]{3,2,0,1:T(8,128)S(1)}, u32[]{:S(2)}, u32[]{:S(2)}) %all-to-all-start) | async-done | bytes 2097184 | tf_op jit(solution)/shard_map/all_to_all | solution.py:112
  34.5 3.0 %copy.59 = f32[16,32,8,128]{3,2,1,0:T(8,128)} copy(f32[16,32,8,128]{3,1,0,2:T(8,128)S(1)} %bitcast.124) | data formatting | bytes 4194304 | tf_op jit(solution)/shard_map/transpose | solution.py:121
  37.5 2.8 %reshape.467 = f32[512,1024,1]{1,0,2:T(8,128)} reshape(f32[16,32,8,128]{3,2,1,0:T(8,128)} %copy.59) | data formatting | bytes 4194304 | tf_op jit(solution)/shard_map/reshape | solution.py:121
  40.2 9.3 %convolution_bitcast_fusion = f32[512,8,128]{0,2,1:T(8,128)S(1)} fusion(f32[1024,8,128]{0,2,1:T(8,128)} %bitcast.123, f32[512,1024,1]{1,0,2:T(8,128)} %reshape.467), kind=kOutput, calls=%fused_computation.71 | convolution fusion | flops 6442450944 | bytes 8388608 | tf_op jit(solution)/shard_map/dot_general | solution.py:120
  49.5 1.6 fusion.74
  51.1 1.7 copy.61
  54.0 1.9 %collective-permute-start = (f32[8,32,8,128]{3,1,2,0:T(8,128)}, f32[8,32,8,128]{3,1,2,0:T(8,128)}, u32[]{:S(2)}, u32[]{:S(2)}) collective-permute-start(f32[8,32,8,128]{3,1,2,0:T(8,128)} %copy.62), channel_id=1, source_target_pairs={{0,8},{8,16},{16,24},{24,32},{32,40},{40,48},{48,56},{56,64},{64,7... | collective-permute-start | bytes 3145736 | tf_op jit(solution)/shard_map/ppermute | solution.py:18
  56.1 1.6 copy.64
  58.9 6.8 %collective-permute-start.1 = (f32[8,32,8,128]{3,1,2,0:T(8,128)}, f32[8,32,8,128]{3,1,2,0:T(8,128)S(1)}, u32[]{:S(2)}, u32[]{:S(2)}) collective-permute-start(f32[8,32,8,128]{3,1,2,0:T(8,128)} %copy.65), channel_id=1, source_target_pairs={{8,0},{16,8},{24,16},{32,24},{40,32},{48,40},{56,48},{64,56},{72,6... | collective-permute-start | bytes 3145736 | tf_op jit(solution)/shard_map/ppermute | solution.py:19
  66.3 1.8 copy.63
  68.1 5.5 %collective-permute-done = f32[8,32,8,128]{3,1,2,0:T(8,128)} collective-permute-done((f32[8,32,8,128]{3,1,2,0:T(8,128)}, f32[8,32,8,128]{3,1,2,0:T(8,128)}, u32[]{:S(2)}, u32[]{:S(2)}) %collective-permute-start) | collective-permute-done | bytes 1048608 | tf_op jit(solution)/shard_map/ppermute | solution.py:18
  75.0 2.0 %copy_dynamic-update-slice_fusion = f32[32,32,8,128]{3,1,2,0:T(8,128)S(1)} fusion(f32[32,32,8,128]{3,1,2,0:T(8,128)S(1)} %constant_dynamic-update-slice_fusion.1, f32[16,32,8,128]{3,2,1,0:T(8,128)} %bitcast.125), kind=kLoop, calls=%fused_computation.70 | loop fusion | bytes 4194304
  76.9 12.1 %collective-permute-done.1 = f32[8,32,8,128]{3,1,2,0:T(8,128)S(1)} collective-permute-done((f32[8,32,8,128]{3,1,2,0:T(8,128)}, f32[8,32,8,128]{3,1,2,0:T(8,128)S(1)}, u32[]{:S(2)}, u32[]{:S(2)}) %collective-permute-start.1) | collective-permute-done | bytes 1048608 | tf_op jit(solution)/shard_map/ppermute | solution.py:19
  89.4 3.2 %collective-permute-start.2 = (f32[32,4,8,128]{3,1,2,0:T(4,128)S(1)}, f32[32,4,8,128]{3,1,2,0:T(4,128)S(1)}, u32[]{:S(2)}, u32[]{:S(2)}) collective-permute-start(f32[32,4,8,128]{3,1,2,0:T(4,128)S(1)} %get-tuple-element.18), channel_id=1, source_target_pairs={{0,1},{1,2},{2,3},{3,4},{4,5},{5,6},{6,7},{8,9},{9,10},{10,11},{11... | collective-permute-start | bytes 1572872 | tf_op jit(solution)/shard_map/ppermute | solution.py:18
  101.8 3.1 %copy.87 = f32[128,8,8,128]{3,2,1,0:T(8,128)} copy(f32[128,8,8,128]{3,1,2,0:T(8,128)S(1)} %bitcast.120) | data formatting | bytes 8388608
  106.1 2.6 %collective-permute-done.3 = f32[32,4,8,128]{3,1,2,0:T(4,128)S(1)} collective-permute-done((f32[32,4,8,128]{3,1,2,0:T(4,128)S(1)}, f32[32,4,8,128]{3,1,2,0:T(4,128)S(1)}, u32[]{:S(2)}, u32[]{:S(2)}) %collective-permute-start.3) | collective-permute-done | bytes 524320 | tf_op jit(solution)/shard_map/ppermute | solution.py:19
  108.7 2.8 %pad_maximum_fusion = (f32[32,40,8,128]{3,1,2,0:T(8,128)}, f32[32,40,8,128]{3,1,2,0:T(8,128)S(1)}) fusion(f32[32,4,8,128]{3,1,2,0:T(4,128)S(1)} %collective-permute-done.3, f32[32,32,8,128]{3,1,2,0:T(8,128)S(1)} %constant_dynamic-update-slice_fusion, f32[32,4,8,128]{3,1,2,0:T(4,128)S(1)} %collective-permute-done.2, f32[8,128]{1,0:T(8,128)S(1)} %get-tuple-element.9), kind=kLoop, calls=%fused_computation | loop fusion | flops 3932160 | bytes 15732736 | tf_op jit(solution)/shard_map/concatenate | solution.py:20
  111.6 2.0 %slice.279 = f32[20,34,8,128]{3,1,2,0:T(8,128)} slice(f32[32,40,8,128]{3,1,2,0:T(8,128)S(1)} %get-tuple-element.17), slice={[6:26], [3:37], [0:8], [0:128]} | slice | bytes 5570560 | tf_op jit(solution)/shard_map/slice | solution.py:95
  113.6 7.9 %multiply_add_fusion = (f32[28,38,8,128]{3,1,2,0:T(8,128)S(1)}, f32[28,38,8,128]{3,1,2,0:T(8,128)}) fusion(f32[8,128]{1,0:T(8,128)} %get-tuple-element.28, f32[8,128]{1,0:T(8,128)S(1)} %get-tuple-element.26, f32[32,40,8,128]{3,1,2,0:T(8,128)S(1)} %get-tuple-element.17, f32[28,38]{1,0:T(8,128)S(1)} %slice_bitcast_fusion.5, f32[38]{0:T(128)} %slice.205, ...), kind=kLoop, calls=%fused_computation.13 | loop fusion | flops 17432576 | bytes 43749840 | tf_op jit(solution)/shard_map/add | solution.py:100
  121.5 2.0 %slice.280 = f32[20,34,8,128]{3,1,2,0:T(8,128)} slice(f32[28,38,8,128]{3,1,2,0:T(8,128)S(1)} %get-tuple-element.14), slice={[4:24], [2:36], [0:8], [0:128]} | slice | bytes 5570560 | tf_op jit(solution)/shard_map/slice | solution.py:95
  125.0 5.6 %multiply_add_fusion.2 = (f32[24,36,8,128]{3,1,2,0:T(8,128)S(1)}, f32[24,36,8,128]{3,1,2,0:T(8,128)}) fusion(f32[8,128]{1,0:T(8,128)S(1)} %get-tuple-element.29, f32[8,128]{1,0:T(8,128)S(1)} %get-tuple-element.31, f32[28,38,8,128]{3,1,2,0:T(8,128)S(1)} %get-tuple-element.14, f32[24,36]{1,0:T(8,128)S(1)} %slice_bitcast_fusion.7, f32[36]{0:T(128)S(1)} %copy-done.15, ...), kind=kLoop, calls=%fused_computation.36 | loop fusion | flops 14155776 | bytes 35548832 | tf_op jit(solution)/shard_map/add | solution.py:100
  130.6 5.1 %multiply_add_fusion.3 = (f32[20,34,8,128]{3,1,2,0:T(8,128)S(1)}, f32[20,34,8,128]{3,1,2,0:T(8,128)S(1)}, f32[20,34,8,128]{3,1,2,0:T(8,128)S(1)}) fusion(f32[8,128]{1,0:T(8,128)S(1)} %get-tuple-element.30, f32[8,128]{1,0:T(8,128)S(1)} %get-tuple-element.27, f32[24,36,8,128]{3,1,2,0:T(8,128)S(1)} %get-tuple-element.12, f32[20,34]{1,0:T(8,128)S(1)} %slice_bitcast_fusion.6, ...), kind=kLoop, calls=%fused_computation.49 | loop fusion | flops 11141120 | bytes 30788528 | tf_op jit(solution)/shard_map/add | solution.py:100
  135.8 4.3 %fusion.38 = f32[16,32,8,128]{3,1,2,0:T(8,128)S(1)} fusion(f32[20,34,8,128]{3,1,2,0:T(8,128)S(1)} %get-tuple-element.10, f32[20,34,8,128]{3,1,2,0:T(8,128)S(1)} %get-tuple-element.11, f32[20,34,8,128]{3,1,2,0:T(8,128)S(1)} %get-tuple-element.20, f32[20,34,8,128]{3,1,2,0:T(8,128)} %slice.280, f32[20,34,8,128]{3,1,2,0:T(8,128)S(1)} %copy-done.3, ...), kind=kLoop, calls=%fused_computation.59 | loop fusion | flops 10485760 | bytes 25307392 | tf_op jit(solution)/shard_map/add | solution.py:102
  140.1 2.4 %fusion.46 = f32[8,8,32,128]{3,2,1,0:T(8,128)S(1)} fusion(f32[8,128,8,128]{3,2,1,0:T(8,128)S(1)} %bitcast.122, f32[16,32,8,128]{3,1,2,0:T(8,128)S(1)} %fusion.38), kind=kOutput, calls=%fused_computation.73 | convolution fusion | flops 1610612736 | bytes 6291456 | tf_op jit(solution)/shard_map/dot_general | solution.py:159
  143.6 6.1 %all-to-all-start.2 = ((f32[8,8,32,128]{3,2,0,1:T(8,128)}), f32[8,8,32,128]{3,2,0,1:T(8,128)}, u32[]{:S(2)}, u32[]{:S(2)}) async-start(f32[8,8,32,128]{3,2,0,1:T(8,128)} %copy.74), calls=%async_computation.2 | async-start | bytes 2097152 | tf_op jit(solution)/shard_map/all_to_all | solution.py:166
  149.7 4.9 %fusion.43 = f32[8,8,32,128]{3,2,1,0:T(8,128)S(1)} fusion(f32[8,128,8,128]{3,2,1,0:T(8,128)} %bitcast.121, f32[16,32,8,128]{3,1,2,0:T(8,128)S(1)} %fusion.38), kind=kOutput, calls=%fused_computation.72 | convolution fusion | flops 1610612736 | bytes 6291456 | tf_op jit(solution)/shard_map/dot_general | solution.py:159
  154.7 10.4 %all-to-all-done.2 = f32[8,8,32,128]{3,2,0,1:T(8,128)} async-done(((f32[8,8,32,128]{3,2,0,1:T(8,128)}), f32[8,8,32,128]{3,2,0,1:T(8,128)}, u32[]{:S(2)}, u32[]{:S(2)}) %all-to-all-start.2) | async-done | bytes 1048608 | tf_op jit(solution)/shard_map/all_to_all | solution.py:166
  165.1 19.1 %all_to_all.15 = f32[8,8,32,128]{3,2,0,1:T(8,128)S(1)} all-to-all(f32[8,8,32,128]{3,2,0,1:T(8,128)S(1)} %copy.72), channel_id=1, replica_groups=mesh['ax'=64,'md'=8] {'md'}, dimensions={1} | all-to-all | bytes 2097152 | tf_op jit(solution)/shard_map/all_to_all | solution.py:166
  (86 shorter events, 23.2 us)
Async XLA Ops:
  3.1 31.3 %all-to-all-start = ((f32[16,8,32,128]{3,2,0,1:T(8,128)}), f32[16,8,32,128]{3,2,0,1:T(8,128)S(1)}, u32[]{:S(2)}, u32[]{:S(2)}) async-start(f32[16,8,32,128]{3,2,0,1:T(8,128)} %copy.58), calls=%async_computation | async-start | bytes 4194304 | tf_op jit(solution)/shard_map/all_to_all | solution.py:112
  49.5 6.4 %copy-start.10 = (f32[255]{0:T(256)S(1)}, f32[255]{0:T(256)}, u32[]{:S(2)}) copy-start(f32[255]{0:T(256)} %param.5) | copy-start | bytes 3064
  51.1 14.6 %copy-start.8 = (f32[256]{0:T(256)S(1)}, f32[256]{0:T(256)}, u32[]{:S(2)}) copy-start(f32[256]{0:T(256)} %param.7) | copy-start | bytes 3076
  51.1 14.6 %copy-start.9 = (f32[256]{0:T(256)S(1)}, f32[256]{0:T(256)}, u32[]{:S(2)}) copy-start(f32[256]{0:T(256)} %param.6) | copy-start | bytes 3076
  54.0 19.6 %collective-permute-start = (f32[8,32,8,128]{3,1,2,0:T(8,128)}, f32[8,32,8,128]{3,1,2,0:T(8,128)}, u32[]{:S(2)}, u32[]{:S(2)}) collective-permute-start(f32[8,32,8,128]{3,1,2,0:T(8,128)} %copy.62), channel_id=1, source_target_pairs={{0,8},{8,16},{16,24},{24,32},{32,40},{40,48},{48,56},{56,64},{64,7... | collective-permute-start | bytes 3145736 | tf_op jit(solution)/shard_map/ppermute | solution.py:18
  58.9 30.1 %collective-permute-start.1 = (f32[8,32,8,128]{3,1,2,0:T(8,128)}, f32[8,32,8,128]{3,1,2,0:T(8,128)S(1)}, u32[]{:S(2)}, u32[]{:S(2)}) collective-permute-start(f32[8,32,8,128]{3,1,2,0:T(8,128)} %copy.65), channel_id=1, source_target_pairs={{8,0},{16,8},{24,16},{32,24},{40,32},{48,40},{56,48},{64,56},{72,6... | collective-permute-start | bytes 3145736 | tf_op jit(solution)/shard_map/ppermute | solution.py:19
  76.9 24.8 %copy-start = (f32[1024,1024]{1,0:T(8,128)S(1)}, f32[1024,1024]{1,0:T(8,128)}, u32[]{:S(2)}) copy-start(f32[1024,1024]{1,0:T(8,128)} %fusion.12) | copy-start | bytes 12582916
  89.4 16.8 %collective-permute-start.2 = (f32[32,4,8,128]{3,1,2,0:T(4,128)S(1)}, f32[32,4,8,128]{3,1,2,0:T(4,128)S(1)}, u32[]{:S(2)}, u32[]{:S(2)}) collective-permute-start(f32[32,4,8,128]{3,1,2,0:T(4,128)S(1)} %get-tuple-element.18), channel_id=1, source_target_pairs={{0,1},{1,2},{2,3},{3,4},{4,5},{5,6},{6,7},{8,9},{9,10},{10,11},{11... | collective-permute-start | bytes 1572872 | tf_op jit(solution)/shard_map/ppermute | solution.py:18
  92.6 16.2 %collective-permute-start.3 = (f32[32,4,8,128]{3,1,2,0:T(4,128)S(1)}, f32[32,4,8,128]{3,1,2,0:T(4,128)S(1)}, u32[]{:S(2)}, u32[]{:S(2)}) collective-permute-start(f32[32,4,8,128]{3,1,2,0:T(4,128)S(1)} %get-tuple-element.19), channel_id=1, source_target_pairs={{1,0},{2,1},{3,2},{4,3},{5,4},{6,5},{7,6},{9,8},{10,9},{11,10},{12... | collective-permute-start | bytes 1572872 | tf_op jit(solution)/shard_map/ppermute | solution.py:19
  121.5 3.5 %copy-start.2 = (f32[28,38,8,128]{3,1,2,0:T(8,128)S(1)}, f32[28,38,8,128]{3,1,2,0:T(8,128)}, u32[]{:S(2)}) copy-start(f32[28,38,8,128]{3,1,2,0:T(8,128)} %get-tuple-element.15) | copy-start | bytes 13074436
  121.5 3.5 %copy-start.4 = (f32[36,8,128]{2,0,1:T(8,128)S(1)}, f32[36,8,128]{2,0,1:T(8,128)}, u32[]{:S(2)}) copy-start(f32[36,8,128]{2,0,1:T(8,128)} %copy.68) | copy-start | bytes 442372
  121.5 3.5 %copy-start.15 = (f32[36]{0:T(128)S(1)}, f32[36]{0:T(128)}, u32[]{:S(2)}) copy-start(f32[36]{0:T(128)} %slice.218) | copy-start | bytes 436
  121.5 3.5 %copy-start.16 = (f32[36]{0:T(128)S(1)}, f32[36]{0:T(128)}, u32[]{:S(2)}) copy-start(f32[36]{0:T(128)} %slice.216) | copy-start | bytes 436
  125.0 5.6 %copy-start.13 = (f32[34]{0:T(128)S(1)}, f32[34]{0:T(128)}, u32[]{:S(2)}) copy-start(f32[34]{0:T(128)} %slice.231) | copy-start | bytes 412
  125.0 5.6 %copy-start.14 = (f32[34]{0:T(128)S(1)}, f32[34]{0:T(128)}, u32[]{:S(2)}) copy-start(f32[34]{0:T(128)} %slice.229) | copy-start | bytes 412
  130.6 5.1 %copy-start.3 = (f32[20,34,8,128]{3,1,2,0:T(8,128)S(1)}, f32[20,34,8,128]{3,1,2,0:T(8,128)}, u32[]{:S(2)}) copy-start(f32[20,34,8,128]{3,1,2,0:T(8,128)} %slice.279) | copy-start | bytes 8355844
  130.6 5.1 %copy-start.5 = (f32[32,8,128]{2,0,1:T(8,128)S(1)}, f32[32,8,128]{2,0,1:T(8,128)}, u32[]{:S(2)}) copy-start(f32[32,8,128]{2,0,1:T(8,128)} %copy_bitcast_fusion) | copy-start | bytes 393220
  130.6 5.1 %copy-start.6 = (f32[8,128]{1,0:T(8,128)S(1)}, f32[8,128]{1,0:T(8,128)}, u32[]{:S(2)}) copy-start(f32[8,128]{1,0:T(8,128)} %get-tuple-element.7) | copy-start | bytes 12292
  130.6 5.1 %copy-start.7 = (f32[8,128]{1,0:T(8,128)S(1)}, f32[8,128]{1,0:T(8,128)}, u32[]{:S(2)}) copy-start(f32[8,128]{1,0:T(8,128)} %get-tuple-element.25) | copy-start | bytes 12292
  130.6 5.1 %copy-start.11 = (f32[32]{0:T(128)S(1)}, f32[32]{0:T(128)}, u32[]{:S(2)}) copy-start(f32[32]{0:T(128)} %slice.244) | copy-start | bytes 388
  130.6 5.1 %copy-start.12 = (f32[32]{0:T(128)S(1)}, f32[32]{0:T(128)}, u32[]{:S(2)}) copy-start(f32[32]{0:T(128)} %slice.242) | copy-start | bytes 388
  135.7 4.3 %copy-start.1 = (f32[128,8,8,128]{3,2,1,0:T(8,128)S(1)}, f32[128,8,8,128]{3,2,1,0:T(8,128)}, u32[]{:S(2)}) copy-start(f32[128,8,8,128]{3,2,1,0:T(8,128)} %copy.87) | copy-start | bytes 12582916
  143.6 21.5 %all-to-all-start.2 = ((f32[8,8,32,128]{3,2,0,1:T(8,128)}), f32[8,8,32,128]{3,2,0,1:T(8,128)}, u32[]{:S(2)}, u32[]{:S(2)}) async-start(f32[8,8,32,128]{3,2,0,1:T(8,128)} %copy.74), calls=%async_computation.2 | async-start | bytes 2097152 | tf_op jit(solution)/shard_map/all_to_all | solution.py:166

commit v8 on v6

--- a/solution.py
+++ b/solution.py
@@ -118,9 +118,9 @@
     )
     fold = (points // 128, 128)
     spectral = lax.dot_general(
-        gridded.transpose(0, 2, 1, 3).reshape(planes * local_radii, points),
-        basis_table.reshape(points, *fold),
-        (((1,), (0,)), ((), ())),
+        gridded,
+        basis_table.reshape(group_size, local_points, *fold),
+        (((1, 3), (0, 1)), ((), ())),
         precision=lax.Precision.HIGHEST,
         preferred_element_type=jnp.float32,
     ).reshape(planes, local_radii, *fold)

time: 164 us -> 170 us (1.037)
  the two profiles are of different devices: /device:TPU:488 before, /device:TPU:448 now
where the time goes in v8:
time: 170 us; the launch traced here: 169 us
  waiting for transfers between devices  40.3 us (24%)
  blocking collectives  32.8 us (19%)
  other arithmetic  29.5 us (17%)
  local copies, waits for them, and re-layouts  27.2 us (16%)
  starting transfers between devices  20.6 us (12%)
  matrix products  18.8 us (11%)
    all_to_all x1, blocking collectives, per_device(): lax.all_to_all(solved, 'md', split_axis=1, concat_axis=1, tiled=True)  32.8 us
    add x3, other arithmetic, chebyshev(): direction = renewed * factor * direction + 2.0 * renewed / spread * residual  21.4 us
    ppermute x2, waiting for transfers between devices, with_halo(): after = lax.ppermute(leading, axis, down)  14.3 us
    all_to_all x1, waiting for transfers between devices, per_device(): lax.all_to_all(right_side.reshape(planes, group_size, local_radii, local_...  13.9 us
    ppermute x2, waiting for transfers between devices, with_halo(): before = lax.ppermute(last, axis, up)  12.2 us
    dot_general x1, matrix products, per_device(): lax.dot_general(solution.reshape(planes * local_radii, *fold), basis_tabl...  9.56 us
    dot_general x1, matrix products, per_device(): lax.dot_general(gridded, basis_table.reshape(group_size, local_points, *f...  9.25 us
    ppermute x2, starting transfers between devices, with_halo(): after = lax.ppermute(leading, axis, down)  7.94 us
  transfers between devices with their start and end apart: 5, of which 5 were waited for; matrix products, arithmetic and copies ran while one was open for 13% of the time, Pallas kernels for 0%

profile of v8, /device:TPU:448, one launch (start us, length us, event | category | flops | bytes accessed | tf_op | source)
XLA Modules:
  0.0 169.5 jit_solution(3453524742022264851)
XLA Ops:
  0.0 3.1 %copy.34 = f32[16,8,32,128]{3,2,0,1:T(8,128)} copy(f32[16,8,32,128]{3,2,1,0:T(8,128)} %bitcast.110) | data formatting | bytes 4194304 | tf_op jit(solution)/shard_map/reshape | solution.py:113
  3.1 5.3 %all-to-all-start = ((f32[16,8,32,128]{3,2,0,1:T(8,128)}), f32[16,8,32,128]{3,2,0,1:T(8,128)S(1)}, u32[]{:S(2)}, u32[]{:S(2)}) async-start(f32[16,8,32,128]{3,2,0,1:T(8,128)} %copy.34), calls=%async_computation | async-start | bytes 4194304 | tf_op jit(solution)/shard_map/all_to_all | solution.py:112
  8.5 1.1 fusion.69
  9.6 1.2 multiply_subtract_fusion
  10.8 1.4 fusion.12
  12.2 3.1 %copy.54 = f32[128,8,8,128]{3,2,1,0:T(8,128)} copy(f32[128,8,8,128]{3,1,2,0:T(8,128)S(1)} %bitcast.109) | data formatting | bytes 8388608
  15.5 0.7 slice_bitcast_fusion.4
  16.2 4.4 %bitcast_bitcast_fusion = f32[8,128,8,128,1]{3,2,1,0,4:T(8,128)} fusion(f32[8,128,8,128]{3,2,1,0:T(8,128)} %bitcast.107), kind=kLoop, calls=%fused_computation.141 | loop fusion | bytes 8388608 | tf_op jit(solution)/shard_map/reshape | solution.py:122
  20.6 13.9 %all-to-all-done = f32[16,8,32,128]{3,2,0,1:T(8,128)S(1)} async-done(((f32[16,8,32,128]{3,2,0,1:T(8,128)}), f32[16,8,32,128]{3,2,0,1:T(8,128)S(1)}, u32[]{:S(2)}, u32[]{:S(2)}) %all-to-all-start) | async-done | bytes 2097184 | tf_op jit(solution)/shard_map/all_to_all | solution.py:112
  34.5 9.2 %fusion.46 = f32[16,32,8,128]{3,1,0,2:T(8,128)S(1)} fusion(f32[16,8,32,128]{3,2,0,1:T(8,128)S(1)} %all-to-all-done, f32[8,128,8,128,1]{3,2,1,0,4:T(8,128)} %bitcast_bitcast_fusion), kind=kOutput, calls=%fused_computation.72 | convolution fusion | flops 6442450944 | bytes 8388608 | tf_op jit(solution)/shard_map/dot_general | solution.py:120
  44.2 1.9 %collective-permute-start = (f32[8,32,8,128]{3,1,0,2:T(8,128)S(1)}, f32[8,32,8,128]{3,1,0,2:T(8,128)S(1)}, u32[]{:S(2)}, u32[]{:S(2)}) collective-permute-start(f32[8,32,8,128]{3,1,0,2:T(8,128)S(1)} %get-tuple-element.21), channel_id=1, source_target_pairs={{0,8},{8,16},{16,24},{24,32},{32,40},{40,48},{48,56},{56,64},{64,7... | collective-permute-start | bytes 3145736 | tf_op jit(solution)/shard_map/ppermute | solution.py:18
  46.1 6.7 %collective-permute-start.1 = (f32[8,32,8,128]{3,1,0,2:T(8,128)S(1)}, f32[8,32,8,128]{3,1,0,2:T(8,128)S(1)}, u32[]{:S(2)}, u32[]{:S(2)}) collective-permute-start(f32[8,32,8,128]{3,1,0,2:T(8,128)S(1)} %get-tuple-element.22), channel_id=1, source_target_pairs={{8,0},{16,8},{24,16},{32,24},{40,32},{48,40},{56,48},{64,56},{72,6... | collective-permute-start | bytes 3145736 | tf_op jit(solution)/shard_map/ppermute | solution.py:19
  53.5 10.1 %collective-permute-done = f32[8,32,8,128]{3,1,0,2:T(8,128)S(1)} collective-permute-done((f32[8,32,8,128]{3,1,0,2:T(8,128)S(1)}, f32[8,32,8,128]{3,1,0,2:T(8,128)S(1)}, u32[]{:S(2)}, u32[]{:S(2)}) %collective-permute-start) | collective-permute-done | bytes 1048608 | tf_op jit(solution)/shard_map/ppermute | solution.py:18
  63.6 10.1 %collective-permute-done.1 = f32[8,32,8,128]{3,1,0,2:T(8,128)S(1)} collective-permute-done((f32[8,32,8,128]{3,1,0,2:T(8,128)S(1)}, f32[8,32,8,128]{3,1,0,2:T(8,128)S(1)}, u32[]{:S(2)}, u32[]{:S(2)}) %collective-permute-start.1) | collective-permute-done | bytes 1048608 | tf_op jit(solution)/shard_map/ppermute | solution.py:19
  73.9 5.4 %collective-permute-start.2 = (f32[32,4,8,128]{3,1,0,2:T(4,128)S(1)}, f32[32,4,8,128]{3,1,0,2:T(4,128)S(1)}, u32[]{:S(2)}, u32[]{:S(2)}) collective-permute-start(f32[32,4,8,128]{3,1,0,2:T(4,128)S(1)} %get-tuple-element.18), channel_id=1, source_target_pairs={{0,1},{1,2},{2,3},{3,4},{4,5},{5,6},{6,7},{8,9},{9,10},{10,11},{11... | collective-permute-start | bytes 1572872 | tf_op jit(solution)/shard_map/ppermute | solution.py:18
  79.4 1.3 collective-permute-start.3
  85.9 0.7 copy.39
  86.7 0.7 copy.37
  87.4 0.7 copy.38
  88.8 0.7 copy_bitcast_fusion
  89.4 2.1 %collective-permute-done.2 = f32[32,4,8,128]{3,1,0,2:T(4,128)S(1)} collective-permute-done((f32[32,4,8,128]{3,1,0,2:T(4,128)S(1)}, f32[32,4,8,128]{3,1,0,2:T(4,128)S(1)}, u32[]{:S(2)}, u32[]{:S(2)}) %collective-permute-start.2) | collective-permute-done | bytes 524320 | tf_op jit(solution)/shard_map/ppermute | solution.py:18
  91.5 4.1 %collective-permute-done.3 = f32[32,4,8,128]{3,1,0,2:T(4,128)S(1)} collective-permute-done((f32[32,4,8,128]{3,1,0,2:T(4,128)S(1)}, f32[32,4,8,128]{3,1,0,2:T(4,128)S(1)}, u32[]{:S(2)}, u32[]{:S(2)}) %collective-permute-start.3) | collective-permute-done | bytes 524320 | tf_op jit(solution)/shard_map/ppermute | solution.py:19
  95.6 2.9 %pad_maximum_fusion = (f32[32,40,8,128]{3,1,0,2:T(8,128)}, f32[32,40,8,128]{3,1,0,2:T(8,128)S(1)}) fusion(f32[32,4,8,128]{3,1,0,2:T(4,128)S(1)} %collective-permute-done.3, f32[8,32,8,128]{3,1,0,2:T(8,128)S(1)} %collective-permute-done.1, f32[16,32,8,128]{3,1,0,2:T(8,128)S(1)} %fusion.46, f32[8,32,8,128]{3,1,0,2:T(8,128)S(1)} %collective-permute-done, ...), kind=kLoop, calls=%fused_computation | loop fusion | flops 6553600 | bytes 15732736 | tf_op jit(solution)/shard_map/concatenate | solution.py:20
  98.5 2.0 %slice.261 = f32[20,34,8,128]{3,1,0,2:T(8,128)} slice(f32[32,40,8,128]{3,1,0,2:T(8,128)S(1)} %get-tuple-element.17), slice={[6:26], [3:37], [0:8], [0:128]} | slice | bytes 5570560 | tf_op jit(solution)/shard_map/slice | solution.py:95
  100.5 8.7 %multiply_add_fusion = (f32[28,38,8,128]{3,1,0,2:T(8,128)S(1)}, f32[28,38,8,128]{3,1,0,2:T(8,128)}) fusion(f32[8,128]{1,0:T(8,128)S(1)} %get-tuple-element.28, f32[8,128]{1,0:T(8,128)S(1)} %get-tuple-element.26, f32[32,40,8,128]{3,1,0,2:T(8,128)S(1)} %get-tuple-element.17, f32[28,38]{1,0:T(8,128)S(1)} %slice_bitcast_fusion.1, f32[38]{0:T(128)} %slice.191, ...), kind=kLoop, calls=%fused_computation.13 | loop fusion | flops 17432576 | bytes 43749840 | tf_op jit(solution)/shard_map/add | solution.py:100
  109.2 2.0 %slice.262 = f32[20,34,8,128]{3,1,0,2:T(8,128)} slice(f32[28,38,8,128]{3,1,0,2:T(8,128)S(1)} %get-tuple-element.14), slice={[4:24], [2:36], [0:8], [0:128]} | slice | bytes 5570560 | tf_op jit(solution)/shard_map/slice | solution.py:95
  111.2 1.5 copy-done.1
  112.7 5.9 %multiply_add_fusion.2 = (f32[24,36,8,128]{3,1,0,2:T(8,128)S(1)}, f32[24,36,8,128]{3,1,0,2:T(8,128)}) fusion(f32[8,128]{1,0:T(8,128)S(1)} %get-tuple-element.29, f32[8,128]{1,0:T(8,128)S(1)} %get-tuple-element.31, f32[28,38,8,128]{3,1,0,2:T(8,128)S(1)} %get-tuple-element.14, f32[24,36]{1,0:T(8,128)S(1)} %slice_bitcast_fusion.3, f32[36]{0:T(128)S(1)} %copy-done.11, ...), kind=kLoop, calls=%fused_computation.35 | loop fusion | flops 14155776 | bytes 35548832 | tf_op jit(solution)/shard_map/add | solution.py:100
  118.6 6.8 %multiply_add_fusion.3 = (f32[20,34,8,128]{3,1,0,2:T(8,128)S(1)}, f32[20,34,8,128]{3,1,0,2:T(8,128)S(1)}, f32[20,34,8,128]{3,1,0,2:T(8,128)}) fusion(f32[8,128]{1,0:T(8,128)S(1)} %get-tuple-element.30, f32[8,128]{1,0:T(8,128)S(1)} %get-tuple-element.27, f32[24,36,8,128]{3,1,0,2:T(8,128)S(1)} %get-tuple-element.12, f32[20,34]{1,0:T(8,128)S(1)} %slice_bitcast_fusion.2, ...), kind=kLoop, calls=%fused_computation.48 | loop fusion | flops 11141120 | bytes 30788528 | tf_op jit(solution)/shard_map/add | solution.py:100
  125.5 9.6 %fusion.51 = f32[16,8,32,128]{3,2,1,0:T(8,128)S(1)} fusion(f32[8,128,8,128]{3,2,1,0:T(8,128)S(1)} %bitcast.108, f32[20,34,8,128]{3,1,0,2:T(8,128)S(1)} %get-tuple-element.10, f32[20,34,8,128]{3,1,0,2:T(8,128)S(1)} %get-tuple-element.11, f32[20,34,8,128]{3,1,0,2:T(8,128)} %get-tuple-element.20, f32[20,34,8,128]{3,1,0,2:T(8,128)} %slice.262, ...), kind=kOutput, calls=%fused_computation.73 | convolution fusion | flops 3231711232 | bytes 29508608 | tf_op jit(solution)/shard_map/dot_general | solution.py:157
  135.2 32.8 %all_to_all.10 = f32[16,8,32,128]{3,2,0,1:T(8,128)S(1)} all-to-all(f32[16,8,32,128]{3,2,0,1:T(8,128)S(1)} %copy.43), channel_id=1, replica_groups=mesh['ax'=64,'md'=8] {'md'}, dimensions={1} | all-to-all | bytes 4194304 | tf_op jit(solution)/shard_map/all_to_all | solution.py:164
  168.0 1.5 copy.44
  (66 shorter events, 7.7 us)
Async XLA Ops:
  3.1 31.3 %all-to-all-start = ((f32[16,8,32,128]{3,2,0,1:T(8,128)}), f32[16,8,32,128]{3,2,0,1:T(8,128)S(1)}, u32[]{:S(2)}, u32[]{:S(2)}) async-start(f32[16,8,32,128]{3,2,0,1:T(8,128)} %copy.34), calls=%async_computation | async-start | bytes 4194304 | tf_op jit(solution)/shard_map/all_to_all | solution.py:112
  12.2 3.1 %copy-start.8 = (f32[255]{0:T(256)S(1)}, f32[255]{0:T(256)}, u32[]{:S(2)}) copy-start(f32[255]{0:T(256)} %param.5) | copy-start | bytes 3064
  43.8 9.1 %copy-start.6 = (f32[256]{0:T(256)S(1)}, f32[256]{0:T(256)}, u32[]{:S(2)}) copy-start(f32[256]{0:T(256)} %param.7) | copy-start | bytes 3076
  43.8 9.0 %copy-start.7 = (f32[256]{0:T(256)S(1)}, f32[256]{0:T(256)}, u32[]{:S(2)}) copy-start(f32[256]{0:T(256)} %param.6) | copy-start | bytes 3076
  44.2 19.4 %collective-permute-start = (f32[8,32,8,128]{3,1,0,2:T(8,128)S(1)}, f32[8,32,8,128]{3,1,0,2:T(8,128)S(1)}, u32[]{:S(2)}, u32[]{:S(2)}) collective-permute-start(f32[8,32,8,128]{3,1,0,2:T(8,128)S(1)} %get-tuple-element.21), channel_id=1, source_target_pairs={{0,8},{8,16},{16,24},{24,32},{32,40},{40,48},{48,56},{56,64},{64,7... | collective-permute-start | bytes 3145736 | tf_op jit(solution)/shard_map/ppermute | solution.py:18
  46.1 27.6 %collective-permute-start.1 = (f32[8,32,8,128]{3,1,0,2:T(8,128)S(1)}, f32[8,32,8,128]{3,1,0,2:T(8,128)S(1)}, u32[]{:S(2)}, u32[]{:S(2)}) collective-permute-start(f32[8,32,8,128]{3,1,0,2:T(8,128)S(1)} %get-tuple-element.22), channel_id=1, source_target_pairs={{8,0},{16,8},{24,16},{32,24},{40,32},{48,40},{56,48},{64,56},{72,6... | collective-permute-start | bytes 3145736 | tf_op jit(solution)/shard_map/ppermute | solution.py:19
  73.9 17.5 %collective-permute-start.2 = (f32[32,4,8,128]{3,1,0,2:T(4,128)S(1)}, f32[32,4,8,128]{3,1,0,2:T(4,128)S(1)}, u32[]{:S(2)}, u32[]{:S(2)}) collective-permute-start(f32[32,4,8,128]{3,1,0,2:T(4,128)S(1)} %get-tuple-element.18), channel_id=1, source_target_pairs={{0,1},{1,2},{2,3},{3,4},{4,5},{5,6},{6,7},{8,9},{9,10},{10,11},{11... | collective-permute-start | bytes 1572872 | tf_op jit(solution)/shard_map/ppermute | solution.py:18
  79.4 16.3 %collective-permute-start.3 = (f32[32,4,8,128]{3,1,0,2:T(4,128)S(1)}, f32[32,4,8,128]{3,1,0,2:T(4,128)S(1)}, u32[]{:S(2)}, u32[]{:S(2)}) collective-permute-start(f32[32,4,8,128]{3,1,0,2:T(4,128)S(1)} %get-tuple-element.19), channel_id=1, source_target_pairs={{1,0},{2,1},{3,2},{4,3},{5,4},{6,5},{7,6},{9,8},{10,9},{11,10},{12... | collective-permute-start | bytes 1572872 | tf_op jit(solution)/shard_map/ppermute | solution.py:19
  109.2 3.5 %copy-start.1 = (f32[28,38,8,128]{3,1,0,2:T(8,128)S(1)}, f32[28,38,8,128]{3,1,0,2:T(8,128)}, u32[]{:S(2)}) copy-start(f32[28,38,8,128]{3,1,0,2:T(8,128)} %get-tuple-element.15) | copy-start | bytes 13074436
  109.2 3.5 %copy-start.2 = (f32[36,8,128]{2,0,1:T(8,128)S(1)}, f32[36,8,128]{2,0,1:T(8,128)}, u32[]{:S(2)}) copy-start(f32[36,8,128]{2,0,1:T(8,128)} %copy.38) | copy-start | bytes 442372
  109.2 3.5 %copy-start.11 = (f32[36]{0:T(128)S(1)}, f32[36]{0:T(128)}, u32[]{:S(2)}) copy-start(f32[36]{0:T(128)} %slice.204) | copy-start | bytes 436
  109.2 3.5 %copy-start.12 = (f32[36]{0:T(128)S(1)}, f32[36]{0:T(128)}, u32[]{:S(2)}) copy-start(f32[36]{0:T(128)} %slice.202) | copy-start | bytes 436
  112.6 5.9 %copy-start.9 = (f32[34]{0:T(128)S(1)}, f32[34]{0:T(128)}, u32[]{:S(2)}) copy-start(f32[34]{0:T(128)} %slice.217) | copy-start | bytes 412
  112.7 5.9 %copy-start.10 = (f32[34]{0:T(128)S(1)}, f32[34]{0:T(128)}, u32[]{:S(2)}) copy-start(f32[34]{0:T(128)} %slice.215) | copy-start | bytes 412
  118.5 6.9 %copy-start = (f32[128,8,8,128]{3,2,1,0:T(8,128)S(1)}, f32[128,8,8,128]{3,2,1,0:T(8,128)}, u32[]{:S(2)}) copy-start(f32[128,8,8,128]{3,2,1,0:T(8,128)} %copy.54) | copy-start | bytes 12582916
  118.5 6.9 %copy-start.3 = (f32[32,8,128]{2,0,1:T(8,128)S(1)}, f32[32,8,128]{2,0,1:T(8,128)}, u32[]{:S(2)}) copy-start(f32[32,8,128]{2,0,1:T(8,128)} %copy_bitcast_fusion) | copy-start | bytes 393220
  118.6 6.9 %copy-start.4 = (f32[16,32]{1,0:T(8,128)S(1)}, f32[16,32]{1,0:T(8,128)}, u32[]{:S(2)}) copy-start(f32[16,32]{1,0:T(8,128)} %slice_bitcast_fusion.4) | copy-start | bytes 6148
  118.6 6.9 %copy-start.5 = (f32[8,128]{1,0:T(8,128)S(1)}, f32[8,128]{1,0:T(8,128)}, u32[]{:S(2)}) copy-start(f32[8,128]{1,0:T(8,128)} %get-tuple-element.25) | copy-start | bytes 12292
  118.6 6.9 %copy-start.13 = (f32[32]{0:T(128)S(1)}, f32[32]{0:T(128)}, u32[]{:S(2)}) copy-start(f32[32]{0:T(128)} %slice.230) | copy-start | bytes 388
  118.6 6.9 %copy-start.14 = (f32[32]{0:T(128)S(1)}, f32[32]{0:T(128)}, u32[]{:S(2)}) copy-start(f32[32]{0:T(128)} %slice.228) | copy-start | bytes 388
